TPU v7x, 256 devices: a whole 4x4x8 slice. The times are simulated.
256 devices in a mesh: clip: 4 (over z_hi, core), fsdp: 64 (over y, z_lo, x).
Axes of the slice: x: 4, y: 4, z: 8 (z_hi: 2, z_lo: 4; z = z_hi * 4 + z_lo), core: 2. Of those that a mesh axis runs over, the one named last changes fastest.
Arguments:
- span_queries: bfloat16 [64, 512, 2560], P('fsdp', None, 'clip'), may hold values from -20 to 20
- span_keys: bfloat16 [64, 512, 2560], P('fsdp', None, 'clip'), may hold values from -12 to 12
- span_values: bfloat16 [64, 512, 2560], P('fsdp', None, 'clip'), may hold values from -6 to 6
- cache_keys: bfloat16 [128, 512, 2560], P(None, 'fsdp', 'clip'), may hold values from -6 to 6
- cache_values: bfloat16 [128, 512, 2560], P(None, 'fsdp', 'clip'), may hold values from -6 to 6
- page_table: int32 [128], replicated, may hold values from 0 to 127, each once
- frame_lists: int32 [64, 6], replicated, may hold values from 0 to 15, as said below
- list_counts: int32 [64], replicated, may hold values from 1 to 6, as said below
- out_weight: bfloat16 [2560, 5120], P('clip', 'fsdp'), may hold values from -1 to 1
Outputs:
- projected: bfloat16 [64, 512, 5120], P('fsdp', 'clip')
Inputs may be any that keep to these rules, and one draw needn't show every extreme that they name: `frame_lists`: each row holds 6 different cached frames; a frame attends to the first list_counts of them. `list_counts`: the counts of frames 2 * i and 2 * i + 1 sum to exactly 7; some frame attends to exactly 6. `page_table`: every block number once.
All inputs are finite; a program needn't handle non-finite values.
Results may differ from a plain program's by a relative error of at most 0.017.
Values may be sent and summed in bfloat16 or wider, within the bound.
No kernel may reach another device: no remote copies, remote signals or barrier semaphores. Data moves between devices by JAX's collectives and lax.ppermute only.
A program may use at most 128 MiB of HBM per device.

v0:
```python
import math

import jax
import jax.numpy as jnp
from jax import lax
from jax.sharding import PartitionSpec as P

HD = 128
CF = 8
NC = 16


neg_fill = -1e30


def lookup(values_table, positions):
    table_width = values_table.shape[0]
    matches = positions[..., None] == jnp.arange(table_width, dtype=jnp.int32)
    return jnp.sum(jnp.where(matches, values_table, 0), axis=-1)


def block_numbers(frame_index, slot_index, page_table, frame_lists):
    max_slots = frame_lists.shape[1]
    listed = lookup(frame_lists.reshape(-1), frame_index * max_slots + slot_index)
    return lookup(page_table, frame_index // CF * NC + listed)


def pick_blocks(send_blocks, cache_keys, cache_values):
    slot_total = send_blocks.shape[0]
    frames = send_blocks.shape[1]
    token_slice = cache_keys.shape[1]
    row_width = cache_keys.shape[2]
    sent_keys = cache_keys[send_blocks].reshape(slot_total, frames * token_slice, row_width)
    sent_values = cache_values[send_blocks].reshape(slot_total, frames * token_slice, row_width)
    return (sent_keys, sent_values)


def empty_state(tokens_here, heads_here):
    return (
        jnp.full((tokens_here, heads_here), neg_fill, jnp.float32),
        jnp.zeros((tokens_here, heads_here), jnp.float32),
        jnp.zeros((tokens_here, heads_here, HD), jnp.float32),
    )


def absorb(carried, query_block, key_block, value_block):
    running_max, running_sum, running_out = carried
    scores = jnp.einsum(
        "qhd,khd->qhk", query_block, key_block, preferred_element_type=jnp.float32
    ) * (1.0 / math.sqrt(HD))
    new_max = jnp.maximum(running_max, jnp.max(scores, axis=2))
    shrink = jnp.exp(running_max - new_max)
    weights = jnp.exp(scores - new_max[:, :, None])
    running_sum = running_sum * shrink + jnp.sum(weights, axis=2)
    running_out = running_out * shrink[:, :, None] + jnp.einsum(
        "qhk,khd->qhd",
        weights.astype(jnp.bfloat16),
        value_block,
        preferred_element_type=jnp.float32,
    )
    return (new_max, running_sum, running_out)


def local(
    span_queries,
    span_keys,
    span_values,
    cache_keys,
    cache_values,
    page_table,
    frame_lists,
    list_counts,
    out_weight,
):
    frames = lax.axis_size("fsdp")
    own_frame = lax.axis_index("fsdp")
    tokens_here = span_queries.shape[1]
    row_width = span_queries.shape[2]
    heads_here = row_width // HD
    max_slots = frame_lists.shape[1]
    own_queries = span_queries[0].reshape(tokens_here, heads_here, HD)
    own_keys = span_keys[0].reshape(tokens_here, heads_here, HD)
    own_values = span_values[0].reshape(tokens_here, heads_here, HD)
    destinations = jnp.arange(frames, dtype=jnp.int32)[:, None]
    blank = empty_state(tokens_here, heads_here)
    started = absorb(blank, own_queries, own_keys, own_values)
    slot_index = jnp.arange(max_slots, dtype=jnp.int32)[None, :]
    send_blocks = block_numbers(destinations, slot_index, page_table, frame_lists).T
    sent_keys, sent_values = pick_blocks(send_blocks, cache_keys, cache_values)
    arrived_keys, arrived_values = (
        lax.all_to_all(sent_keys, "fsdp", split_axis=1, concat_axis=1, tiled=True),
        lax.all_to_all(sent_values, "fsdp", split_axis=1, concat_axis=1, tiled=True),
    )
    arrived_keys = arrived_keys.reshape(max_slots, tokens_here, heads_here, HD)
    arrived_values = arrived_values.reshape(max_slots, tokens_here, heads_here, HD)
    item_count = lookup(list_counts, own_frame)

    def advance_own(item_number, carried_one):
        return absorb(
            carried_one, own_queries, arrived_keys[item_number], arrived_values[item_number]
        )

    final_state = lax.fori_loop(0, item_count, advance_own, started)
    running_sum = final_state[1]
    running_out = final_state[2]
    attended = (
        (running_out / running_sum[:, :, None]).astype(jnp.bfloat16).reshape(tokens_here, row_width)
    )
    partial_value = jnp.dot(
        attended,
        lax.all_gather(out_weight, "fsdp", axis=1, tiled=True),
        preferred_element_type=jnp.float32,
    )
    own_rows = lax.psum_scatter(
        partial_value.astype(jnp.bfloat16), "clip", scatter_dimension=0, tiled=True
    )
    return own_rows[None]


def solution(mesh):
    in_specs = (
        P("fsdp", None, "clip"),
        P("fsdp", None, "clip"),
        P("fsdp", None, "clip"),
        P(None, "fsdp", "clip"),
        P(None, "fsdp", "clip"),
        P(),
        P(),
        P(),
        P("clip", "fsdp"),
    )
    out_specs = P("fsdp", "clip", None)
    return jax.shard_map(local, mesh=mesh, in_specs=in_specs, out_specs=out_specs, check_vma=False)
```

profile of v0, /device:TPU:50, one launch (start us, length us, event | category | flops | bytes accessed | tf_op | source)
XLA Modules:
  0.0 630.3 jit_solution(13444650917698095707)
XLA Ops:
  6.5 0.0 copy-start
  6.5 0.9 copy.82
  7.4 0.1 reshape.110
  7.6 0.3 select_reduce_fusion
  7.9 0.9 select_reduce_fusion.1
  8.8 0.1 reshape.118
  8.9 0.0 copy-done
  8.9 3.6 gather_fusion
  12.5 6.8 %copy.83 = bf16[6,512,640]{2,0,1:T(8,128)(2,1)} copy(bf16[6,512,640]{2,1,0:T(8,128)(2,1)} %bitcast.77) | data formatting | bytes 7864320 | tf_op jit(solution)/shard_map/reshape | solution.py:33
  19.3 0.0 copy-start.2
  19.3 11.8 %all-to-all-start = ((bf16[6,512,640]{2,0,1:T(8,128)(2,1)}), bf16[6,512,640]{2,0,1:T(8,128)(2,1)}, u32[]{:S(2)}, u32[]{:S(2)}) async-start(bf16[6,512,640]{2,0,1:T(8,128)(2,1)} %copy.83), calls=%async_computation | async-start | bytes 10485760 | tf_op jit(solution)/shard_map/all_to_all | solution.py:91
  31.1 0.0 copy-done.2
  31.1 3.5 gather_fusion.1
  34.6 6.8 %copy.85 = bf16[6,512,640]{2,0,1:T(8,128)(2,1)} copy(bf16[6,512,640]{2,1,0:T(8,128)(2,1)} %bitcast.76) | data formatting | bytes 7864320 | tf_op jit(solution)/shard_map/reshape | solution.py:34
  41.4 0.0 copy-start.3
  41.4 0.0 copy-start.4
  41.4 0.0 copy-start.5
  41.4 103.3 %all-to-all-done = bf16[6,512,640]{2,0,1:T(8,128)(2,1)} async-done(((bf16[6,512,640]{2,0,1:T(8,128)(2,1)}), bf16[6,512,640]{2,0,1:T(8,128)(2,1)}, u32[]{:S(2)}, u32[]{:S(2)}) %all-to-all-start) | async-done | bytes 3932192 | tf_op jit(solution)/shard_map/all_to_all | solution.py:91
  144.7 10.9 %all-to-all-start.1 = ((bf16[6,512,640]{2,0,1:T(8,128)(2,1)}), bf16[6,512,640]{2,0,1:T(8,128)(2,1)}, u32[]{:S(2)}, u32[]{:S(2)}) async-start(bf16[6,512,640]{2,0,1:T(8,128)(2,1)} %copy.85), calls=%async_computation.1 | async-start | bytes 10485760 | tf_op jit(solution)/shard_map/all_to_all | solution.py:92
  155.6 0.0 all-gather.2.cloned.1.call-start
  155.7 0.7 all-gather.2.cloned.1.call-update
  156.4 0.2 reduce-scatter.2.cloned.1.call-start
  156.6 0.0 copy-done.3
  156.6 0.3 copy.76
  156.9 0.0 copy-done.4
  156.9 0.3 copy.75
  157.2 0.0 copy-done.5
  157.2 0.3 copy.79
  157.4 0.3 copy.89
  157.7 0.9 bitcast_reduce_fusion.1
  158.7 0.9 fusion.23
  159.5 0.0 copy-start.6
  159.6 2.5 fusion.31
  162.1 1.7 copy.87
  163.8 0.0 copy-done.6
  163.9 0.7 fusion.35
  164.6 8.1 %copy.84 = bf16[6,512,640]{1,2,0:T(8,128)(2,1)} copy(bf16[6,512,640]{2,0,1:T(8,128)(2,1)} %all-to-all-done) | data formatting | bytes 7864320 | tf_op jit(solution)/shard_map/all_to_all | solution.py:91
  172.6 111.5 %all-to-all-done.1 = bf16[6,512,640]{2,0,1:T(8,128)(2,1)} async-done(((bf16[6,512,640]{2,0,1:T(8,128)(2,1)}), bf16[6,512,640]{2,0,1:T(8,128)(2,1)}, u32[]{:S(2)}, u32[]{:S(2)}) %all-to-all-start.1) | async-done | bytes 3932192 | tf_op jit(solution)/shard_map/all_to_all | solution.py:92
  284.1 8.1 %copy.86 = bf16[6,512,640]{1,2,0:T(8,128)(2,1)} copy(bf16[6,512,640]{2,0,1:T(8,128)(2,1)} %all-to-all-done.1) | data formatting | bytes 7864320 | tf_op jit(solution)/shard_map/all_to_all | solution.py:92
  292.1 13.0 %while.14 = (s32[]{:T(128)}, f32[512,5]{0,1:T(8,128)S(1)}, f32[512,5]{0,1:T(8,128)S(1)}, f32[512,5,128]{0,2,1:T(8,128)S(1)}, s32[]{:T(128)}, /*index=5*/bf16[6,5...) while((s32[]{:T(128)}, f32[512,5]{0,1:T(8,128)S(1)}, ...), condition=%wide.region_8.9_spmd, body=%wide.region_5.8_spmd.sunk | while | flops 682234880 | bytes 20480152 | solution.py:103
  292.9 2.0 bitcast_reduce_fusion.3
  294.9 0.9 fusion.52
  295.8 2.5 fusion.53
  299.0 2.0 bitcast_reduce_fusion.3
  301.0 0.9 fusion.52
  301.9 2.5 fusion.53
  305.1 0.2 divide_convert_fusion
  305.3 176.5 %all-gather.2.cloned.1.call-done = bf16[640,5120]{0,1:T(8,128)(2,1)} async-done(((bf16[640,80]{0,1:T(8,128)(2,1)}), bf16[640,5120]{0,1:T(8,128)(2,1)}) %all-gather.2.cloned.1.call-update) | async-done | bytes 6553616 | tf_op jit(solution)/shard_map/all_gather | solution.py:111
  481.8 0.0 copy-start.1
  481.8 9.1 %convolution_convert_fusion = bf16[512,5120]{1,0:T(8,128)(2,1)} fusion(bf16[512,640]{0,1:T(8,128)(2,1)S(1)} %bitcast.84, bf16[640,5120]{0,1:T(8,128)(2,1)} %all-gather.2.cloned.1.call-done), kind=kOutput, calls=%fused_computation.22 | convolution fusion | flops 3358064640 | bytes 12451840 | tf_op jit(solution)/shard_map/dot_general | solution.py:109
  490.8 0.0 reduce-scatter.2.cloned.1.call-update
  490.8 132.6 %reduce-scatter.2.cloned.1.call-done = bf16[128,5120]{1,0:T(8,128)(2,1)} async-done(((bf16[512,5120]{1,0:T(8,128)(2,1)}), bf16[128,5120]{1,0:T(8,128)(2,1)}) %reduce-scatter.2.cloned.1.call-update) | async-done | bytes 1310736 | tf_op jit(solution)/shard_map/reduce_scatter | solution.py:114
  623.4 0.0 copy-done.1
  (14 shorter events, 0.1 us)
Async XLA Ops:
  6.5 2.4 copy-start
  19.3 11.8 %copy-start.2 = (bf16[128,8,640]{2,1,0:T(8,128)(2,1)S(1)}, bf16[128,8,640]{2,1,0:T(8,128)(2,1)}, u32[]{:S(2)}) copy-start(bf16[128,8,640]{2,1,0:T(8,128)(2,1)} %param.15) | copy-start | bytes 3932164
  19.3 125.4 %all-to-all-start = ((bf16[6,512,640]{2,0,1:T(8,128)(2,1)}), bf16[6,512,640]{2,0,1:T(8,128)(2,1)}, u32[]{:S(2)}, u32[]{:S(2)}) async-start(bf16[6,512,640]{2,0,1:T(8,128)(2,1)} %copy.83), calls=%async_computation | async-start | bytes 10485760 | tf_op jit(solution)/shard_map/all_to_all | solution.py:91
  41.4 115.2 %copy-start.3 = (bf16[1,512,640]{2,1,0:T(8,128)(2,1)S(1)}, bf16[1,512,640]{2,1,0:T(8,128)(2,1)}, u32[]{:S(2)}) copy-start(bf16[1,512,640]{2,1,0:T(8,128)(2,1)} %param.11) | copy-start | bytes 1966084
  41.4 115.5 %copy-start.4 = (bf16[1,512,640]{2,1,0:T(8,128)(2,1)S(1)}, bf16[1,512,640]{2,1,0:T(8,128)(2,1)}, u32[]{:S(2)}) copy-start(bf16[1,512,640]{2,1,0:T(8,128)(2,1)} %param.12) | copy-start | bytes 1966084
  41.4 115.8 %copy-start.5 = (bf16[1,512,640]{2,1,0:T(8,128)(2,1)S(1)}, bf16[1,512,640]{2,1,0:T(8,128)(2,1)}, u32[]{:S(2)}) copy-start(bf16[1,512,640]{2,1,0:T(8,128)(2,1)} %param.13) | copy-start | bytes 1966084
  144.7 139.4 %all-to-all-start.1 = ((bf16[6,512,640]{2,0,1:T(8,128)(2,1)}), bf16[6,512,640]{2,0,1:T(8,128)(2,1)}, u32[]{:S(2)}, u32[]{:S(2)}) async-start(bf16[6,512,640]{2,0,1:T(8,128)(2,1)} %copy.85), calls=%async_computation.1 | async-start | bytes 10485760 | tf_op jit(solution)/shard_map/all_to_all | solution.py:92
  155.6 326.1 %all-gather.2.cloned.1.call-start = ((), (), s32[]{:S(2)}) async-start(), calls=%async_computation.3 | async-start | bytes 6656000 | tf_op jit(solution)/shard_map/all_gather | solution.py:111
  156.4 467.1 %reduce-scatter.2.cloned.1.call-start = ((), (), s32[]{:S(2)}) async-start(), calls=%async_computation.4 | async-start | bytes 6553600 | tf_op jit(solution)/shard_map/reduce_scatter | solution.py:114
  159.5 4.3 copy-start.6
  481.8 141.7 %copy-start.1 = (bf16[128,8,640]{2,1,0:T(8,128)(2,1)S(1)}, bf16[128,8,640]{2,1,0:T(8,128)(2,1)}, u32[]{:S(2)}) copy-start(bf16[128,8,640]{2,1,0:T(8,128)(2,1)} %param.14) | copy-start | bytes 3932164
Sparse Core Ops, SparseCore 0:
  158.2 323.4 all-gather.1
  491.0 132.4 reduce-scatter.1
where the time goes:
time: 634 us; the launch traced here: 630 us
  waiting for transfers between devices  525 us (83%)
  local copies, waits for them, and re-layouts  40.7 us (6%)
  starting transfers between devices  23 us (4%)
  matrix products  21.5 us (3%)
  between operations  13.6 us (2%)
    all_gather x1, waiting for transfers between devices, local(): lax.all_gather(out_weight, 'fsdp', axis=1, tiled=True)  176 us
    reduce_scatter x1, waiting for transfers between devices, local(): lax.psum_scatter(partial_value.astype(jnp.bfloat16), 'clip', scatter_dime...  133 us
    all_to_all x1, waiting for transfers between devices, local(): lax.all_to_all(sent_values, 'fsdp', split_axis=1, concat_axis=1, tiled=True)  111 us
    all_to_all x1, waiting for transfers between devices, local(): lax.all_to_all(sent_keys, 'fsdp', split_axis=1, concat_axis=1, tiled=True)  103 us
  transfers between devices with their start and end apart: 4, of which 4 were waited for; matrix products, arithmetic and copies ran while one was open for 7% of the time, Pallas kernels for 0%

commit v1 on v0

v1 whole, which is shorter than its diff:
```python
import math

import jax
import jax.numpy as jnp
import numpy as np
from jax import lax
from jax.sharding import Mesh
from jax.sharding import PartitionSpec as P

HD = 128
CF = 8
NC = 16

FRAME_AXES = ("y", "zl", "x")

neg_fill = -1e30


def empty_state(tokens_here, heads_here):
    return (
        jnp.full((tokens_here, heads_here), neg_fill, jnp.float32),
        jnp.zeros((tokens_here, heads_here), jnp.float32),
        jnp.zeros((tokens_here, heads_here, HD), jnp.float32),
    )


def absorb(carried, query_block, key_block, value_block):
    running_max, running_sum, running_out = carried
    scores = jnp.einsum(
        "qhd,khd->qhk", query_block, key_block, preferred_element_type=jnp.float32
    ) * (1.0 / math.sqrt(HD))
    new_max = jnp.maximum(running_max, jnp.max(scores, axis=2))
    shrink = jnp.exp(running_max - new_max)
    weights = jnp.exp(scores - new_max[:, :, None])
    running_sum = running_sum * shrink + jnp.sum(weights, axis=2)
    running_out = running_out * shrink[:, :, None] + jnp.einsum(
        "qhk,khd->qhd",
        weights.astype(jnp.bfloat16),
        value_block,
        preferred_element_type=jnp.float32,
    )
    return (new_max, running_sum, running_out)


def pair_schedule(frames, half_slots, page_table, frame_lists, list_counts):
    dest = jnp.arange(frames, dtype=jnp.int32)[:, None]
    slot = jnp.arange(half_slots, dtype=jnp.int32)[None, :]
    even = dest - dest % 2
    global_half = (dest % 2) * half_slots + slot
    combined = global_half // 2
    row_half = global_half % 2
    even_count = list_counts[even]
    for_even = combined < even_count
    listed_even = frame_lists[even, jnp.minimum(combined, frame_lists.shape[1] - 1)]
    listed_odd = frame_lists[even + 1, jnp.clip(combined - even_count, 0, frame_lists.shape[1] - 1)]
    listed = jnp.where(for_even, listed_even, listed_odd)
    blocks = page_table[(even // CF) * NC + listed]
    return blocks, row_half, for_even


def local(
    span_queries,
    span_keys,
    span_values,
    cache_keys,
    cache_values,
    page_table,
    frame_lists,
    list_counts,
    out_weight,
):
    frames = lax.axis_size(FRAME_AXES)
    own_frame = lax.axis_index(FRAME_AXES)
    tokens_here = span_queries.shape[1]
    row_width = span_queries.shape[2]
    heads_here = row_width // HD
    blocks_total, rows_here, _ = cache_keys.shape
    half_rows = rows_here // 2
    half_slots = frame_lists.shape[1] + 1
    own_queries = span_queries[0].reshape(tokens_here, heads_here, HD)
    own_keys = span_keys[0].reshape(tokens_here, heads_here, HD)
    own_values = span_values[0].reshape(tokens_here, heads_here, HD)

    blocks, row_half, for_even = pair_schedule(
        frames, half_slots, page_table, frame_lists, list_counts
    )
    split_keys = cache_keys.reshape(blocks_total, 2, half_rows, row_width)
    split_values = cache_values.reshape(blocks_total, 2, half_rows, row_width)
    sent = jnp.stack(
        [split_keys[blocks, row_half], split_values[blocks, row_half]], axis=1
    )
    sent = sent.reshape(frames, -1, 128)
    arrived = lax.all_to_all(sent, FRAME_AXES, split_axis=0, concat_axis=0, tiled=True)
    arrived = arrived.reshape(frames, 2, half_slots, half_rows, heads_here, HD)
    arrived = arrived.transpose(1, 2, 0, 3, 4, 5).reshape(
        2, half_slots, frames * half_rows, heads_here, HD
    )
    arrived_keys = arrived[0]
    arrived_values = arrived[1]

    swap = [(i, i ^ 1) for i in range(lax.axis_size("x"))]
    partner_queries = lax.ppermute(own_queries, "x", swap)
    is_even = own_frame % 2 == 0
    mine = for_even[own_frame] == is_even

    own_state = absorb(
        empty_state(tokens_here, heads_here), own_queries, own_keys, own_values
    )
    other_state = empty_state(tokens_here, heads_here)
    def advance(slot, states):
        key_block = arrived_keys[slot]
        value_block = arrived_values[slot]

        def take_own(states):
            return (absorb(states[0], own_queries, key_block, value_block), states[1])

        def take_other(states):
            return (states[0], absorb(states[1], partner_queries, key_block, value_block))

        return lax.cond(mine[slot], take_own, take_other, states)

    own_state, other_state = lax.fori_loop(
        0, half_slots, advance, (own_state, other_state)
    )

    got_max, got_sum, got_out = lax.ppermute(other_state, "x", swap)
    own_max, own_sum, own_out = own_state
    top = jnp.maximum(own_max, got_max)
    own_scale = jnp.exp(own_max - top)
    got_scale = jnp.exp(got_max - top)
    total_sum = own_sum * own_scale + got_sum * got_scale
    total_out = own_out * own_scale[:, :, None] + got_out * got_scale[:, :, None]
    attended = (
        (total_out / total_sum[:, :, None]).astype(jnp.bfloat16).reshape(tokens_here, row_width)
    )
    weight = out_weight
    for axis in reversed(FRAME_AXES):
        weight = lax.all_gather(weight, axis, axis=1, tiled=True)
    partial_value = jnp.dot(attended, weight, preferred_element_type=jnp.float32)
    own_rows = lax.psum_scatter(
        partial_value.astype(jnp.bfloat16), "clip", scatter_dimension=0, tiled=True
    )
    return own_rows[None]


def solution(mesh):
    frames = mesh.shape["fsdp"]
    fine = Mesh(
        np.asarray(mesh.devices).reshape(mesh.shape["clip"], frames // 16, 4, 4),
        ("clip",) + FRAME_AXES,
    )
    in_specs = (
        P(FRAME_AXES, None, "clip"),
        P(FRAME_AXES, None, "clip"),
        P(FRAME_AXES, None, "clip"),
        P(None, FRAME_AXES, "clip"),
        P(None, FRAME_AXES, "clip"),
        P(),
        P(),
        P(),
        P("clip", FRAME_AXES),
    )
    out_specs = P(FRAME_AXES, "clip", None)
    return jax.shard_map(local, mesh=fine, in_specs=in_specs, out_specs=out_specs, check_vma=False)
```

time: 634 us -> 379 us (0.60)
  waiting for transfers between devices: 525 us -> 203 us
  local copies, waits for them, and re-layouts: 40.7 us -> 73.9 us
  blocking collectives: 0 us -> 13.7 us
  matrix products: 21.5 us -> 31.9 us
  other arithmetic: 4.77 us -> 14.5 us
    all_gather x1 -> x2, waiting for transfers between devices: 176 us -> 0.04 us  [local(): weight = lax.all_gather(weight, axis, axis=1, tiled=True)]
    all_to_all x2 -> x1, waiting for transfers between devices: 215 us -> 52.8 us  [local(): lax.all_to_all(sent, FRAME_AXES, split_axis=0, concat_axis=0, tiled=True)]
    ppermute x0 -> x4, waiting for transfers between devices: none -> 55.5 us  [the longest x1 30.3 us: local(): partner_queries = lax.ppermute(own_queries, 'x', swap)]
    reduce_scatter x1, waiting for transfers between devices: 133 us -> 93.5 us  [local(): lax.psum_scatter(partial_value.astype(jnp.bfloat16), 'clip', scatter_dime...]
    gather x2 -> x9, local copies, waits for them, and re-layouts: 7.04 us -> 22.8 us  [the longest x1 7.06 us: local(): split_keys[blocks, row_half]]
    all_gather x0 -> x1, blocking collectives: none -> 13.7 us  [local(): weight = lax.all_gather(weight, axis, axis=1, tiled=True)]
    all_to_all x2 -> x1, local copies, waits for them, and re-layouts: 16.1 us -> 3.52 us  [local(): lax.all_to_all(sent, FRAME_AXES, split_axis=0, concat_axis=0, tiled=True)]
    all_to_all x2 -> x1, starting transfers between devices: 22.8 us -> 11.7 us  [local(): lax.all_to_all(sent, FRAME_AXES, split_axis=0, concat_axis=0, tiled=True)]
  transfers between devices with their start and end apart: 4 -> 8, of which waited for: 4 -> 5; matrix products, arithmetic and copies ran while one was open for 7% -> 30% of each run, Pallas kernels for 0% -> 0%
where the time goes in v1:
time: 379 us; the launch traced here: 376 us
  waiting for transfers between devices  203 us (54%)
  local copies, waits for them, and re-layouts  73.9 us (19%)
  matrix products  31.9 us (8%)
  starting transfers between devices  20.3 us (5%)
  other arithmetic  14.5 us (4%)
  blocking collectives  13.7 us (4%)
  between operations  13.4 us (4%)
  loops' own time  5.37 us (1%)
    reduce_scatter x1, waiting for transfers between devices, local(): lax.psum_scatter(partial_value.astype(jnp.bfloat16), 'clip', scatter_dime...  93.5 us
    all_to_all x1, waiting for transfers between devices, local(): lax.all_to_all(sent, FRAME_AXES, split_axis=0, concat_axis=0, tiled=True)  52.8 us
    ppermute x1, waiting for transfers between devices, local(): partner_queries = lax.ppermute(own_queries, 'x', swap)  30.3 us
    ppermute x3, waiting for transfers between devices, local(): got_max, got_sum, got_out = lax.ppermute(other_state, 'x', swap)  25.2 us
    all_gather x1, blocking collectives, local(): weight = lax.all_gather(weight, axis, axis=1, tiled=True)  13.7 us
    dot_general x8, matrix products, absorb(): jnp.einsum('qhd,khd->qhk', query_block, key_block, preferred_element_type...  12.7 us
    all_to_all x1, starting transfers between devices, local(): lax.all_to_all(sent, FRAME_AXES, split_axis=0, concat_axis=0, tiled=True)  11.7 us
    dot_general x8, matrix products, absorb(): jnp.einsum('qhk,khd->qhd', weights.astype(jnp.bfloat16), value_block, pre...  10.2 us
  transfers between devices with their start and end apart: 8, of which 5 were waited for; matrix products, arithmetic and copies ran while one was open for 30% of the time, Pallas kernels for 0%

profile of v1, /device:TPU:50, one launch (start us, length us, event | category | flops | bytes accessed | tf_op | source)
XLA Modules:
  0.0 375.5 jit_solution(15196628837934634941)
XLA Ops:
  6.5 13.7 %all_gather.9 = bf16[640,320]{0,1:T(8,128)(2,1)} all-gather(bf16[640,80]{0,1:T(8,128)(2,1)} %param.21), channel_id=1, replica_groups=mesh['clip'=4,'y'=4,'zl'=4,'x'=4] {'x'}, dimensions={1}, use_global_device_ids=true | all-gather | bytes 512000 | tf_op jit(solution)/shard_map/all_gather | solution.py:138
  20.3 2.6 reshape.464
  22.9 0.8 gather_fusion
  24.0 2.3 gather_fusion.1
  26.5 2.3 gather_fusion.2
  29.5 3.0 gather_fusion.3
  32.9 2.7 reshape.463
  35.6 7.0 %gather_fusion.5 = bf16[448,4,640]{2,1,0:T(4,128)(2,1)} fusion(bf16[128,2,4,640]{3,2,1,0:T(4,128)(2,1)S(1)} %reshape.464, s32[448]{0:T(512)S(1)} %reshape.497), kind=kCustom, calls=%fused_computation.5 | custom fusion | bytes 4591104 | tf_op jit(solution)/shard_map/gather | solution.py:90
  42.6 7.1 %gather_fusion.4 = bf16[448,4,640]{2,1,0:T(4,128)(2,1)} fusion(bf16[128,2,4,640]{3,2,1,0:T(4,128)(2,1)S(1)} %reshape.463, s32[448]{0:T(512)S(1)} %reshape.497), kind=kCustom, calls=%fused_computation.4 | custom fusion | bytes 4591104 | tf_op jit(solution)/shard_map/gather | solution.py:90
  49.6 7.4 %pad_maximum_fusion = bf16[64,2,7,4,640]{4,3,2,1,0:T(4,128)(2,1)} fusion(bf16[64,1,7,4,640]{4,3,2,1,0:T(4,128)(2,1)} %bitcast.90, bf16[64,1,7,4,640]{4,3,2,1,0:T(4,128)(2,1)} %bitcast.91), kind=kLoop, calls=%fused_computation.39 | loop fusion | flops 2293760 | bytes 9175040 | tf_op jit(solution)/shard_map/stack | solution.py:89
  57.0 8.6 %reshape.465 = bf16[64,280,128]{2,1,0:T(8,128)(2,1)} reshape(bf16[64,2,7,4,640]{4,3,2,1,0:T(4,128)(2,1)} %pad_maximum_fusion) | data formatting | bytes 9175040 | tf_op jit(solution)/shard_map/reshape | solution.py:92
  65.7 11.7 %all-to-all-start = ((bf16[64,280,128]{2,1,0:T(8,128)(2,1)}), bf16[64,280,128]{2,1,0:T(8,128)(2,1)}, u32[]{:S(2)}, u32[]{:S(2)}) async-start(bf16[64,280,128]{2,1,0:T(8,128)(2,1)} %reshape.465), calls=%async_computation | async-start | bytes 9175040 | tf_op jit(solution)/shard_map/all_to_all | solution.py:93
  79.7 0.9 bitcast_reduce_fusion.2
  80.6 0.9 fusion.20
  81.5 2.5 fusion.28
  84.0 1.4 copy.57
  85.5 2.1 copy.55
  89.0 30.3 %collective-permute-done = bf16[512,5,128]{0,2,1:T(8,128)(2,1)} collective-permute-done((bf16[512,5,128]{0,2,1:T(8,128)(2,1)S(1)}, bf16[512,5,128]{0,2,1:T(8,128)(2,1)}, u32[]{:S(2)}, u32[]{:S(2)}) %collective-permute-start) | collective-permute-done | bytes 655392 | tf_op jit(solution)/shard_map/ppermute | solution.py:102
  119.3 2.2 copy.56
  121.5 52.8 %all-to-all-done = bf16[64,280,128]{2,1,0:T(8,128)(2,1)} async-done(((bf16[64,280,128]{2,1,0:T(8,128)(2,1)}), bf16[64,280,128]{2,1,0:T(8,128)(2,1)}, u32[]{:S(2)}, u32[]{:S(2)}) %all-to-all-start) | async-done | bytes 4587552 | tf_op jit(solution)/shard_map/all_to_all | solution.py:93
  174.3 3.5 copy.52
  177.8 1.1 fusion.62
  178.9 3.6 copy.53
  182.5 3.6 copy.54
  186.2 43.5 %while.23 = (s32[]{:T(128)}, f32[512,5]{0,1:T(8,128)S(1)}, f32[512,5]{0,1:T(8,128)S(1)}, f32[512,5,128]{2,1,0:T(8,128)S(1)}, f32[512,5]{0,1:T(8,128)S(1)}, /*ind...) while((s32[]{:T(128)}, f32[512,5]{0,1:T(8,128)S(1)}, ...), condition=%wide.region_9.10_spmd, body=%wide.region_2.9_spmd.sunk | while | flops 341447680 | bytes 15933780 | solution.py:122
  187.4 1.1 dynamic-slice_bitcast_fusion.3
  188.5 3.2 conditional.2
  188.5 1.6 bitcast_reduce_fusion
  190.6 1.1 fusion.3
  193.0 1.1 dynamic-slice_bitcast_fusion.3
  194.1 3.2 conditional.2
  194.1 1.6 bitcast_reduce_fusion
  196.2 1.1 fusion.3
  198.6 1.1 dynamic-slice_bitcast_fusion.3
  199.7 3.2 conditional.2
  199.7 1.6 bitcast_reduce_fusion
  201.8 1.1 fusion.3
  204.2 1.1 dynamic-slice_bitcast_fusion.3
  205.3 4.2 %conditional.2 = (f32[512,5]{0,1:T(8,128)S(1)}, f32[512,5]{0,1:T(8,128)S(1)}, f32[512,5,128]{2,1,0:T(8,128)S(1)}, f32[512,5]{0,1:T(8,128)S(1)}, f32[512,5]{0,1:T(8,128)S(1)}, /*index=5*/f32[512,5,128]{2,0,1:T(8,128)S(1)}) conditional(s32[]{:T(128)} %bitcast.88, (bf16[256,5,128]{2,0,1:T(8,128)(2,1)S(1)}, bf16[512,5,128]{2,0,1:T(8,128)(2,1)}, ...), branch_computations={%region_3.5_spmd, %region_6.8_spmd} | conditional | flops 341447680 | bytes 14602288 | solution.py:120
  205.3 1.8 bitcast_reduce_fusion.1
  207.6 1.1 fusion.11
  208.7 0.8 copy.42
  210.8 1.1 dynamic-slice_bitcast_fusion.3
  211.9 4.2 %conditional.2 = (f32[512,5]{0,1:T(8,128)S(1)}, f32[512,5]{0,1:T(8,128)S(1)}, f32[512,5,128]{2,1,0:T(8,128)S(1)}, f32[512,5]{0,1:T(8,128)S(1)}, f32[512,5]{0,1:T(8,128)S(1)}, /*index=5*/f32[512,5,128]{2,0,1:T(8,128)S(1)}) conditional(s32[]{:T(128)} %bitcast.88, (bf16[256,5,128]{2,0,1:T(8,128)(2,1)S(1)}, bf16[512,5,128]{2,0,1:T(8,128)(2,1)}, ...), branch_computations={%region_3.5_spmd, %region_6.8_spmd} | conditional | flops 341447680 | bytes 14602288 | solution.py:120
  211.9 1.7 bitcast_reduce_fusion.1
  214.2 1.1 fusion.11
  215.3 0.8 copy.42
  217.4 1.1 dynamic-slice_bitcast_fusion.3
  218.5 4.2 %conditional.2 = (f32[512,5]{0,1:T(8,128)S(1)}, f32[512,5]{0,1:T(8,128)S(1)}, f32[512,5,128]{2,1,0:T(8,128)S(1)}, f32[512,5]{0,1:T(8,128)S(1)}, f32[512,5]{0,1:T(8,128)S(1)}, /*index=5*/f32[512,5,128]{2,0,1:T(8,128)S(1)}) conditional(s32[]{:T(128)} %bitcast.88, (bf16[256,5,128]{2,0,1:T(8,128)(2,1)S(1)}, bf16[512,5,128]{2,0,1:T(8,128)(2,1)}, ...), branch_computations={%region_3.5_spmd, %region_6.8_spmd} | conditional | flops 341447680 | bytes 14602288 | solution.py:120
  218.6 1.8 bitcast_reduce_fusion.1
  220.8 1.1 fusion.11
  221.9 0.8 copy.42
  224.0 1.1 dynamic-slice_bitcast_fusion.3
  225.1 4.2 %conditional.2 = (f32[512,5]{0,1:T(8,128)S(1)}, f32[512,5]{0,1:T(8,128)S(1)}, f32[512,5,128]{2,1,0:T(8,128)S(1)}, f32[512,5]{0,1:T(8,128)S(1)}, f32[512,5]{0,1:T(8,128)S(1)}, /*index=5*/f32[512,5,128]{2,0,1:T(8,128)S(1)}) conditional(s32[]{:T(128)} %bitcast.88, (bf16[256,5,128]{2,0,1:T(8,128)(2,1)S(1)}, bf16[512,5,128]{2,0,1:T(8,128)(2,1)}, ...), branch_computations={%region_3.5_spmd, %region_6.8_spmd} | conditional | flops 341447680 | bytes 14602288 | solution.py:120
  225.2 1.7 bitcast_reduce_fusion.1
  227.4 1.1 fusion.11
  228.5 0.8 copy.42
  229.6 1.5 copy.59
  231.1 5.8 %collective-permute-start.2 = (f32[512,5,128]{0,2,1:T(8,128)}, f32[512,5,128]{0,2,1:T(8,128)}, u32[]{:S(2)}, u32[]{:S(2)}) collective-permute-start(f32[512,5,128]{0,2,1:T(8,128)} %copy.59), channel_id=1, source_target_pairs={{0,1},{1,0},{2,3},{3,2},{4,5},{5,4},{6,7},{7,6},{8,9},{9,8},{10,11... | collective-permute-start | bytes 3932168 | tf_op jit(solution)/shard_map/ppermute | solution.py:126
  236.9 2.0 collective-permute-start.1
  239.6 25.0 %collective-permute-done.3 = f32[512,5]{0,1:T(8,128)S(1)} collective-permute-done((f32[512,5]{0,1:T(8,128)S(1)}, f32[512,5]{0,1:T(8,128)S(1)}, u32[]{:S(2)}, u32[]{:S(2)}) %collective-permute-start.3) | collective-permute-done | bytes 10272 | tf_op jit(solution)/shard_map/ppermute | solution.py:126
  264.8 1.7 divide_convert_fusion
  266.5 8.9 %convolution_convert_fusion = bf16[512,5120]{1,0:T(8,128)(2,1)} fusion(bf16[512,640]{0,1:T(8,128)(2,1)S(1)} %bitcast.99, bf16[640,5120]{0,1:T(8,128)(2,1)} %all-gather.5.cloned.1.call-done), kind=kOutput, calls=%fused_computation.35 | convolution fusion | flops 3358064640 | bytes 12451840 | tf_op jit(solution)/shard_map/dot_general | solution.py:139
  275.5 93.5 %reduce-scatter.2.cloned.1.call-done = bf16[128,5120]{1,0:T(8,128)(2,1)} async-done(((bf16[512,5120]{1,0:T(8,128)(2,1)}), bf16[128,5120]{1,0:T(8,128)(2,1)}) %reduce-scatter.2.cloned.1.call-update) | async-done | bytes 1310736 | tf_op jit(solution)/shard_map/reduce_scatter | solution.py:140
  (98 shorter events, 13.7 us)
Async XLA Ops:
  6.5 17.4 %copy-start = (s32[64,6]{0,1:T(8,128)S(1)}, s32[64,6]{0,1:T(8,128)}, u32[]{:S(2)}) copy-start(s32[64,6]{0,1:T(8,128)} %param.19) | copy-start | bytes 4612
  6.5 16.4 %copy-start.3 = (s32[64]{0:T(128)S(1)}, s32[64]{0:T(128)}, u32[]{:S(2)}) copy-start(s32[64]{0:T(128)} %param.20) | copy-start | bytes 772
  6.5 71.0 %all-gather.3.cloned.1.call-start = ((), (), s32[]{:S(2)}) async-start(), calls=%async_computation.2 | async-start | bytes 2048000 | tf_op jit(solution)/shard_map/all_gather | solution.py:138
  28.8 0.7 copy-start.2
  65.7 12.6 %copy-start.4 = (bf16[1,512,640]{2,1,0:T(8,128)(2,1)S(1)}, bf16[1,512,640]{2,1,0:T(8,128)(2,1)}, u32[]{:S(2)}) copy-start(bf16[1,512,640]{2,1,0:T(8,128)(2,1)} %param.13) | copy-start | bytes 1966084
  65.7 108.6 %all-to-all-start = ((bf16[64,280,128]{2,1,0:T(8,128)(2,1)}), bf16[64,280,128]{2,1,0:T(8,128)(2,1)}, u32[]{:S(2)}, u32[]{:S(2)}) async-start(bf16[64,280,128]{2,1,0:T(8,128)(2,1)} %reshape.465), calls=%async_computation | async-start | bytes 9175040 | tf_op jit(solution)/shard_map/all_to_all | solution.py:93
  77.4 1.7 copy-start.5
  77.4 2.0 copy-start.6
  77.4 189.1 %all-gather.5.cloned.1.call-start = ((), (), s32[]{:S(2)}) async-start(), calls=%async_computation.3 | async-start | bytes 8192000 | tf_op jit(solution)/shard_map/all_gather | solution.py:138
  78.2 290.8 %reduce-scatter.2.cloned.1.call-start = ((), (), s32[]{:S(2)}) async-start(), calls=%async_computation.4 | async-start | bytes 6553600 | tf_op jit(solution)/shard_map/reduce_scatter | solution.py:140
  78.5 40.8 %collective-permute-start = (bf16[512,5,128]{0,2,1:T(8,128)(2,1)S(1)}, bf16[512,5,128]{0,2,1:T(8,128)(2,1)}, u32[]{:S(2)}, u32[]{:S(2)}) collective-permute-start(bf16[512,5,128]{0,2,1:T(8,128)(2,1)S(1)} %bitcast.94), channel_id=1, source_target_pairs={{0,1},{1,0},{2,3},{3,2},{4,5},{5,4},{6,7},{7,6},{8,9},{9,8},{10,11... | collective-permute-start | bytes 1966088 | tf_op jit(solution)/shard_map/ppermute | solution.py:102
  231.1 33.7 %collective-permute-start.2 = (f32[512,5,128]{0,2,1:T(8,128)}, f32[512,5,128]{0,2,1:T(8,128)}, u32[]{:S(2)}, u32[]{:S(2)}) collective-permute-start(f32[512,5,128]{0,2,1:T(8,128)} %copy.59), channel_id=1, source_target_pairs={{0,1},{1,0},{2,3},{3,2},{4,5},{5,4},{6,7},{7,6},{8,9},{9,8},{10,11... | collective-permute-start | bytes 3932168 | tf_op jit(solution)/shard_map/ppermute | solution.py:126
  236.9 27.7 %collective-permute-start.3 = (f32[512,5]{0,1:T(8,128)S(1)}, f32[512,5]{0,1:T(8,128)S(1)}, u32[]{:S(2)}, u32[]{:S(2)}) collective-permute-start(f32[512,5]{0,1:T(8,128)S(1)} %get-tuple-element.286), channel_id=1, source_target_pairs={{0,1},{1,0},{2,3},{3,2},{4,5},{5,4},{6,7},{7,6},{8,9},{9,8},{10,11... | collective-permute-start | bytes 30728 | tf_op jit(solution)/shard_map/ppermute | solution.py:126
  236.9 27.9 %collective-permute-start.1 = (f32[512,5]{0,1:T(8,128)S(1)}, f32[512,5]{0,1:T(8,128)S(1)}, u32[]{:S(2)}, u32[]{:S(2)}) collective-permute-start(f32[512,5]{0,1:T(8,128)S(1)} %get-tuple-element.283), channel_id=1, source_target_pairs={{0,1},{1,0},{2,3},{3,2},{4,5},{5,4},{6,7},{7,6},{8,9},{9,8},{10,11... | collective-permute-start | bytes 30728 | tf_op jit(solution)/shard_map/ppermute | solution.py:126
  275.5 93.5 %copy-start.1 = (s32[64,6]{0,1:T(8,128)S(1)}, s32[64,6]{0,1:T(8,128)}, u32[]{:S(2)}) copy-start(s32[64,6]{0,1:T(8,128)} %param.19) | copy-start | bytes 4612
Sparse Core Ops, SparseCore 0:
  20.4 43.7 all-gather.2
  80.1 101.3 all-gather.4
  275.6 93.3 reduce-scatter.1

commit v2 on v1

v2 whole, which is shorter than its diff:
```python
import math

import jax
import jax.numpy as jnp
import numpy as np
from jax import lax
from jax.sharding import Mesh
from jax.sharding import PartitionSpec as P

HD = 128
CF = 8
NC = 16

FRAME_AXES = ("y", "zl", "x")

neg_fill = -1e30


def empty_state(tokens_here, heads_here):
    return (
        jnp.full((tokens_here, heads_here), neg_fill, jnp.float32),
        jnp.zeros((tokens_here, heads_here), jnp.float32),
        jnp.zeros((tokens_here, heads_here, HD), jnp.float32),
    )


def absorb(carried, query_block, key_block, value_block):
    running_max, running_sum, running_out = carried
    scores = jnp.einsum(
        "qhd,khd->qhk", query_block, key_block, preferred_element_type=jnp.float32
    ) * (1.0 / math.sqrt(HD))
    new_max = jnp.maximum(running_max, jnp.max(scores, axis=2))
    shrink = jnp.exp(running_max - new_max)
    weights = jnp.exp(scores - new_max[:, :, None])
    running_sum = running_sum * shrink + jnp.sum(weights, axis=2)
    running_out = running_out * shrink[:, :, None] + jnp.einsum(
        "qhk,khd->qhd",
        weights.astype(jnp.bfloat16),
        value_block,
        preferred_element_type=jnp.float32,
    )
    return (new_max, running_sum, running_out)


def lookup(values_table, positions):
    table_width = values_table.shape[0]
    matches = positions[..., None] == jnp.arange(table_width, dtype=jnp.int32)
    return jnp.sum(jnp.where(matches, values_table, 0), axis=-1)


def pair_schedule(frames, slots, page_table, frame_lists, list_counts):
    max_slots = frame_lists.shape[1]
    dest = jnp.arange(frames, dtype=jnp.int32)[:, None]
    slot = jnp.arange(slots, dtype=jnp.int32)[None, :]
    even = dest - dest % 2
    combined = jnp.minimum((dest % 2) * slots + slot, max_slots)
    even_count = lookup(list_counts, even)
    for_even = combined < even_count
    listed_even = lookup(frame_lists.reshape(-1), even * max_slots + jnp.minimum(combined, max_slots - 1))
    listed_odd = lookup(
        frame_lists.reshape(-1),
        (even + 1) * max_slots + jnp.clip(combined - even_count, 0, max_slots - 1),
    )
    listed = jnp.where(for_even, listed_even, listed_odd)
    return lookup(page_table, (even // CF) * NC + listed)


def local(
    span_queries,
    span_keys,
    span_values,
    cache_keys,
    cache_values,
    page_table,
    frame_lists,
    list_counts,
    out_weight,
):
    frames = lax.axis_size(FRAME_AXES)
    own_frame = lax.axis_index(FRAME_AXES)
    tokens_here = span_queries.shape[1]
    row_width = span_queries.shape[2]
    heads_here = row_width // HD
    max_slots = frame_lists.shape[1]
    pair_blocks = max_slots + 1
    slots = (pair_blocks + 1) // 2
    own_queries = span_queries[0].reshape(tokens_here, heads_here, HD)
    own_keys = span_keys[0].reshape(tokens_here, heads_here, HD)
    own_values = span_values[0].reshape(tokens_here, heads_here, HD)

    weight = lax.all_gather(out_weight, ("zl", "x"), axis=1, tiled=True)
    weight = lax.all_gather(weight, "y", axis=1, tiled=True)

    blocks = pair_schedule(frames, slots, page_table, frame_lists, list_counts).T
    sent = jnp.stack([cache_keys[blocks], cache_values[blocks]], axis=0)
    arrived = lax.all_to_all(sent, FRAME_AXES, split_axis=2, concat_axis=2, tiled=True)
    arrived = arrived.reshape(2, slots, tokens_here, heads_here, HD)
    arrived_keys = arrived[0]
    arrived_values = arrived[1]

    swap = [(i, i ^ 1) for i in range(lax.axis_size("x"))]
    partner_queries = lax.ppermute(own_queries, "x", swap)
    odd = own_frame % 2
    even_count = lookup(list_counts, own_frame - odd)
    other_count = jnp.where(
        odd == 0, jnp.maximum(0, slots - even_count), jnp.maximum(0, even_count - slots)
    )
    mine_count = jnp.where(
        odd == 0, jnp.minimum(even_count, slots), pair_blocks - jnp.maximum(even_count, slots)
    )

    def slot_of(step):
        return jnp.where(odd == 0, slots - 1 - step, step)

    def advance_other(step, state):
        slot = slot_of(step)
        return absorb(state, partner_queries, arrived_keys[slot], arrived_values[slot])

    def advance_own(step, state):
        slot = slot_of(step)
        return absorb(state, own_queries, arrived_keys[slot], arrived_values[slot])

    other_state = lax.fori_loop(
        0, other_count, advance_other, empty_state(tokens_here, heads_here)
    )
    got_max, got_sum, got_out = lax.ppermute(other_state, "x", swap)
    own_state = absorb(
        empty_state(tokens_here, heads_here), own_queries, own_keys, own_values
    )
    own_state = lax.fori_loop(other_count, other_count + mine_count, advance_own, own_state)

    own_max, own_sum, own_out = own_state
    top = jnp.maximum(own_max, got_max)
    own_scale = jnp.exp(own_max - top)
    got_scale = jnp.exp(got_max - top)
    total_sum = own_sum * own_scale + got_sum * got_scale
    total_out = own_out * own_scale[:, :, None] + got_out * got_scale[:, :, None]
    attended = (
        (total_out / total_sum[:, :, None]).astype(jnp.bfloat16).reshape(tokens_here, row_width)
    )
    partial_value = jnp.dot(attended, weight, preferred_element_type=jnp.float32)
    own_rows = lax.psum_scatter(
        partial_value.astype(jnp.bfloat16), "clip", scatter_dimension=0, tiled=True
    )
    return own_rows[None]


def solution(mesh):
    frames = mesh.shape["fsdp"]
    fine = Mesh(
        np.asarray(mesh.devices).reshape(mesh.shape["clip"], frames // 16, 4, 4),
        ("clip",) + FRAME_AXES,
    )
    in_specs = (
        P(FRAME_AXES, None, "clip"),
        P(FRAME_AXES, None, "clip"),
        P(FRAME_AXES, None, "clip"),
        P(None, FRAME_AXES, "clip"),
        P(None, FRAME_AXES, "clip"),
        P(),
        P(),
        P(),
        P("clip", FRAME_AXES),
    )
    out_specs = P(FRAME_AXES, "clip", None)
    return jax.shard_map(local, mesh=fine, in_specs=in_specs, out_specs=out_specs, check_vma=False)
```

time: 379 us -> 360 us (0.950)
  waiting for transfers between devices: 203 us -> 230 us
  local copies, waits for them, and re-layouts: 73.9 us -> 49.4 us
  blocking collectives: 13.7 us -> 0 us
  loops' own time: 5.37 us -> 0.42 us
    all_to_all x1, waiting for transfers between devices: 52.8 us -> 27.5 us  [local(): lax.all_to_all(sent, FRAME_AXES, split_axis=2, concat_axis=2, tiled=True)]
    all_gather x2, waiting for transfers between devices: 0.04 us -> 24.1 us  [the longest x1 24.1 us: local(): weight = lax.all_gather(out_weight, ('zl', 'x'), axis=1, tiled=True)]
    ppermute x1, waiting for transfers between devices: 30.3 us -> 51.6 us  [local(): partner_queries = lax.ppermute(own_queries, 'x', swap)]
    gather x9 -> x2, local copies, waits for them, and re-layouts: 22.8 us -> 4.87 us  [local(): sent = jnp.stack([cache_keys[blocks], cache_values[blocks]], axis=0)]
    reduce_scatter x1, waiting for transfers between devices: 93.5 us -> 110 us  [local(): lax.psum_scatter(partial_value.astype(jnp.bfloat16), 'clip', scatter_dime...]
    reshape x3 -> x1, local copies, waits for them, and re-layouts: 13.9 us -> 0.14 us  [pair_schedule(): frame_lists.reshape(-1)]
    all_gather x1 -> x0, blocking collectives: 13.7 us -> none  [local(): weight = lax.all_gather(weight, axis, axis=1, tiled=True)]
    ppermute x3, waiting for transfers between devices: 25.2 us -> 16.7 us  [local(): got_max, got_sum, got_out = lax.ppermute(other_state, 'x', swap)]
  transfers between devices with their start and end apart: 8 -> 8, of which waited for: 5 -> 5; matrix products, arithmetic and copies ran while one was open for 30% -> 18% of each run, Pallas kernels for 0% -> 0%
where the time goes in v2:
time: 360 us; the launch traced here: 356 us
  waiting for transfers between devices  230 us (64%)
  local copies, waits for them, and re-layouts  49.4 us (14%)
  matrix products  28.3 us (8%)
  starting transfers between devices  20.9 us (6%)
  between operations  16 us (4%)
  other arithmetic  11 us (3%)
    reduce_scatter x1, waiting for transfers between devices, local(): lax.psum_scatter(partial_value.astype(jnp.bfloat16), 'clip', scatter_dime...  110 us
    ppermute x1, waiting for transfers between devices, local(): partner_queries = lax.ppermute(own_queries, 'x', swap)  51.6 us
    all_to_all x1, waiting for transfers between devices, local(): lax.all_to_all(sent, FRAME_AXES, split_axis=2, concat_axis=2, tiled=True)  27.5 us
    all_gather x1, waiting for transfers between devices, local(): weight = lax.all_gather(out_weight, ('zl', 'x'), axis=1, tiled=True)  24.1 us
    ppermute x3, waiting for transfers between devices, local(): got_max, got_sum, got_out = lax.ppermute(other_state, 'x', swap)  16.7 us
    while x4, local copies, waits for them, and re-layouts, local(): lax.fori_loop(other_count, other_count + mine_count, advance_own, own_state)  13.7 us
    dot_general x4, matrix products, absorb(): jnp.einsum('qhk,khd->qhd', weights.astype(jnp.bfloat16), value_block, pre...  12.4 us
    all_to_all x1, starting transfers between devices, local(): lax.all_to_all(sent, FRAME_AXES, split_axis=2, concat_axis=2, tiled=True)  11.8 us
  transfers between devices with their start and end apart: 8, of which 5 were waited for; matrix products, arithmetic and copies ran while one was open for 18% of the time, Pallas kernels for 0%

profile of v2, /device:TPU:50, one launch (start us, length us, event | category | flops | bytes accessed | tf_op | source)
XLA Modules:
  0.0 356.4 jit_solution(4894857643274426945)
XLA Ops:
  6.6 0.9 copy.83
  7.4 0.1 reshape.295
  7.6 0.8 select_reduce_fusion.3
  8.4 0.3 select_reduce_fusion
  8.8 0.9 select_reduce_fusion.2
  9.7 0.1 reshape.299
  9.8 0.0 copy-start.4
  9.8 2.4 gather_fusion
  12.2 2.4 gather_fusion.1
  14.7 3.1 pad_maximum_fusion
  17.7 3.2 copy.84
  20.9 11.8 %all-to-all-start = ((bf16[2,4,64,8,640]{4,3,1,0,2:T(8,128)(2,1)}), bf16[2,4,64,8,640]{4,3,1,0,2:T(8,128)(2,1)}, u32[]{:S(2)}, u32[]{:S(2)}) async-start(bf16[2,4,64,8,640]{4,3,1,0,2:T(8,128)(2,1)} %copy.84), calls=%async_computation | async-start | bytes 10485760 | tf_op jit(solution)/shard_map/all_to_all | solution.py:96
  32.8 0.0 all-gather.3.cloned.1.call-start
  32.8 0.7 all-gather.3.cloned.1.call-update
  33.5 0.0 all-gather.5.cloned.1.call-start
  33.6 0.3 copy.77
  33.8 0.6 collective-permute-start
  34.5 0.3 copy.76
  34.7 0.9 bitcast_reduce_fusion.2
  35.7 0.0 copy-start.8
  35.7 0.0 copy-start.7
  35.7 0.9 fusion.44
  36.6 1.4 copy-done.2
  37.9 0.6 fusion.58
  40.5 0.3 copy.89
  41.5 0.3 copy.80
  41.8 5.0 %fusion.52 = f32[512,5,128]{2,0,1:T(8,128)} fusion(bf16[512,5,128]{0,2,1:T(8,128)(2,1)S(1)} %bitcast.123, f32[5,512,512]{2,1,0:T(8,128)} %copy-done.2, f32[512,5]{0,1:T(8,128)S(1)} %broadcast_maximum_fusion, f32[512,5]{0,1:T(8,128)S(1)} %get-tuple-element.363), kind=kOutput, calls=%fused_computation.53 | convolution fusion | flops 339804160 | bytes 7229440 | tf_op jit(solution)/shard_map/qhk,khd->qhd/dot_general | solution.py:36
  46.8 1.7 copy.87
  48.5 51.6 %collective-permute-done = bf16[512,5,128]{0,2,1:T(8,128)(2,1)} collective-permute-done((bf16[512,5,128]{0,2,1:T(8,128)(2,1)S(1)}, bf16[512,5,128]{0,2,1:T(8,128)(2,1)}, u32[]{:S(2)}, u32[]{:S(2)}) %collective-permute-start) | collective-permute-done | bytes 655392 | tf_op jit(solution)/shard_map/ppermute | solution.py:102
  100.1 2.2 copy.92
  102.2 24.1 %all-gather.3.cloned.1.call-done = bf16[640,1280]{0,1:T(8,128)(2,1)} async-done(((bf16[640,80]{0,1:T(8,128)(2,1)}), bf16[640,1280]{0,1:T(8,128)(2,1)}) %all-gather.3.cloned.1.call-update) | async-done | bytes 1638416 | tf_op jit(solution)/shard_map/all_gather | solution.py:91
  126.3 0.0 all-gather.5.cloned.1.call-update
  126.3 0.2 reduce-scatter.2.cloned.1.call-start
  126.5 27.5 %all-to-all-done = bf16[2,4,64,8,640]{4,3,1,0,2:T(8,128)(2,1)} async-done(((bf16[2,4,64,8,640]{4,3,1,0,2:T(8,128)(2,1)}), bf16[2,4,64,8,640]{4,3,1,0,2:T(8,128)(2,1)}, u32[]{:S(2)}, u32[]{:S(2)}) %all-to-all-start) | async-done | bytes 5242912 | tf_op jit(solution)/shard_map/all_to_all | solution.py:96
  154.0 4.5 %fusion.64 = (bf16[1,4,64,8,640]{4,3,1,0,2:T(8,128)(2,1)}, bf16[1,4,64,8,640]{4,3,1,0,2:T(8,128)(2,1)S(1)}) fusion(bf16[2,4,64,8,640]{4,3,1,0,2:T(8,128)(2,1)} %all-to-all-done), kind=kLoop, calls=%fused_computation.92 | loop fusion | bytes 10485760 | tf_op jit(solution)/shard_map/slice | solution.py:99
  158.5 1.8 copy.85
  160.3 7.0 %squeeze.26 = bf16[4,512,5,128]{3,2,1,0:T(8,128)(2,1)} reshape(bf16[1,4,64,8,640]{4,3,2,1,0:T(8,128)(2,1)} %copy.85) | data formatting | bytes 5242880 | tf_op jit(solution)/shard_map/squeeze | solution.py:98
  167.3 4.6 %copy.88 = bf16[4,512,5,128]{3,1,2,0:T(8,128)(2,1)} copy(bf16[4,512,5,128]{3,2,1,0:T(8,128)(2,1)} %squeeze.26) | data formatting | bytes 5242880 | tf_op jit(solution)/shard_map/while | solution.py:130
  171.9 1.7 copy.86
  173.6 7.0 %squeeze.27 = bf16[4,512,5,128]{3,2,1,0:T(8,128)(2,1)} reshape(bf16[1,4,64,8,640]{4,3,2,1,0:T(8,128)(2,1)} %copy.86) | data formatting | bytes 5242880 | tf_op jit(solution)/shard_map/squeeze | solution.py:99
  180.7 7.1 %copy.90 = bf16[4,512,5,128]{1,3,2,0:T(8,128)(2,1)} copy(bf16[4,512,5,128]{3,2,1,0:T(8,128)(2,1)} %squeeze.27) | data formatting | bytes 5242880 | tf_op jit(solution)/shard_map/while | solution.py:130
  187.8 0.1 broadcast.376
  187.9 5.6 %while.33 = (s32[]{:T(128)}, f32[512,5]{0,1:T(8,128)S(1)}, f32[512,5]{0,1:T(8,128)S(1)}, f32[512,5,128]{0,2,1:T(8,128)S(1)}, s32[]{:T(128)}, /*index=5*/pred[]{:...) while((s32[]{:T(128)}, f32[512,5]{0,1:T(8,128)S(1)}, ...), condition=%wide.region_14.15_spmd, body=%wide.region_11.14_spmd.sunk | while | flops 682234880 | bytes 20480192 | solution.py:123
  188.0 2.1 bitcast_reduce_fusion.6
  190.1 0.9 fusion.90
  191.0 2.5 fusion.91
  193.5 6.1 %collective-permute-start.1 = (f32[512,5]{0,1:T(8,128)S(1)}, f32[512,5]{0,1:T(8,128)S(1)}, u32[]{:S(2)}, u32[]{:S(2)}) collective-permute-start(f32[512,5]{0,1:T(8,128)S(1)} %get-tuple-element.227), channel_id=1, source_target_pairs={{0,1},{1,0},{2,3},{3,2},{4,5},{5,4},{6,7},{7,6},{8,9},{9,8},{10,11... | collective-permute-start | bytes 30728 | tf_op jit(solution)/shard_map/ppermute | solution.py:126
  199.7 0.1 collective-permute-start.3
  199.8 1.9 collective-permute-start.2
  201.7 11.0 %while.32 = (s32[]{:T(128)}, f32[512,5]{0,1:T(8,128)S(1)}, f32[512,5]{0,1:T(8,128)S(1)}, f32[512,5,128]{0,2,1:T(8,128)S(1)}, s32[]{:T(128)}, /*index=5*/pred[]{:...) while((s32[]{:T(128)}, f32[512,5]{0,1:T(8,128)S(1)}, ...), condition=%wide.region_10.11_spmd, body=%wide.region_7.10_spmd.sunk | while | flops 682234880 | bytes 20480192 | solution.py:130
  201.7 1.9 bitcast_reduce_fusion.5
  203.6 0.9 fusion.85
  204.5 2.5 fusion.86
  207.1 1.9 bitcast_reduce_fusion.5
  209.0 0.9 fusion.85
  209.9 2.5 fusion.86
  212.7 0.0 collective-permute-done.1
  212.7 0.0 collective-permute-done.3
  212.7 16.7 %collective-permute-done.2 = f32[512,5,128]{0,2,1:T(8,128)} collective-permute-done((f32[512,5,128]{0,2,1:T(8,128)S(1)}, f32[512,5,128]{0,2,1:T(8,128)}, u32[]{:S(2)}, u32[]{:S(2)}) %collective-permute-start.2) | collective-permute-done | bytes 1310752 | tf_op jit(solution)/shard_map/ppermute | solution.py:126
  229.4 1.7 divide_convert_fusion
  231.1 0.0 all-gather.5.cloned.1.call-done
  231.1 9.0 %convolution_convert_fusion = bf16[512,5120]{1,0:T(8,128)(2,1)} fusion(bf16[512,640]{0,1:T(8,128)(2,1)S(1)} %bitcast.125, bf16[640,5120]{0,1:T(8,128)(2,1)} %all-gather.5.cloned.1.call-done), kind=kOutput, calls=%fused_computation.42 | convolution fusion | flops 3358064640 | bytes 12451840 | tf_op jit(solution)/shard_map/dot_general | solution.py:141
  240.1 0.0 reduce-scatter.2.cloned.1.call-update
  240.1 109.8 %reduce-scatter.2.cloned.1.call-done = bf16[128,5120]{1,0:T(8,128)(2,1)} async-done(((bf16[512,5120]{1,0:T(8,128)(2,1)}), bf16[128,5120]{1,0:T(8,128)(2,1)}) %reduce-scatter.2.cloned.1.call-update) | async-done | bytes 1310736 | tf_op jit(solution)/shard_map/reduce_scatter | solution.py:142
  (35 shorter events, 0.2 us)
Async XLA Ops:
  6.5 3.2 copy-start
  9.8 2.5 copy-start.4
  20.9 12.6 %copy-start.5 = (bf16[1,512,640]{2,1,0:T(8,128)(2,1)S(1)}, bf16[1,512,640]{2,1,0:T(8,128)(2,1)}, u32[]{:S(2)}) copy-start(bf16[1,512,640]{2,1,0:T(8,128)(2,1)} %param.13) | copy-start | bytes 1966084
  20.9 13.5 %copy-start.6 = (bf16[1,512,640]{2,1,0:T(8,128)(2,1)S(1)}, bf16[1,512,640]{2,1,0:T(8,128)(2,1)}, u32[]{:S(2)}) copy-start(bf16[1,512,640]{2,1,0:T(8,128)(2,1)} %param.14) | copy-start | bytes 1966084
  20.9 133.1 %all-to-all-start = ((bf16[2,4,64,8,640]{4,3,1,0,2:T(8,128)(2,1)}), bf16[2,4,64,8,640]{4,3,1,0,2:T(8,128)(2,1)}, u32[]{:S(2)}, u32[]{:S(2)}) async-start(bf16[2,4,64,8,640]{4,3,1,0,2:T(8,128)(2,1)} %copy.84), calls=%async_computation | async-start | bytes 10485760 | tf_op jit(solution)/shard_map/all_to_all | solution.py:96
  32.8 93.5 %all-gather.3.cloned.1.call-start = ((), (), s32[]{:S(2)}) async-start(), calls=%async_computation.2 | async-start | bytes 1740800 | tf_op jit(solution)/shard_map/all_gather | solution.py:91
  33.5 197.6 %all-gather.5.cloned.1.call-start = ((), (), s32[]{:S(2)}) async-start(), calls=%async_computation.3 | async-start | bytes 8192000 | tf_op jit(solution)/shard_map/all_gather | solution.py:92
  33.8 66.2 %collective-permute-start = (bf16[512,5,128]{0,2,1:T(8,128)(2,1)S(1)}, bf16[512,5,128]{0,2,1:T(8,128)(2,1)}, u32[]{:S(2)}, u32[]{:S(2)}) collective-permute-start(bf16[512,5,128]{0,2,1:T(8,128)(2,1)S(1)} %bitcast.120), channel_id=1, source_target_pairs={{0,1},{1,0},{2,3},{3,2},{4,5},{5,4},{6,7},{7,6},{8,9},{9,8},{10,11... | collective-permute-start | bytes 1966088 | tf_op jit(solution)/shard_map/ppermute | solution.py:102
  35.6 2.3 copy-start.2
  35.7 2.3 copy-start.8
  35.7 5.8 %copy-start.7 = (bf16[1,512,640]{2,1,0:T(8,128)(2,1)S(1)}, bf16[1,512,640]{2,1,0:T(8,128)(2,1)}, u32[]{:S(2)}) copy-start(bf16[1,512,640]{2,1,0:T(8,128)(2,1)} %param.15) | copy-start | bytes 1966084
  126.3 223.6 %reduce-scatter.2.cloned.1.call-start = ((), (), s32[]{:S(2)}) async-start(), calls=%async_computation.4 | async-start | bytes 6553600 | tf_op jit(solution)/shard_map/reduce_scatter | solution.py:142
  167.3 4.6 %copy-start.3 = (bf16[1,4,64,8,640]{4,3,1,0,2:T(8,128)(2,1)S(1)}, bf16[1,4,64,8,640]{4,3,1,0,2:T(8,128)(2,1)}, u32[]{:S(2)}) copy-start(bf16[1,4,64,8,640]{4,3,1,0,2:T(8,128)(2,1)} %get-tuple-element.361) | copy-start | bytes 7864324
  193.5 19.1 %collective-permute-start.1 = (f32[512,5]{0,1:T(8,128)S(1)}, f32[512,5]{0,1:T(8,128)S(1)}, u32[]{:S(2)}, u32[]{:S(2)}) collective-permute-start(f32[512,5]{0,1:T(8,128)S(1)} %get-tuple-element.227), channel_id=1, source_target_pairs={{0,1},{1,0},{2,3},{3,2},{4,5},{5,4},{6,7},{7,6},{8,9},{9,8},{10,11... | collective-permute-start | bytes 30728 | tf_op jit(solution)/shard_map/ppermute | solution.py:126
  199.7 13.0 %collective-permute-start.3 = (f32[512,5]{0,1:T(8,128)S(1)}, f32[512,5]{0,1:T(8,128)S(1)}, u32[]{:S(2)}, u32[]{:S(2)}) collective-permute-start(f32[512,5]{0,1:T(8,128)S(1)} %get-tuple-element.230), channel_id=1, source_target_pairs={{0,1},{1,0},{2,3},{3,2},{4,5},{5,4},{6,7},{7,6},{8,9},{9,8},{10,11... | collective-permute-start | bytes 30728 | tf_op jit(solution)/shard_map/ppermute | solution.py:126
  199.8 29.7 %collective-permute-start.2 = (f32[512,5,128]{0,2,1:T(8,128)S(1)}, f32[512,5,128]{0,2,1:T(8,128)}, u32[]{:S(2)}, u32[]{:S(2)}) collective-permute-start(f32[512,5,128]{0,2,1:T(8,128)S(1)} %get-tuple-element.228), channel_id=1, source_target_pairs={{0,1},{1,0},{2,3},{3,2},{4,5},{5,4},{6,7},{7,6},{8,9},{9,8},{10,11... | collective-permute-start | bytes 3932168 | tf_op jit(solution)/shard_map/ppermute | solution.py:126
  240.1 109.8 %copy-start.1 = (bf16[128,8,640]{2,1,0:T(8,128)(2,1)S(1)}, bf16[128,8,640]{2,1,0:T(8,128)(2,1)}, u32[]{:S(2)}) copy-start(bf16[128,8,640]{2,1,0:T(8,128)(2,1)} %param.16) | copy-start | bytes 3932164
Sparse Core Ops, SparseCore 0:
  35.4 90.8 all-gather.2
  128.1 77.7 all-gather.4
  240.2 109.6 reduce-scatter.1

commit v3 on v2

v3 whole, which is shorter than its diff:
```python
import math

import jax
import jax.numpy as jnp
import numpy as np
from jax import lax
from jax.experimental import pallas as pl
from jax.experimental.pallas import tpu as pltpu
from jax.sharding import Mesh
from jax.sharding import PartitionSpec as P

HD = 128
CF = 8
NC = 16

FRAME_AXES = ("y", "zl", "x")

neg_fill = -1e30


def attend_kernel(order_ref, count_ref, q_ref, k_ref, v_ref, *rest, with_own):
    if with_own:
        own_k_ref, own_v_ref, o_ref, m_ref, l_ref = rest
    else:
        o_ref, m_ref, l_ref = rest
    step = pl.program_id(1)
    first = 1 if with_own else 0

    @pl.when(step == 0)
    def _init():
        m_ref[...] = jnp.full(m_ref.shape, neg_fill, jnp.float32)
        l_ref[...] = jnp.zeros(l_ref.shape, jnp.float32)
        o_ref[...] = jnp.zeros(o_ref.shape, jnp.float32)

    def absorb(key_block, value_block):
        scores = lax.dot_general(
            q_ref[...], key_block, (((1,), (1,)), ((), ())),
            preferred_element_type=jnp.float32,
        ) * (1.0 / math.sqrt(HD))
        running_max = m_ref[:, :1]
        new_max = jnp.maximum(running_max, jnp.max(scores, axis=1, keepdims=True))
        shrink = jnp.exp(running_max - new_max)
        weights = jnp.exp(scores - new_max)
        l_ref[...] = l_ref[...] * shrink + jnp.sum(weights, axis=1, keepdims=True)
        o_ref[...] = o_ref[...] * shrink + jnp.dot(
            weights.astype(jnp.bfloat16), value_block, preferred_element_type=jnp.float32
        )
        m_ref[...] = jnp.broadcast_to(new_max, m_ref.shape)

    if with_own:
        @pl.when(step == 0)
        def _own():
            absorb(own_k_ref[...], own_v_ref[...])

    @pl.when((step >= first) & (step - first < count_ref[0]))
    def _slot():
        absorb(k_ref[0, 0], v_ref[0, 0])


def attend(queries, arrived, order, count, own_keys=None, own_values=None):
    tokens, width = queries.shape
    slots = arrived.shape[1]
    heads = width // HD
    with_own = own_keys is not None
    first = 1 if with_own else 0
    steps = slots + first

    def slot_at(s, order_ref, count_ref):
        visit = jnp.clip(s - first, 0, jnp.maximum(count_ref[0] - 1, 0))
        return order_ref[visit]

    q_spec = pl.BlockSpec((tokens, HD), lambda h, s, o, c: (0, h))
    k_spec = pl.BlockSpec((1, 1, tokens, HD), lambda h, s, o, c: (0, slot_at(s, o, c), 0, h))
    v_spec = pl.BlockSpec((1, 1, tokens, HD), lambda h, s, o, c: (1, slot_at(s, o, c), 0, h))
    in_specs = [q_spec, k_spec, v_spec]
    operands = [queries, arrived, arrived]
    if with_own:
        in_specs += [q_spec, q_spec]
        operands += [own_keys, own_values]
    out_spec = pl.BlockSpec((tokens, HD), lambda h, s, o, c: (0, h))
    state_shape = jax.ShapeDtypeStruct((tokens, width), jnp.float32)
    return pl.pallas_call(
        lambda *refs: attend_kernel(*refs, with_own=with_own),
        grid_spec=pltpu.PrefetchScalarGridSpec(
            num_scalar_prefetch=2,
            grid=(heads, steps),
            in_specs=in_specs,
            out_specs=[out_spec, out_spec, out_spec],
        ),
        out_shape=[state_shape, state_shape, state_shape],
        compiler_params=pltpu.CompilerParams(dimension_semantics=("arbitrary", "arbitrary")),
    )(order, count, *operands)


def lookup(values_table, positions):
    table_width = values_table.shape[0]
    matches = positions[..., None] == jnp.arange(table_width, dtype=jnp.int32)
    return jnp.sum(jnp.where(matches, values_table, 0), axis=-1)


def pair_schedule(frames, slots, page_table, frame_lists, list_counts):
    max_slots = frame_lists.shape[1]
    dest = jnp.arange(frames, dtype=jnp.int32)[:, None]
    slot = jnp.arange(slots, dtype=jnp.int32)[None, :]
    even = dest - dest % 2
    combined = jnp.minimum((dest % 2) * slots + slot, max_slots)
    even_count = lookup(list_counts, even)
    for_even = combined < even_count
    listed_even = lookup(frame_lists.reshape(-1), even * max_slots + jnp.minimum(combined, max_slots - 1))
    listed_odd = lookup(
        frame_lists.reshape(-1),
        (even + 1) * max_slots + jnp.clip(combined - even_count, 0, max_slots - 1),
    )
    listed = jnp.where(for_even, listed_even, listed_odd)
    return lookup(page_table, (even // CF) * NC + listed)


def local(
    span_queries,
    span_keys,
    span_values,
    cache_keys,
    cache_values,
    page_table,
    frame_lists,
    list_counts,
    out_weight,
):
    frames = lax.axis_size(FRAME_AXES)
    own_frame = lax.axis_index(FRAME_AXES)
    tokens_here = span_queries.shape[1]
    row_width = span_queries.shape[2]
    heads_here = row_width // HD
    max_slots = frame_lists.shape[1]
    pair_blocks = max_slots + 1
    slots = (pair_blocks + 1) // 2
    own_queries = span_queries[0]
    own_keys = span_keys[0]
    own_values = span_values[0]

    weight = lax.all_gather(out_weight, ("zl", "x"), axis=1, tiled=True)
    weight = lax.all_gather(weight, "y", axis=1, tiled=True)

    blocks = pair_schedule(frames, slots, page_table, frame_lists, list_counts).T
    sent = jnp.stack([cache_keys[blocks], cache_values[blocks]], axis=0)
    arrived = lax.all_to_all(sent, FRAME_AXES, split_axis=2, concat_axis=2, tiled=True)
    arrived = arrived.reshape(2, slots, tokens_here, row_width)

    swap = [(i, i ^ 1) for i in range(lax.axis_size("x"))]
    partner_queries = lax.ppermute(own_queries, "x", swap)
    odd = own_frame % 2
    even_count = lookup(list_counts, own_frame - odd)
    other_count = jnp.where(
        odd == 0, jnp.maximum(0, slots - even_count), jnp.maximum(0, even_count - slots)
    )
    mine_count = jnp.where(
        odd == 0, jnp.minimum(even_count, slots), pair_blocks - jnp.maximum(even_count, slots)
    )
    step = jnp.arange(slots, dtype=jnp.int32)
    visit = jnp.where(odd == 0, slots - 1 - step, step)
    own_visit = jnp.where(odd == 0, slots - 1 - jnp.minimum(step + other_count, slots - 1),
                          jnp.minimum(step + other_count, slots - 1))

    other_out, other_max, other_sum = attend(
        partner_queries, arrived, visit, other_count.reshape(1)
    )
    got_max, got_sum, got_out = lax.ppermute(
        (other_max[:, ::HD], other_sum[:, ::HD], other_out), "x", swap
    )
    own_out, own_max, own_sum = attend(
        own_queries, arrived, own_visit, mine_count.reshape(1), own_keys, own_values
    )
    got_max = jnp.repeat(got_max, HD, axis=1)
    got_sum = jnp.repeat(got_sum, HD, axis=1)
    top = jnp.maximum(own_max, got_max)
    own_scale = jnp.exp(own_max - top)
    got_scale = jnp.exp(got_max - top)
    total_sum = own_sum * own_scale + got_sum * got_scale
    total_out = own_out * own_scale + got_out * got_scale
    attended = (total_out / total_sum).astype(jnp.bfloat16)
    partial_value = jnp.dot(attended, weight, preferred_element_type=jnp.float32)
    own_rows = lax.psum_scatter(
        partial_value.astype(jnp.bfloat16), "clip", scatter_dimension=0, tiled=True
    )
    return own_rows[None]


def solution(mesh):
    frames = mesh.shape["fsdp"]
    fine = Mesh(
        np.asarray(mesh.devices).reshape(mesh.shape["clip"], frames // 16, 4, 4),
        ("clip",) + FRAME_AXES,
    )
    in_specs = (
        P(FRAME_AXES, None, "clip"),
        P(FRAME_AXES, None, "clip"),
        P(FRAME_AXES, None, "clip"),
        P(None, FRAME_AXES, "clip"),
        P(None, FRAME_AXES, "clip"),
        P(),
        P(),
        P(),
        P("clip", FRAME_AXES),
    )
    out_specs = P(FRAME_AXES, "clip", None)
    return jax.shard_map(local, mesh=fine, in_specs=in_specs, out_specs=out_specs, check_vma=False)
```

time: 360 us -> 357 us (level)
  Pallas kernels: 0 us -> 43.4 us
  local copies, waits for them, and re-layouts: 49.4 us -> 23.7 us
  starting transfers between devices: 20.9 us -> 45.3 us
  waiting for transfers between devices: 230 us -> 208 us
  matrix products: 28.3 us -> 12.1 us
  other arithmetic: 11 us -> 7.07 us
    ppermute x1, waiting for transfers between devices: 51.6 us -> 0.01 us  [local(): partner_queries = lax.ppermute(own_queries, 'x', swap)]
    all_gather x1, waiting for transfers between devices: 24.1 us -> 73.9 us  [local(): weight = lax.all_gather(out_weight, ('zl', 'x'), axis=1, tiled=True)]
    pallas_call x0 -> x2, Pallas kernels: none -> 43.4 us  [attend(): pl.pallas_call(lambda *refs: attend_kernel(*refs, with_own=with_own), gri...]
    ppermute x3, starting transfers between devices: 8.14 us -> 32 us  [local(): lax.ppermute((other_max[:, ::HD], other_sum[:, ::HD], other_out), 'x', swap)]
    dot_general x8 -> x0, matrix products: 19.4 us -> none  [the longest x4 12.4 us: absorb(): jnp.einsum('qhk,khd->qhd', weights.astype(jnp.bfloat16), value_block, pre...]
    reduce_scatter x1, waiting for transfers between devices: 110 us -> 93 us  [local(): lax.psum_scatter(partial_value.astype(jnp.bfloat16), 'clip', scatter_dime...]
    ppermute x3, waiting for transfers between devices: 16.7 us -> 0.01 us  [local(): lax.ppermute((other_max[:, ::HD], other_sum[:, ::HD], other_out), 'x', swap)]
    while x8 -> x0, local copies, waits for them, and re-layouts: 15.9 us -> none  [the longest x4 13.7 us: local(): lax.fori_loop(other_count, other_count + mine_count, advance_own, own_state)]
  transfers between devices with their start and end apart: 8 -> 8, of which waited for: 5 -> 3; matrix products, arithmetic and copies ran while one was open for 18% -> 8% of each run, Pallas kernels for 0% -> 12%
where the time goes in v3:
time: 357 us; the launch traced here: 355 us
  waiting for transfers between devices  208 us (58%)
  starting transfers between devices  45.3 us (13%)
  Pallas kernels  43.4 us (12%)
  local copies, waits for them, and re-layouts  23.7 us (7%)
  between operations  16 us (4%)
  matrix products  12.1 us (3%)
  other arithmetic  7.07 us (2%)
    reduce_scatter x1, waiting for transfers between devices, local(): lax.psum_scatter(partial_value.astype(jnp.bfloat16), 'clip', scatter_dime...  93 us
    all_gather x1, waiting for transfers between devices, local(): weight = lax.all_gather(out_weight, ('zl', 'x'), axis=1, tiled=True)  73.9 us
    pallas_call x2, Pallas kernels, attend(): pl.pallas_call(lambda *refs: attend_kernel(*refs, with_own=with_own), gri...  43.4 us
    all_to_all x1, waiting for transfers between devices, local(): lax.all_to_all(sent, FRAME_AXES, split_axis=2, concat_axis=2, tiled=True)  40 us
    ppermute x3, starting transfers between devices, local(): lax.ppermute((other_max[:, ::HD], other_sum[:, ::HD], other_out), 'x', swap)  32 us
    dot_general x1, matrix products, local(): jnp.dot(attended, weight, preferred_element_type=jnp.float32)  12.1 us
    all_to_all x1, starting transfers between devices, local(): lax.all_to_all(sent, FRAME_AXES, split_axis=2, concat_axis=2, tiled=True)  11.7 us
  transfers between devices with their start and end apart: 8, of which 3 were waited for; matrix products, arithmetic and copies ran while one was open for 8% of the time, Pallas kernels for 12%

profile of v3, /device:TPU:50, one launch (start us, length us, event | category | flops | bytes accessed | tf_op | source)
XLA Modules:
  0.0 355.2 jit_solution(5689870379597072795)
XLA Ops:
  6.5 0.0 copy-start
  6.5 0.0 all-gather.3.cloned.1.call-start
  6.5 0.7 all-gather.3.cloned.1.call-update
  7.3 0.8 copy.31
  8.1 0.1 reshape.289
  8.2 0.8 select_reduce_fusion.3
  9.1 0.3 select_reduce_fusion
  9.4 0.9 select_reduce_fusion.2
  10.3 0.1 reshape.296
  10.4 0.0 copy-done
  10.4 0.0 copy-start.1
  10.4 2.4 gather_fusion
  12.9 0.0 copy-done.1
  12.9 2.4 gather_fusion.1
  15.3 3.1 pad_maximum_fusion
  18.4 3.2 copy.32
  21.6 11.7 %all-to-all-start = ((bf16[2,4,64,8,640]{4,3,1,0,2:T(8,128)(2,1)}), bf16[2,4,64,8,640]{4,3,1,0,2:T(8,128)(2,1)}, u32[]{:S(2)}, u32[]{:S(2)}) async-start(bf16[2,4,64,8,640]{4,3,1,0,2:T(8,128)(2,1)} %copy.32), calls=%async_computation | async-start | bytes 10485760 | tf_op jit(solution)/shard_map/all_to_all | solution.py:146
  33.3 0.0 copy-start.2
  33.4 0.0 copy-start.4
  33.4 0.0 all-gather.5.cloned.1.call-start
  33.4 73.9 %all-gather.3.cloned.1.call-done = bf16[640,1280]{0,1:T(8,128)(2,1)} async-done(((bf16[640,80]{0,1:T(8,128)(2,1)}), bf16[640,1280]{0,1:T(8,128)(2,1)}) %all-gather.3.cloned.1.call-update) | async-done | bytes 1638416 | tf_op jit(solution)/shard_map/all_gather | solution.py:141
  107.3 0.0 all-gather.5.cloned.1.call-update
  107.3 0.0 reduce-scatter.2.cloned.1.call-start
  107.3 0.0 copy-done.2
  107.4 1.5 collective-permute-start
  108.8 0.0 copy-done.4
  108.8 0.7 fusion.3
  110.9 0.6 broadcast_select_fusion.refs_0_
  111.5 40.0 %all-to-all-done = bf16[2,4,64,8,640]{4,3,1,0,2:T(8,128)(2,1)} async-done(((bf16[2,4,64,8,640]{4,3,1,0,2:T(8,128)(2,1)}), bf16[2,4,64,8,640]{4,3,1,0,2:T(8,128)(2,1)}, u32[]{:S(2)}, u32[]{:S(2)}) %all-to-all-start) | async-done | bytes 5242912 | tf_op jit(solution)/shard_map/all_to_all | solution.py:146
  151.5 5.3 %copy.40 = bf16[2,4,64,8,640]{4,3,2,1,0:T(8,128)(2,1)} copy(bf16[2,4,64,8,640]{4,3,1,0,2:T(8,128)(2,1)} %all-to-all-done) | data formatting | bytes 10485760 | tf_op jit(solution)/shard_map/all_to_all | solution.py:146
  156.8 0.0 collective-permute-done.refs_2_
  156.8 0.0 copy-start.3
  156.9 0.8 copy-done.3
  157.7 9.3 %shard_map.92 = (f32[512,640]{1,0:T(8,128)}, f32[512,640]{1,0:T(8,128)}, f32[512,640]{1,0:T(8,128)}) custom-call(s32[4]{0:T(128)} %broadcast_select_fusion.refs_0_, s32[1]{0:T(128)} %bitcast.8.refs_1_, bf16[512,640]{1,0:T(8,128)(2,1)} %copy-done.3, bf16[2,4,512,640]{3,2,1,0:T(8,128)(2,1)} %bitcast.16, bf16[2,4,512,640]{3,2,1,0:T(8,128)(2,1)} %bitcast.17), custom_call_target="tpu_custom_call" | custom-call | tf_op jit(solution)/shard_map/pallas_call | solution.py:82
  167.0 29.7 %collective-permute-start.2 = (f32[512,640]{1,0:T(8,128)}, f32[512,640]{1,0:T(8,128)}, u32[]{:S(2)}, u32[]{:S(2)}) collective-permute-start(f32[512,640]{1,0:T(8,128)} %get-tuple-element.14), channel_id=1, source_target_pairs={{0,1},{1,0},{2,3},{3,2},{4,5},{5,4},{6,7},{7,6},{8,9},{9,8},{10,11... | collective-permute-start | bytes 3932168 | tf_op jit(solution)/shard_map/ppermute | solution.py:167
  196.7 2.4 slice.6
  199.2 0.1 collective-permute-start.1
  199.3 2.4 slice.7
  201.7 2.3 collective-permute-start.3
  204.0 0.6 broadcast_select_fusion.1.refs_0_
  206.0 34.1 %shard_map.91 = (f32[512,640]{1,0:T(8,128)}, f32[512,640]{1,0:T(8,128)}, f32[512,640]{1,0:T(8,128)}) custom-call(s32[4]{0:T(128)} %broadcast_select_fusion.1.refs_0_, s32[1]{0:T(128)} %bitcast.refs_1_, bf16[512,640]{1,0:T(8,128)(2,1)} %bitcast.24, bf16[2,4,512,640]{3,2,1,0:T(8,128)(2,1)} %bitcast.18, bf16[2,4,512,640]{3,2,1,0:T(8,128)(2,1)} %bitcast.19, ...), custom_call_target="tpu_custom_call" | custom-call | tf_op jit(solution)/shard_map/pallas_call | solution.py:82
  240.0 0.0 collective-permute-done.1
  240.0 0.1 copy.34
  240.1 0.2 broadcast_in_dim.62
  240.3 1.5 copy.35
  241.8 0.0 collective-permute-done.3
  241.8 0.1 copy.37
  241.9 0.2 broadcast_in_dim.63
  242.1 1.5 copy.38
  243.6 0.0 collective-permute-done.2
  243.6 0.0 all-gather.5.cloned.1.call-done
  243.6 12.1 %convolution_convert_fusion = bf16[512,5120]{1,0:T(8,128)(2,1)} fusion(bf16[640,5120]{0,1:T(8,128)(2,1)} %all-gather.5.cloned.1.call-done, f32[512,640]{1,0:T(8,128)} %copy.38, f32[512,640]{1,0:T(8,128)} %get-tuple-element.15, f32[512,640]{1,0:T(8,128)} %collective-permute-done.2, f32[512,640]{1,0:T(8,128)} %copy.35, f32[512,640]{1,0:T(8,128)} %get-tuple-element.12, ...), kind=kOutput, calls=%fused_computation.2 | convolution fusion | flops 3361669120 | bytes 19660800 | tf_op jit(solution)/shard_map/dot_general | solution.py:181
  255.7 0.0 reduce-scatter.2.cloned.1.call-update
  255.7 93.0 %reduce-scatter.2.cloned.1.call-done = bf16[128,5120]{1,0:T(8,128)(2,1)} async-done(((bf16[512,5120]{1,0:T(8,128)(2,1)}), bf16[128,5120]{1,0:T(8,128)(2,1)}) %reduce-scatter.2.cloned.1.call-update) | async-done | bytes 1310736 | tf_op jit(solution)/shard_map/reduce_scatter | solution.py:182
  (7 shorter events, 0.1 us)
Async XLA Ops:
  6.5 3.9 %copy-start = (bf16[128,8,640]{2,1,0:T(8,128)(2,1)S(1)}, bf16[128,8,640]{2,1,0:T(8,128)(2,1)}, u32[]{:S(2)}) copy-start(bf16[128,8,640]{2,1,0:T(8,128)(2,1)} %param.12) | copy-start | bytes 3932164
  6.5 100.7 %all-gather.3.cloned.1.call-start = ((), (), s32[]{:S(2)}) async-start(), calls=%async_computation.2 | async-start | bytes 1740800 | tf_op jit(solution)/shard_map/all_gather | solution.py:141
  10.4 2.5 copy-start.1
  21.6 129.9 %all-to-all-start = ((bf16[2,4,64,8,640]{4,3,1,0,2:T(8,128)(2,1)}), bf16[2,4,64,8,640]{4,3,1,0,2:T(8,128)(2,1)}, u32[]{:S(2)}, u32[]{:S(2)}) async-start(bf16[2,4,64,8,640]{4,3,1,0,2:T(8,128)(2,1)} %copy.32), calls=%async_computation | async-start | bytes 10485760 | tf_op jit(solution)/shard_map/all_to_all | solution.py:146
  33.3 74.0 %copy-start.2 = (bf16[1,512,640]{2,1,0:T(8,128)(2,1)S(1)}, bf16[1,512,640]{2,1,0:T(8,128)(2,1)}, u32[]{:S(2)}) copy-start(bf16[1,512,640]{2,1,0:T(8,128)(2,1)} %param.9) | copy-start | bytes 1966084
  33.4 75.5 %copy-start.4 = (s32[64]{0:T(128)S(1)}, s32[64]{0:T(128)}, u32[]{:S(2)}) copy-start(s32[64]{0:T(128)} %param.16) | copy-start | bytes 772
  33.4 210.2 %all-gather.5.cloned.1.call-start = ((), (), s32[]{:S(2)}) async-start(), calls=%async_computation.3 | async-start | bytes 8192000 | tf_op jit(solution)/shard_map/all_gather | solution.py:142
  107.3 241.4 %reduce-scatter.2.cloned.1.call-start = ((), (), s32[]{:S(2)}) async-start(), calls=%async_computation.4 | async-start | bytes 6553600 | tf_op jit(solution)/shard_map/reduce_scatter | solution.py:182
  107.4 49.5 %collective-permute-start = (bf16[512,640]{1,0:T(8,128)(2,1)S(1)}, bf16[512,640]{1,0:T(8,128)(2,1)S(1)}, u32[]{:S(2)}, u32[]{:S(2)}) collective-permute-start(bf16[512,640]{1,0:T(8,128)(2,1)S(1)} %bitcast.25), channel_id=1, source_target_pairs={{0,1},{1,0},{2,3},{3,2},{4,5},{5,4},{6,7},{7,6},{8,9},{9,8},{10,11... | collective-permute-start | bytes 1966088 | tf_op jit(solution)/shard_map/ppermute | solution.py:150
  156.8 0.9 copy-start.3
  167.0 76.5 %collective-permute-start.2 = (f32[512,640]{1,0:T(8,128)}, f32[512,640]{1,0:T(8,128)}, u32[]{:S(2)}, u32[]{:S(2)}) collective-permute-start(f32[512,640]{1,0:T(8,128)} %get-tuple-element.14), channel_id=1, source_target_pairs={{0,1},{1,0},{2,3},{3,2},{4,5},{5,4},{6,7},{7,6},{8,9},{9,8},{10,11... | collective-permute-start | bytes 3932168 | tf_op jit(solution)/shard_map/ppermute | solution.py:167
  199.2 40.9 %collective-permute-start.1 = (f32[512,5]{1,0:T(8,128)S(1)}, f32[512,5]{1,0:T(8,128)S(1)}, u32[]{:S(2)}, u32[]{:S(2)}) collective-permute-start(f32[512,5]{1,0:T(8,128)S(1)} %slice.6), channel_id=1, source_target_pairs={{0,1},{1,0},{2,3},{3,2},{4,5},{5,4},{6,7},{7,6},{8,9},{9,8},{10,11... | collective-permute-start | bytes 30728 | tf_op jit(solution)/shard_map/ppermute | solution.py:167
  201.7 40.1 %collective-permute-start.3 = (f32[512,5]{1,0:T(8,128)S(1)}, f32[512,5]{1,0:T(8,128)S(1)}, u32[]{:S(2)}, u32[]{:S(2)}) collective-permute-start(f32[512,5]{1,0:T(8,128)S(1)} %slice.7), channel_id=1, source_target_pairs={{0,1},{1,0},{2,3},{3,2},{4,5},{5,4},{6,7},{7,6},{8,9},{9,8},{10,11... | collective-permute-start | bytes 30728 | tf_op jit(solution)/shard_map/ppermute | solution.py:167
Sparse Core Ops, SparseCore 0:
  9.1 98.1 all-gather.2
  109.1 88.5 all-gather.4
  255.8 92.8 reduce-scatter.1

commit v4 on v3

--- a/solution.py
+++ b/solution.py
@@ -69,13 +69,15 @@
         visit = jnp.clip(s - first, 0, jnp.maximum(count_ref[0] - 1, 0))
         return order_ref[visit]
 
+    keys_each = arrived.shape[2]
     q_spec = pl.BlockSpec((tokens, HD), lambda h, s, o, c: (0, h))
-    k_spec = pl.BlockSpec((1, 1, tokens, HD), lambda h, s, o, c: (0, slot_at(s, o, c), 0, h))
-    v_spec = pl.BlockSpec((1, 1, tokens, HD), lambda h, s, o, c: (1, slot_at(s, o, c), 0, h))
+    own_spec = pl.BlockSpec((keys_each, HD), lambda h, s, o, c: (0, h))
+    k_spec = pl.BlockSpec((1, 1, keys_each, HD), lambda h, s, o, c: (0, slot_at(s, o, c), 0, h))
+    v_spec = pl.BlockSpec((1, 1, keys_each, HD), lambda h, s, o, c: (1, slot_at(s, o, c), 0, h))
     in_specs = [q_spec, k_spec, v_spec]
     operands = [queries, arrived, arrived]
     if with_own:
-        in_specs += [q_spec, q_spec]
+        in_specs += [own_spec, own_spec]
         operands += [own_keys, own_values]
     out_spec = pl.BlockSpec((tokens, HD), lambda h, s, o, c: (0, h))
     state_shape = jax.ShapeDtypeStruct((tokens, width), jnp.float32)
@@ -161,27 +163,42 @@
     own_visit = jnp.where(odd == 0, slots - 1 - jnp.minimum(step + other_count, slots - 1),
                           jnp.minimum(step + other_count, slots - 1))
 
-    other_out, other_max, other_sum = attend(
-        partner_queries, arrived, visit, other_count.reshape(1)
-    )
-    got_max, got_sum, got_out = lax.ppermute(
-        (other_max[:, ::HD], other_sum[:, ::HD], other_out), "x", swap
-    )
-    own_out, own_max, own_sum = attend(
-        own_queries, arrived, own_visit, mine_count.reshape(1), own_keys, own_values
-    )
-    got_max = jnp.repeat(got_max, HD, axis=1)
-    got_sum = jnp.repeat(got_sum, HD, axis=1)
-    top = jnp.maximum(own_max, got_max)
-    own_scale = jnp.exp(own_max - top)
-    got_scale = jnp.exp(got_max - top)
-    total_sum = own_sum * own_scale + got_sum * got_scale
-    total_out = own_out * own_scale + got_out * got_scale
-    attended = (total_out / total_sum).astype(jnp.bfloat16)
-    partial_value = jnp.dot(attended, weight, preferred_element_type=jnp.float32)
-    own_rows = lax.psum_scatter(
-        partial_value.astype(jnp.bfloat16), "clip", scatter_dimension=0, tiled=True
-    )
+    quarters = lax.axis_size("clip")
+    quarter_rows = tokens_here // quarters
+    halves = 2
+
+    def half_rows(rows, half):
+        rows = rows.reshape(quarters, halves, quarter_rows // halves, rows.shape[-1])
+        return rows[:, half].reshape(tokens_here // halves, rows.shape[-1])
+
+    finished = []
+    for half in range(halves):
+        mine_q = half_rows(own_queries, half)
+        other_q = half_rows(partner_queries, half)
+        other_out, other_max, other_sum = attend(
+            other_q, arrived, visit, other_count.reshape(1)
+        )
+        got_max, got_sum, got_out = lax.ppermute(
+            (other_max[:, ::HD], other_sum[:, ::HD], other_out), "x", swap
+        )
+        own_out, own_max, own_sum = attend(
+            mine_q, arrived, own_visit, mine_count.reshape(1), own_keys, own_values
+        )
+        got_max = jnp.repeat(got_max, HD, axis=1)
+        got_sum = jnp.repeat(got_sum, HD, axis=1)
+        top = jnp.maximum(own_max, got_max)
+        own_scale = jnp.exp(own_max - top)
+        got_scale = jnp.exp(got_max - top)
+        total_sum = own_sum * own_scale + got_sum * got_scale
+        total_out = own_out * own_scale + got_out * got_scale
+        attended = (total_out / total_sum).astype(jnp.bfloat16)
+        partial_value = jnp.dot(attended, weight, preferred_element_type=jnp.float32)
+        finished.append(
+            lax.psum_scatter(
+                partial_value.astype(jnp.bfloat16), "clip", scatter_dimension=0, tiled=True
+            )
+        )
+    own_rows = jnp.concatenate(finished, axis=0)
     return own_rows[None]
 
 

time: 357 us -> 361 us (1.011)
  Pallas kernels: 43.4 us -> 61.5 us
  waiting for transfers between devices: 208 us -> 190 us
    all_to_all x1, waiting for transfers between devices: 40 us -> 20.7 us  [local(): lax.all_to_all(sent, FRAME_AXES, split_axis=2, concat_axis=2, tiled=True)]
    ppermute x1, waiting for transfers between devices: 0.01 us -> 18.1 us  [local(): partner_queries = lax.ppermute(own_queries, 'x', swap)]
    pallas_call x2 -> x4, Pallas kernels: 43.4 us -> 61.5 us  [attend(): pl.pallas_call(lambda *refs: attend_kernel(*refs, with_own=with_own), gri...]
    reduce_scatter x1 -> x2, waiting for transfers between devices: 93 us -> 77.2 us  [local(): lax.psum_scatter(partial_value.astype(jnp.bfloat16), 'clip', scatter_dime...]
    dot_general x1 -> x2, matrix products: 12.1 us -> 15.2 us  [local(): jnp.dot(attended, weight, preferred_element_type=jnp.float32)]
    ppermute x3 -> x6, starting transfers between devices: 32 us -> 29.1 us  [local(): lax.ppermute((other_max[:, ::HD], other_sum[:, ::HD], other_out), 'x', swap)]
  transfers between devices with their start and end apart: 8 -> 12, of which waited for: 3 -> 5; matrix products, arithmetic and copies ran while one was open for 8% -> 10% of each run, Pallas kernels for 12% -> 17%
where the time goes in v4:
time: 361 us; the launch traced here: 358 us
  waiting for transfers between devices  190 us (53%)
  Pallas kernels  61.5 us (17%)
  starting transfers between devices  43.8 us (12%)
  local copies, waits for them, and re-layouts  23 us (6%)
  between operations  15.6 us (4%)
  matrix products  15.2 us (4%)
  other arithmetic  8.79 us (2%)
    reduce_scatter x2, waiting for transfers between devices, local(): lax.psum_scatter(partial_value.astype(jnp.bfloat16), 'clip', scatter_dime...  77.2 us
    all_gather x1, waiting for transfers between devices, local(): weight = lax.all_gather(out_weight, ('zl', 'x'), axis=1, tiled=True)  73.3 us
    pallas_call x4, Pallas kernels, attend(): pl.pallas_call(lambda *refs: attend_kernel(*refs, with_own=with_own), gri...  61.5 us
    ppermute x6, starting transfers between devices, local(): lax.ppermute((other_max[:, ::HD], other_sum[:, ::HD], other_out), 'x', swap)  29.1 us
    all_to_all x1, waiting for transfers between devices, local(): lax.all_to_all(sent, FRAME_AXES, split_axis=2, concat_axis=2, tiled=True)  20.7 us
    ppermute x1, waiting for transfers between devices, local(): partner_queries = lax.ppermute(own_queries, 'x', swap)  18.1 us
    dot_general x2, matrix products, local(): jnp.dot(attended, weight, preferred_element_type=jnp.float32)  15.2 us
    all_to_all x1, starting transfers between devices, local(): lax.all_to_all(sent, FRAME_AXES, split_axis=2, concat_axis=2, tiled=True)  11.8 us
  transfers between devices with their start and end apart: 12, of which 5 were waited for; matrix products, arithmetic and copies ran while one was open for 10% of the time, Pallas kernels for 17%

profile of v4, /device:TPU:50, one launch (start us, length us, event | category | flops | bytes accessed | tf_op | source)
XLA Modules:
  0.0 358.0 jit_solution(6552140539097413745)
XLA Ops:
  6.5 0.7 all-gather.3.cloned.1.call-update
  7.3 0.8 copy.63
  8.0 0.1 reshape.301
  8.2 0.8 select_reduce_fusion.3
  9.1 0.3 select_reduce_fusion
  9.4 0.9 select_reduce_fusion.2
  10.3 0.1 reshape.311
  10.4 0.0 copy-start.1
  10.4 2.4 gather_fusion
  12.9 2.4 gather_fusion.1
  15.3 3.1 pad_maximum_fusion
  18.4 3.2 copy.64
  21.6 11.8 %all-to-all-start = ((bf16[2,4,64,8,640]{4,3,1,0,2:T(8,128)(2,1)}), bf16[2,4,64,8,640]{4,3,1,0,2:T(8,128)(2,1)}, u32[]{:S(2)}, u32[]{:S(2)}) async-start(bf16[2,4,64,8,640]{4,3,1,0,2:T(8,128)(2,1)} %copy.64), calls=%async_computation | async-start | bytes 10485760 | tf_op jit(solution)/shard_map/all_to_all | solution.py:148
  33.4 0.0 all-gather.5.cloned.1.call-start
  33.5 73.3 %all-gather.3.cloned.1.call-done = bf16[640,1280]{0,1:T(8,128)(2,1)} async-done(((bf16[640,80]{0,1:T(8,128)(2,1)}), bf16[640,1280]{0,1:T(8,128)(2,1)}) %all-gather.3.cloned.1.call-update) | async-done | bytes 1638416 | tf_op jit(solution)/shard_map/all_gather | solution.py:143
  106.8 0.0 all-gather.5.cloned.1.call-update
  106.8 0.0 reduce-scatter.3.cloned.1.call-start
  106.9 2.7 collective-permute-start
  109.6 0.6 fusion.5
  111.3 0.6 broadcast_select_fusion
  111.9 18.1 %collective-permute-done = bf16[512,640]{1,0:T(8,128)(2,1)S(1)} collective-permute-done((bf16[512,640]{1,0:T(8,128)(2,1)S(1)}, bf16[512,640]{1,0:T(8,128)(2,1)S(1)}, u32[]{:S(2)}, u32[]{:S(2)}) %collective-permute-start) | collective-permute-done | bytes 655392 | tf_op jit(solution)/shard_map/ppermute | solution.py:152
  130.0 0.9 fusion.8
  130.9 20.7 %all-to-all-done = bf16[2,4,64,8,640]{4,3,1,0,2:T(8,128)(2,1)} async-done(((bf16[2,4,64,8,640]{4,3,1,0,2:T(8,128)(2,1)}), bf16[2,4,64,8,640]{4,3,1,0,2:T(8,128)(2,1)}, u32[]{:S(2)}, u32[]{:S(2)}) %all-to-all-start) | async-done | bytes 5242912 | tf_op jit(solution)/shard_map/all_to_all | solution.py:148
  151.7 5.3 %copy.84 = bf16[2,4,64,8,640]{4,3,2,1,0:T(8,128)(2,1)} copy(bf16[2,4,64,8,640]{4,3,1,0,2:T(8,128)(2,1)} %all-to-all-done) | data formatting | bytes 10485760 | tf_op jit(solution)/shard_map/all_to_all | solution.py:148
  157.0 8.3 %shard_map.92 = (f32[256,640]{1,0:T(8,128)}, f32[256,640]{1,0:T(8,128)}, f32[256,640]{1,0:T(8,128)}) custom-call(s32[4]{0:T(128)} %get-tuple-element.37.refs_0_, s32[1]{0:T(128)} %bitcast.9.refs_1_, bf16[256,640]{1,0:T(8,128)(2,1)} %bitcast.55, bf16[2,4,512,640]{3,2,1,0:T(8,128)(2,1)} %bitcast.34, bf16[2,4,512,640]{3,2,1,0:T(8,128)(2,1)} %bitcast.35), custom_call_target="tpu_custom_call" | custom-call | tf_op jit(solution)/shard_map/pallas_call | solution.py:84
  165.3 21.8 %collective-permute-start.2 = (f32[256,640]{1,0:T(8,128)}, f32[256,640]{1,0:T(8,128)}, u32[]{:S(2)}, u32[]{:S(2)}) collective-permute-start(f32[256,640]{1,0:T(8,128)} %get-tuple-element.20), channel_id=1, source_target_pairs={{0,1},{1,0},{2,3},{3,2},{4,5},{5,4},{6,7},{7,6},{8,9},{9,8},{10,11... | collective-permute-start | bytes 1966088 | tf_op jit(solution)/shard_map/ppermute | solution.py:181
  187.1 1.3 slice.26
  188.4 0.1 collective-permute-start.1
  188.5 1.3 slice.27
  189.8 2.1 collective-permute-start.3
  191.9 0.9 fusion.7
  193.9 22.4 %shard_map.91 = (f32[256,640]{1,0:T(8,128)}, f32[256,640]{1,0:T(8,128)}, f32[256,640]{1,0:T(8,128)}) custom-call(s32[4]{0:T(128)} %get-tuple-element.38.refs_0_, s32[1]{0:T(128)} %bitcast.refs_1_, bf16[256,640]{1,0:T(8,128)(2,1)} %bitcast.54, bf16[2,4,512,640]{3,2,1,0:T(8,128)(2,1)} %bitcast.36, bf16[2,4,512,640]{3,2,1,0:T(8,128)(2,1)} %bitcast.37, ...), custom_call_target="tpu_custom_call" | custom-call | tf_op jit(solution)/shard_map/pallas_call | solution.py:84
  216.3 0.0 collective-permute-done.1
  216.3 0.1 copy.67
  216.4 0.1 broadcast_in_dim.68
  216.5 0.2 copy.68
  216.7 0.0 collective-permute-done.3
  216.7 0.1 copy.70
  216.8 0.1 broadcast_in_dim.69
  216.9 0.2 copy.71
  217.1 0.0 collective-permute-done.2
  217.1 0.0 all-gather.5.cloned.1.call-done
  217.1 7.6 %convolution_convert_fusion.1 = bf16[256,5120]{1,0:T(8,128)(2,1)} fusion(bf16[640,5120]{0,1:T(8,128)(2,1)} %all-gather.5.cloned.1.call-done, f32[256,640]{1,0:T(8,128)S(1)} %copy.71, f32[256,640]{1,0:T(8,128)} %get-tuple-element.21, f32[256,640]{1,0:T(8,128)} %collective-permute-done.2, f32[256,640]{1,0:T(8,128)S(1)} %copy.68, ...), kind=kOutput, calls=%fused_computation.3 | convolution fusion | flops 1680834560 | bytes 13107200 | tf_op jit(solution)/shard_map/dot_general | solution.py:195
  224.7 0.0 reduce-scatter.3.cloned.1.call-update
  224.8 0.0 reduce-scatter.5.cloned.1.call-start
  224.8 8.3 %shard_map.94 = (f32[256,640]{1,0:T(8,128)}, f32[256,640]{1,0:T(8,128)}, f32[256,640]{1,0:T(8,128)}) custom-call(s32[4]{0:T(128)} %get-tuple-element.37.refs_0_, s32[1]{0:T(128)} %bitcast.9.refs_1_, bf16[256,640]{1,0:T(8,128)(2,1)} %bitcast.52, bf16[2,4,512,640]{3,2,1,0:T(8,128)(2,1)} %bitcast.38, bf16[2,4,512,640]{3,2,1,0:T(8,128)(2,1)} %bitcast.39), custom_call_target="tpu_custom_call" | custom-call | tf_op jit(solution)/shard_map/pallas_call | solution.py:84
  233.1 2.8 collective-permute-start.5
  235.9 1.3 slice.30
  237.2 0.3 collective-permute-start.4
  237.5 1.4 slice.31
  238.9 2.0 collective-permute-start.6
  240.9 22.5 %shard_map.93 = (f32[256,640]{1,0:T(8,128)}, f32[256,640]{1,0:T(8,128)}, f32[256,640]{1,0:T(8,128)}) custom-call(s32[4]{0:T(128)} %get-tuple-element.38.refs_0_, s32[1]{0:T(128)} %bitcast.refs_1_, bf16[256,640]{1,0:T(8,128)(2,1)} %bitcast.53, bf16[2,4,512,640]{3,2,1,0:T(8,128)(2,1)} %bitcast.40, bf16[2,4,512,640]{3,2,1,0:T(8,128)(2,1)} %bitcast.41, ...), custom_call_target="tpu_custom_call" | custom-call | tf_op jit(solution)/shard_map/pallas_call | solution.py:84
  263.4 0.0 collective-permute-done.4
  263.4 0.1 copy.74
  263.4 0.1 broadcast_in_dim.70
  263.5 0.2 copy.75
  263.8 0.1 copy.77
  263.8 0.1 broadcast_in_dim.71
  263.9 0.2 copy.78
  264.2 7.6 %convolution_convert_fusion = bf16[256,5120]{1,0:T(8,128)(2,1)} fusion(bf16[640,5120]{0,1:T(8,128)(2,1)} %all-gather.5.cloned.1.call-done, f32[256,640]{1,0:T(8,128)S(1)} %copy.78, f32[256,640]{1,0:T(8,128)} %get-tuple-element.27, f32[256,640]{1,0:T(8,128)} %collective-permute-done.5, f32[256,640]{1,0:T(8,128)S(1)} %copy.75, ...), kind=kOutput, calls=%fused_computation.2 | convolution fusion | flops 1680834560 | bytes 13107200 | tf_op jit(solution)/shard_map/dot_general | solution.py:195
  271.8 0.0 reduce-scatter.5.cloned.1.call-update
  271.8 15.0 %reduce-scatter.3.cloned.1.call-done = bf16[64,5120]{1,0:T(8,128)(2,1)} async-done(((bf16[256,5120]{1,0:T(8,128)(2,1)}), bf16[64,5120]{1,0:T(8,128)(2,1)}) %reduce-scatter.3.cloned.1.call-update) | async-done | bytes 655376 | tf_op jit(solution)/shard_map/reduce_scatter | solution.py:197
  286.8 62.2 %reduce-scatter.5.cloned.1.call-done = bf16[64,5120]{1,0:T(8,128)(2,1)} async-done(((bf16[256,5120]{1,0:T(8,128)(2,1)}), bf16[64,5120]{1,0:T(8,128)(2,1)}) %reduce-scatter.5.cloned.1.call-update) | async-done | bytes 655376 | tf_op jit(solution)/shard_map/reduce_scatter | solution.py:197
  349.0 2.4 maximum_bitcast_fusion
  (17 shorter events, 0.1 us)
Async XLA Ops:
  6.5 3.9 %copy-start = (bf16[128,8,640]{2,1,0:T(8,128)(2,1)S(1)}, bf16[128,8,640]{2,1,0:T(8,128)(2,1)}, u32[]{:S(2)}) copy-start(bf16[128,8,640]{2,1,0:T(8,128)(2,1)} %param.12) | copy-start | bytes 3932164
  6.5 100.3 %all-gather.3.cloned.1.call-start = ((), (), s32[]{:S(2)}) async-start(), calls=%async_computation.3 | async-start | bytes 1740800 | tf_op jit(solution)/shard_map/all_gather | solution.py:143
  10.4 2.5 copy-start.1
  21.6 85.3 %copy-start.2 = (bf16[1,512,640]{2,1,0:T(8,128)(2,1)S(1)}, bf16[1,512,640]{2,1,0:T(8,128)(2,1)}, u32[]{:S(2)}) copy-start(bf16[1,512,640]{2,1,0:T(8,128)(2,1)} %param.9) | copy-start | bytes 1966084
  21.6 88.0 %copy-start.3 = (s32[64]{0:T(128)S(1)}, s32[64]{0:T(128)}, u32[]{:S(2)}) copy-start(s32[64]{0:T(128)} %param.16) | copy-start | bytes 772
  21.6 130.1 %all-to-all-start = ((bf16[2,4,64,8,640]{4,3,1,0,2:T(8,128)(2,1)}), bf16[2,4,64,8,640]{4,3,1,0,2:T(8,128)(2,1)}, u32[]{:S(2)}, u32[]{:S(2)}) async-start(bf16[2,4,64,8,640]{4,3,1,0,2:T(8,128)(2,1)} %copy.64), calls=%async_computation | async-start | bytes 10485760 | tf_op jit(solution)/shard_map/all_to_all | solution.py:148
  33.4 183.7 %all-gather.5.cloned.1.call-start = ((), (), s32[]{:S(2)}) async-start(), calls=%async_computation.4 | async-start | bytes 8192000 | tf_op jit(solution)/shard_map/all_gather | solution.py:144
  106.8 180.0 %reduce-scatter.3.cloned.1.call-start = ((), (), s32[]{:S(2)}) async-start(), calls=%async_computation.5 | async-start | bytes 3276800 | tf_op jit(solution)/shard_map/reduce_scatter | solution.py:197
  106.9 23.1 %collective-permute-start = (bf16[512,640]{1,0:T(8,128)(2,1)S(1)}, bf16[512,640]{1,0:T(8,128)(2,1)S(1)}, u32[]{:S(2)}, u32[]{:S(2)}) collective-permute-start(bf16[512,640]{1,0:T(8,128)(2,1)S(1)} %bitcast.56), channel_id=1, source_target_pairs={{0,1},{1,0},{2,3},{3,2},{4,5},{5,4},{6,7},{7,6},{8,9},{9,8},{10,11... | collective-permute-start | bytes 1966088 | tf_op jit(solution)/shard_map/ppermute | solution.py:152
  165.3 51.8 %collective-permute-start.2 = (f32[256,640]{1,0:T(8,128)}, f32[256,640]{1,0:T(8,128)}, u32[]{:S(2)}, u32[]{:S(2)}) collective-permute-start(f32[256,640]{1,0:T(8,128)} %get-tuple-element.20), channel_id=1, source_target_pairs={{0,1},{1,0},{2,3},{3,2},{4,5},{5,4},{6,7},{7,6},{8,9},{9,8},{10,11... | collective-permute-start | bytes 1966088 | tf_op jit(solution)/shard_map/ppermute | solution.py:181
  188.4 27.9 %collective-permute-start.1 = (f32[256,5]{1,0:T(8,128)S(1)}, f32[256,5]{1,0:T(8,128)S(1)}, u32[]{:S(2)}, u32[]{:S(2)}) collective-permute-start(f32[256,5]{1,0:T(8,128)S(1)} %slice.26), channel_id=1, source_target_pairs={{0,1},{1,0},{2,3},{3,2},{4,5},{5,4},{6,7},{7,6},{8,9},{9,8},{10,11... | collective-permute-start | bytes 15368 | tf_op jit(solution)/shard_map/ppermute | solution.py:181
  189.8 26.9 %collective-permute-start.3 = (f32[256,5]{1,0:T(8,128)S(1)}, f32[256,5]{1,0:T(8,128)S(1)}, u32[]{:S(2)}, u32[]{:S(2)}) collective-permute-start(f32[256,5]{1,0:T(8,128)S(1)} %slice.27), channel_id=1, source_target_pairs={{0,1},{1,0},{2,3},{3,2},{4,5},{5,4},{6,7},{7,6},{8,9},{9,8},{10,11... | collective-permute-start | bytes 15368 | tf_op jit(solution)/shard_map/ppermute | solution.py:181
  224.8 124.3 %reduce-scatter.5.cloned.1.call-start = ((), (), s32[]{:S(2)}) async-start(), calls=%async_computation.6 | async-start | bytes 3276800 | tf_op jit(solution)/shard_map/reduce_scatter | solution.py:197
  233.1 31.0 %collective-permute-start.5 = (f32[256,640]{1,0:T(8,128)}, f32[256,640]{1,0:T(8,128)}, u32[]{:S(2)}, u32[]{:S(2)}) collective-permute-start(f32[256,640]{1,0:T(8,128)} %get-tuple-element.26), channel_id=1, source_target_pairs={{0,1},{1,0},{2,3},{3,2},{4,5},{5,4},{6,7},{7,6},{8,9},{9,8},{10,11... | collective-permute-start | bytes 1966088 | tf_op jit(solution)/shard_map/ppermute | solution.py:181
  237.2 26.2 %collective-permute-start.4 = (f32[256,5]{1,0:T(8,128)S(1)}, f32[256,5]{1,0:T(8,128)S(1)}, u32[]{:S(2)}, u32[]{:S(2)}) collective-permute-start(f32[256,5]{1,0:T(8,128)S(1)} %slice.30), channel_id=1, source_target_pairs={{0,1},{1,0},{2,3},{3,2},{4,5},{5,4},{6,7},{7,6},{8,9},{9,8},{10,11... | collective-permute-start | bytes 15368 | tf_op jit(solution)/shard_map/ppermute | solution.py:181
  238.9 24.9 %collective-permute-start.6 = (f32[256,5]{1,0:T(8,128)S(1)}, f32[256,5]{1,0:T(8,128)S(1)}, u32[]{:S(2)}, u32[]{:S(2)}) collective-permute-start(f32[256,5]{1,0:T(8,128)S(1)} %slice.31), channel_id=1, source_target_pairs={{0,1},{1,0},{2,3},{3,2},{4,5},{5,4},{6,7},{7,6},{8,9},{9,8},{10,11... | collective-permute-start | bytes 15368 | tf_op jit(solution)/shard_map/ppermute | solution.py:181
Sparse Core Ops, SparseCore 0:
  9.1 97.6 all-gather.2
  108.6 89.8 all-gather.4
  224.9 61.8 reduce-scatter.2
  289.5 59.5 reduce-scatter.4

commit v5 on v3

--- a/solution.py
+++ b/solution.py
@@ -18,77 +18,79 @@
 neg_fill = -1e30
 
 
-def attend_kernel(order_ref, count_ref, q_ref, k_ref, v_ref, *rest, with_own):
-    if with_own:
-        own_k_ref, own_v_ref, o_ref, m_ref, l_ref = rest
+def attend_kernel(order_ref, count_ref, q_ref, k_ref, v_ref, *rest, with_init, heads):
+    if with_init:
+        o0_ref, m0_ref, l0_ref, o_ref, m_ref, l_ref = rest
     else:
         o_ref, m_ref, l_ref = rest
-    step = pl.program_id(1)
-    first = 1 if with_own else 0
+    step = pl.program_id(0)
 
     @pl.when(step == 0)
     def _init():
-        m_ref[...] = jnp.full(m_ref.shape, neg_fill, jnp.float32)
-        l_ref[...] = jnp.zeros(l_ref.shape, jnp.float32)
-        o_ref[...] = jnp.zeros(o_ref.shape, jnp.float32)
-
-    def absorb(key_block, value_block):
-        scores = lax.dot_general(
-            q_ref[...], key_block, (((1,), (1,)), ((), ())),
-            preferred_element_type=jnp.float32,
-        ) * (1.0 / math.sqrt(HD))
-        running_max = m_ref[:, :1]
-        new_max = jnp.maximum(running_max, jnp.max(scores, axis=1, keepdims=True))
-        shrink = jnp.exp(running_max - new_max)
-        weights = jnp.exp(scores - new_max)
-        l_ref[...] = l_ref[...] * shrink + jnp.sum(weights, axis=1, keepdims=True)
-        o_ref[...] = o_ref[...] * shrink + jnp.dot(
-            weights.astype(jnp.bfloat16), value_block, preferred_element_type=jnp.float32
-        )
-        m_ref[...] = jnp.broadcast_to(new_max, m_ref.shape)
-
-    if with_own:
-        @pl.when(step == 0)
-        def _own():
-            absorb(own_k_ref[...], own_v_ref[...])
-
-    @pl.when((step >= first) & (step - first < count_ref[0]))
+        if with_init:
+            m_ref[...] = m0_ref[...]
+            l_ref[...] = l0_ref[...]
+            o_ref[...] = o0_ref[...]
+        else:
+            m_ref[...] = jnp.full(m_ref.shape, neg_fill, jnp.float32)
+            l_ref[...] = jnp.zeros(l_ref.shape, jnp.float32)
+            o_ref[...] = jnp.zeros(o_ref.shape, jnp.float32)
+
+    @pl.when(step < count_ref[0])
     def _slot():
-        absorb(k_ref[0, 0], v_ref[0, 0])
-
-
-def attend(queries, arrived, order, count, own_keys=None, own_values=None):
+        for head in range(heads):
+            cols = pl.ds(head * HD, HD)
+            scores = lax.dot_general(
+                q_ref[:, cols], k_ref[0, 0, :, cols], (((1,), (1,)), ((), ())),
+                preferred_element_type=jnp.float32,
+            ) * (1.0 / math.sqrt(HD))
+            running_max = m_ref[:, pl.ds(head * HD, 1)]
+            new_max = jnp.maximum(running_max, jnp.max(scores, axis=1, keepdims=True))
+            shrink = jnp.exp(running_max - new_max)
+            weights = jnp.exp(scores - new_max)
+            l_ref[:, cols] = l_ref[:, cols] * shrink + jnp.sum(weights, axis=1, keepdims=True)
+            o_ref[:, cols] = o_ref[:, cols] * shrink + jnp.dot(
+                weights.astype(jnp.bfloat16), v_ref[0, 0, :, cols],
+                preferred_element_type=jnp.float32,
+            )
+            m_ref[:, cols] = jnp.broadcast_to(new_max, (new_max.shape[0], HD))
+
+
+def attend(queries, arrived, order, count, init=None):
     tokens, width = queries.shape
     slots = arrived.shape[1]
+    keys_each = arrived.shape[2]
     heads = width // HD
-    with_own = own_keys is not None
-    first = 1 if with_own else 0
-    steps = slots + first
+    with_init = init is not None
 
     def slot_at(s, order_ref, count_ref):
-        visit = jnp.clip(s - first, 0, jnp.maximum(count_ref[0] - 1, 0))
-        return order_ref[visit]
-
-    q_spec = pl.BlockSpec((tokens, HD), lambda h, s, o, c: (0, h))
-    k_spec = pl.BlockSpec((1, 1, tokens, HD), lambda h, s, o, c: (0, slot_at(s, o, c), 0, h))
-    v_spec = pl.BlockSpec((1, 1, tokens, HD), lambda h, s, o, c: (1, slot_at(s, o, c), 0, h))
+        return order_ref[jnp.clip(s, 0, jnp.maximum(count_ref[0] - 1, 0))]
+
+    q_spec = pl.BlockSpec((tokens, width), lambda s, o, c: (0, 0))
+    k_spec = pl.BlockSpec((1, 1, keys_each, width), lambda s, o, c: (0, slot_at(s, o, c), 0, 0))
+    v_spec = pl.BlockSpec((1, 1, keys_each, width), lambda s, o, c: (1, slot_at(s, o, c), 0, 0))
     in_specs = [q_spec, k_spec, v_spec]
     operands = [queries, arrived, arrived]
-    if with_own:
-        in_specs += [q_spec, q_spec]
-        operands += [own_keys, own_values]
-    out_spec = pl.BlockSpec((tokens, HD), lambda h, s, o, c: (0, h))
+    state_spec = pl.BlockSpec((tokens, width), lambda s, o, c: (0, 0))
+    if with_init:
+        in_specs += [state_spec] * 3
+        operands += list(init)
     state_shape = jax.ShapeDtypeStruct((tokens, width), jnp.float32)
     return pl.pallas_call(
-        lambda *refs: attend_kernel(*refs, with_own=with_own),
+        lambda *refs: attend_kernel(*refs, with_init=with_init, heads=heads),
         grid_spec=pltpu.PrefetchScalarGridSpec(
             num_scalar_prefetch=2,
-            grid=(heads, steps),
+            grid=(slots,),
             in_specs=in_specs,
-            out_specs=[out_spec, out_spec, out_spec],
+            out_specs=[state_spec] * 3,
         ),
-        out_shape=[state_shape, state_shape, state_shape],
-        compiler_params=pltpu.CompilerParams(dimension_semantics=("arbitrary", "arbitrary")),
+        out_shape=[state_shape] * 3,
+        compiler_params=pltpu.CompilerParams(dimension_semantics=("arbitrary",)),
+        cost_estimate=pl.CostEstimate(
+            flops=4 * slots * tokens * keys_each * width,
+            transcendentals=slots * heads * tokens * keys_each,
+            bytes_accessed=2 * slots * keys_each * width * 2 + 6 * tokens * width * 4,
+        ),
     )(order, count, *operands)
 
 
@@ -139,7 +141,6 @@
     own_values = span_values[0]
 
     weight = lax.all_gather(out_weight, ("zl", "x"), axis=1, tiled=True)
-    weight = lax.all_gather(weight, "y", axis=1, tiled=True)
 
     blocks = pair_schedule(frames, slots, page_table, frame_lists, list_counts).T
     sent = jnp.stack([cache_keys[blocks], cache_values[blocks]], axis=0)
@@ -161,6 +162,12 @@
     own_visit = jnp.where(odd == 0, slots - 1 - jnp.minimum(step + other_count, slots - 1),
                           jnp.minimum(step + other_count, slots - 1))
 
+    own_span = jnp.stack([own_keys, own_values])[:, None]
+    own_start = attend(
+        own_queries, own_span, jnp.zeros((1,), jnp.int32), jnp.ones((1,), jnp.int32)
+    )
+    weight, own_start = lax.optimization_barrier((weight, own_start))
+    weight = lax.all_gather(weight, "y", axis=1, tiled=True)
     other_out, other_max, other_sum = attend(
         partner_queries, arrived, visit, other_count.reshape(1)
     )
@@ -168,7 +175,7 @@
         (other_max[:, ::HD], other_sum[:, ::HD], other_out), "x", swap
     )
     own_out, own_max, own_sum = attend(
-        own_queries, arrived, own_visit, mine_count.reshape(1), own_keys, own_values
+        own_queries, arrived, own_visit, mine_count.reshape(1), own_start
     )
     got_max = jnp.repeat(got_max, HD, axis=1)
     got_sum = jnp.repeat(got_sum, HD, axis=1)

time: 357 us -> 349 us (0.978)
  starting transfers between devices: 45.3 us -> 23.4 us
  waiting for transfers between devices: 208 us -> 227 us
  Pallas kernels: 43.4 us -> 37.2 us
    ppermute x3, starting transfers between devices: 32 us -> 8.14 us  [local(): lax.ppermute((other_max[:, ::HD], other_sum[:, ::HD], other_out), 'x', swap)]
    reduce_scatter x1, waiting for transfers between devices: 93 us -> 112 us  [local(): lax.psum_scatter(partial_value.astype(jnp.bfloat16), 'clip', scatter_dime...]
    ppermute x3, waiting for transfers between devices: 0.01 us -> 12.9 us  [local(): lax.ppermute((other_max[:, ::HD], other_sum[:, ::HD], other_out), 'x', swap)]
    all_gather x1, waiting for transfers between devices: 73.9 us -> 62.9 us  [local(): weight = lax.all_gather(out_weight, ('zl', 'x'), axis=1, tiled=True)]
    pallas_call x2 -> x3, Pallas kernels: 43.4 us -> 37.2 us  [attend(): pl.pallas_call(lambda *refs: attend_kernel(*refs, with_init=with_init, he...]
  transfers between devices with their start and end apart: 8 -> 8, of which waited for: 3 -> 4; matrix products, arithmetic and copies ran while one was open for 8% -> 9% of each run, Pallas kernels for 12% -> 11%
where the time goes in v5:
time: 349 us; the launch traced here: 346 us
  waiting for transfers between devices  227 us (65%)
  Pallas kernels  37.2 us (11%)
  starting transfers between devices  23.4 us (7%)
  local copies, waits for them, and re-layouts  22.6 us (6%)
  between operations  16.1 us (5%)
  matrix products  11.7 us (3%)
  other arithmetic  8.2 us (2%)
    reduce_scatter x1, waiting for transfers between devices, local(): lax.psum_scatter(partial_value.astype(jnp.bfloat16), 'clip', scatter_dime...  112 us
    all_gather x1, waiting for transfers between devices, local(): weight = lax.all_gather(out_weight, ('zl', 'x'), axis=1, tiled=True)  62.9 us
    all_to_all x1, waiting for transfers between devices, local(): lax.all_to_all(sent, FRAME_AXES, split_axis=2, concat_axis=2, tiled=True)  38.5 us
    pallas_call x3, Pallas kernels, attend(): pl.pallas_call(lambda *refs: attend_kernel(*refs, with_init=with_init, he...  37.2 us
    ppermute x3, waiting for transfers between devices, local(): lax.ppermute((other_max[:, ::HD], other_sum[:, ::HD], other_out), 'x', swap)  12.9 us
    all_to_all x1, starting transfers between devices, local(): lax.all_to_all(sent, FRAME_AXES, split_axis=2, concat_axis=2, tiled=True)  11.8 us
    dot_general x1, matrix products, local(): jnp.dot(attended, weight, preferred_element_type=jnp.float32)  11.7 us
    ppermute x3, starting transfers between devices, local(): lax.ppermute((other_max[:, ::HD], other_sum[:, ::HD], other_out), 'x', swap)  8.14 us
  transfers between devices with their start and end apart: 8, of which 4 were waited for; matrix products, arithmetic and copies ran while one was open for 9% of the time, Pallas kernels for 11%

profile of v5, /device:TPU:50, one launch (start us, length us, event | category | flops | bytes accessed | tf_op | source)
XLA Modules:
  0.0 346.2 jit_solution(9588339519839171634)
XLA Ops:
  6.5 0.0 copy-start
  6.5 0.0 all-gather.3.cloned.1.call-start
  6.5 0.7 all-gather.3.cloned.1.call-update
  7.3 0.8 copy.31
  8.1 0.1 reshape.289
  8.2 0.8 select_reduce_fusion.3
  9.1 0.3 select_reduce_fusion
  9.4 0.9 select_reduce_fusion.2
  10.3 0.1 reshape.296
  10.4 0.0 copy-done
  10.4 0.0 copy-start.2
  10.4 2.4 gather_fusion.1
  12.9 0.0 copy-done.2
  12.9 2.4 gather_fusion
  15.3 3.1 pad_maximum_fusion
  18.4 3.2 copy.32
  21.6 0.0 copy-start.5
  21.6 0.0 copy-start.6
  21.6 11.8 %all-to-all-start = ((bf16[2,4,64,8,640]{4,3,1,0,2:T(8,128)(2,1)}), bf16[2,4,64,8,640]{4,3,1,0,2:T(8,128)(2,1)}, u32[]{:S(2)}, u32[]{:S(2)}) async-start(bf16[2,4,64,8,640]{4,3,1,0,2:T(8,128)(2,1)} %copy.32), calls=%async_computation | async-start | bytes 10485760 | tf_op jit(solution)/shard_map/all_to_all | solution.py:147
  33.5 0.0 all-gather.5.cloned.1.call-start
  33.5 0.0 copy-done.5
  33.5 0.0 copy-done.6
  33.5 1.2 maximum_bitcast_fusion.refs_3_.refs_4_
  34.7 9.5 %shard_map.91 = (f32[512,640]{1,0:T(8,128)}, f32[512,640]{1,0:T(8,128)}, f32[512,640]{1,0:T(8,128)}) custom-call(s32[1]{0:T(128)} %constant.76.clone.1.refs_0_, s32[1]{0:T(128)} %constant.77.clone.1.refs_1_, bf16[512,640]{1,0:T(8,128)(2,1)} %bitcast.24, bf16[2,1,512,640]{3,2,1,0:T(8,128)(2,1)} %maximum_bitcast_fusion.refs_3_.refs_4_, ...), custom_call_target="tpu_custom_call" | custom-call | flops 671088640 | bytes 9175040 | tf_op jit(solution)/shard_map/pallas_call | solution.py:79
  44.2 0.0 copy-start.3
  44.2 0.0 copy-start.7
  44.2 62.9 %all-gather.3.cloned.1.call-done = bf16[640,1280]{0,1:T(8,128)(2,1)} async-done(((bf16[640,80]{0,1:T(8,128)(2,1)}), bf16[640,1280]{0,1:T(8,128)(2,1)}) %all-gather.3.cloned.1.call-update) | async-done | bytes 1638416 | tf_op jit(solution)/shard_map/all_gather | solution.py:143
  107.2 0.0 all-gather.5.cloned.1.call-update
  107.2 0.0 reduce-scatter.2.cloned.1.call-start
  107.2 0.0 copy-done.3
  107.2 3.4 collective-permute-start
  110.6 0.0 copy-done.7
  110.6 0.7 fusion.3
  112.7 0.5 broadcast_select_fusion.refs_0_
  113.2 38.5 %all-to-all-done = bf16[2,4,64,8,640]{4,3,1,0,2:T(8,128)(2,1)} async-done(((bf16[2,4,64,8,640]{4,3,1,0,2:T(8,128)(2,1)}), bf16[2,4,64,8,640]{4,3,1,0,2:T(8,128)(2,1)}, u32[]{:S(2)}, u32[]{:S(2)}) %all-to-all-start) | async-done | bytes 5242912 | tf_op jit(solution)/shard_map/all_to_all | solution.py:147
  151.8 5.3 %copy.40 = bf16[2,4,64,8,640]{4,3,2,1,0:T(8,128)(2,1)} copy(bf16[2,4,64,8,640]{4,3,1,0,2:T(8,128)(2,1)} %all-to-all-done) | data formatting | bytes 10485760 | tf_op jit(solution)/shard_map/all_to_all | solution.py:147
  157.1 0.0 collective-permute-done.refs_2_
  157.1 0.0 copy-start.4
  157.1 0.8 copy-done.4
  157.9 10.4 %shard_map.93 = (f32[512,640]{1,0:T(8,128)}, f32[512,640]{1,0:T(8,128)}, f32[512,640]{1,0:T(8,128)}) custom-call(s32[4]{0:T(128)} %broadcast_select_fusion.refs_0_, s32[1]{0:T(128)} %bitcast.7.refs_1_, bf16[512,640]{1,0:T(8,128)(2,1)} %copy-done.4, bf16[2,4,512,640]{3,2,1,0:T(8,128)(2,1)} %bitcast.16, bf16[2,4,512,640]{3,2,1,0:T(8,128)(2,1)} %bitcast.17), custom_call_target="tpu_custom_call" | custom-call | flops 2684354560 | bytes 13107200 | tf_op jit(solution)/shard_map/pallas_call | solution.py:79
  168.3 6.0 %collective-permute-start.2 = (f32[512,640]{1,0:T(8,128)}, f32[512,640]{1,0:T(8,128)}, u32[]{:S(2)}, u32[]{:S(2)}) collective-permute-start(f32[512,640]{1,0:T(8,128)} %get-tuple-element.27), channel_id=1, source_target_pairs={{0,1},{1,0},{2,3},{3,2},{4,5},{5,4},{6,7},{7,6},{8,9},{9,8},{10,11... | collective-permute-start | bytes 3932168 | tf_op jit(solution)/shard_map/ppermute | solution.py:174
  175.7 0.6 broadcast_select_fusion.1.refs_0_
  176.3 2.5 slice.6
  178.8 2.4 slice.7
  181.3 0.1 collective-permute-start.3
  181.4 2.0 collective-permute-start.1
  183.4 17.3 %shard_map.92 = (f32[512,640]{1,0:T(8,128)}, f32[512,640]{1,0:T(8,128)}, f32[512,640]{1,0:T(8,128)}) custom-call(s32[4]{0:T(128)} %broadcast_select_fusion.1.refs_0_, s32[1]{0:T(128)} %bitcast.refs_1_, bf16[512,640]{1,0:T(8,128)(2,1)} %bitcast.25, bf16[2,4,512,640]{3,2,1,0:T(8,128)(2,1)} %bitcast.18, bf16[2,4,512,640]{3,2,1,0:T(8,128)(2,1)} %bitcast.19, ...), custom_call_target="tpu_custom_call" | custom-call | flops 2684354560 | bytes 13107200 | tf_op jit(solution)/shard_map/pallas_call | solution.py:79
  200.7 12.9 %collective-permute-done.1 = f32[512,5]{1,0:T(8,128)S(1)} collective-permute-done((f32[512,5]{1,0:T(8,128)S(1)}, f32[512,5]{1,0:T(8,128)S(1)}, u32[]{:S(2)}, u32[]{:S(2)}) %collective-permute-start.1) | collective-permute-done | bytes 10272 | tf_op jit(solution)/shard_map/ppermute | solution.py:174
  213.6 0.1 copy.34
  213.7 0.2 broadcast_in_dim.66
  213.9 0.4 copy.35
  214.3 0.0 collective-permute-done.3
  214.3 0.1 copy.37
  214.4 0.2 broadcast_in_dim.67
  214.6 1.5 copy.38
  216.1 0.0 collective-permute-done.2
  216.1 0.0 all-gather.5.cloned.1.call-done
  216.1 11.7 %convolution_convert_fusion = bf16[512,5120]{1,0:T(8,128)(2,1)} fusion(bf16[640,5120]{0,1:T(8,128)(2,1)} %all-gather.5.cloned.1.call-done, f32[512,640]{1,0:T(8,128)} %copy.38, f32[512,640]{1,0:T(8,128)} %get-tuple-element.28, f32[512,640]{1,0:T(8,128)} %collective-permute-done.2, f32[512,640]{1,0:T(8,128)S(1)} %copy.35, f32[512,640]{1,0:T(8,128)} %get-tuple-element.25, ...), kind=kOutput, calls=%fused_computation.2 | convolution fusion | flops 3361669120 | bytes 19660800 | tf_op jit(solution)/shard_map/dot_general | solution.py:188
  227.8 0.0 reduce-scatter.2.cloned.1.call-update
  227.8 0.0 copy-start.1
  227.8 111.8 %reduce-scatter.2.cloned.1.call-done = bf16[128,5120]{1,0:T(8,128)(2,1)} async-done(((bf16[512,5120]{1,0:T(8,128)(2,1)}), bf16[128,5120]{1,0:T(8,128)(2,1)}) %reduce-scatter.2.cloned.1.call-update) | async-done | bytes 1310736 | tf_op jit(solution)/shard_map/reduce_scatter | solution.py:189
  339.7 0.0 copy-done.1
  (7 shorter events, 0.1 us)
Async XLA Ops:
  6.5 3.9 %copy-start = (bf16[128,8,640]{2,1,0:T(8,128)(2,1)S(1)}, bf16[128,8,640]{2,1,0:T(8,128)(2,1)}, u32[]{:S(2)}) copy-start(bf16[128,8,640]{2,1,0:T(8,128)(2,1)} %param.13) | copy-start | bytes 3932164
  6.5 100.6 %all-gather.3.cloned.1.call-start = ((), (), s32[]{:S(2)}) async-start(), calls=%async_computation.2 | async-start | bytes 1740800 | tf_op jit(solution)/shard_map/all_gather | solution.py:143
  10.4 2.5 copy-start.2
  21.6 11.9 %copy-start.5 = (bf16[1,512,640]{2,1,0:T(8,128)(2,1)S(1)}, bf16[1,512,640]{2,1,0:T(8,128)(2,1)}, u32[]{:S(2)}) copy-start(bf16[1,512,640]{2,1,0:T(8,128)(2,1)} %param.11) | copy-start | bytes 1966084
  21.6 11.9 %copy-start.6 = (bf16[1,512,640]{2,1,0:T(8,128)(2,1)S(1)}, bf16[1,512,640]{2,1,0:T(8,128)(2,1)}, u32[]{:S(2)}) copy-start(bf16[1,512,640]{2,1,0:T(8,128)(2,1)} %param.10) | copy-start | bytes 1966084
  21.6 130.1 %all-to-all-start = ((bf16[2,4,64,8,640]{4,3,1,0,2:T(8,128)(2,1)}), bf16[2,4,64,8,640]{4,3,1,0,2:T(8,128)(2,1)}, u32[]{:S(2)}, u32[]{:S(2)}) async-start(bf16[2,4,64,8,640]{4,3,1,0,2:T(8,128)(2,1)} %copy.32), calls=%async_computation | async-start | bytes 10485760 | tf_op jit(solution)/shard_map/all_to_all | solution.py:147
  33.5 182.6 %all-gather.5.cloned.1.call-start = ((), (), s32[]{:S(2)}) async-start(), calls=%async_computation.3 | async-start | bytes 8192000 | tf_op jit(solution)/shard_map/all_gather | solution.py:170
  44.2 63.0 %copy-start.3 = (bf16[1,512,640]{2,1,0:T(8,128)(2,1)S(1)}, bf16[1,512,640]{2,1,0:T(8,128)(2,1)}, u32[]{:S(2)}) copy-start(bf16[1,512,640]{2,1,0:T(8,128)(2,1)} %param.9) | copy-start | bytes 1966084
  44.2 66.4 %copy-start.7 = (s32[64]{0:T(128)S(1)}, s32[64]{0:T(128)}, u32[]{:S(2)}) copy-start(s32[64]{0:T(128)} %param.16) | copy-start | bytes 772
  107.2 232.5 %reduce-scatter.2.cloned.1.call-start = ((), (), s32[]{:S(2)}) async-start(), calls=%async_computation.4 | async-start | bytes 6553600 | tf_op jit(solution)/shard_map/reduce_scatter | solution.py:189
  107.2 49.8 %collective-permute-start = (bf16[512,640]{1,0:T(8,128)(2,1)S(1)}, bf16[512,640]{1,0:T(8,128)(2,1)S(1)}, u32[]{:S(2)}, u32[]{:S(2)}) collective-permute-start(bf16[512,640]{1,0:T(8,128)(2,1)S(1)} %bitcast.26), channel_id=1, source_target_pairs={{0,1},{1,0},{2,3},{3,2},{4,5},{5,4},{6,7},{7,6},{8,9},{9,8},{10,11... | collective-permute-start | bytes 1966088 | tf_op jit(solution)/shard_map/ppermute | solution.py:151
  157.1 0.8 copy-start.4
  168.3 47.8 %collective-permute-start.2 = (f32[512,640]{1,0:T(8,128)}, f32[512,640]{1,0:T(8,128)}, u32[]{:S(2)}, u32[]{:S(2)}) collective-permute-start(f32[512,640]{1,0:T(8,128)} %get-tuple-element.27), channel_id=1, source_target_pairs={{0,1},{1,0},{2,3},{3,2},{4,5},{5,4},{6,7},{7,6},{8,9},{9,8},{10,11... | collective-permute-start | bytes 3932168 | tf_op jit(solution)/shard_map/ppermute | solution.py:174
  181.3 33.1 %collective-permute-start.3 = (f32[512,5]{1,0:T(8,128)S(1)}, f32[512,5]{1,0:T(8,128)S(1)}, u32[]{:S(2)}, u32[]{:S(2)}) collective-permute-start(f32[512,5]{1,0:T(8,128)S(1)} %slice.7), channel_id=1, source_target_pairs={{0,1},{1,0},{2,3},{3,2},{4,5},{5,4},{6,7},{7,6},{8,9},{9,8},{10,11... | collective-permute-start | bytes 30728 | tf_op jit(solution)/shard_map/ppermute | solution.py:174
  181.4 32.3 %collective-permute-start.1 = (f32[512,5]{1,0:T(8,128)S(1)}, f32[512,5]{1,0:T(8,128)S(1)}, u32[]{:S(2)}, u32[]{:S(2)}) collective-permute-start(f32[512,5]{1,0:T(8,128)S(1)} %slice.6), channel_id=1, source_target_pairs={{0,1},{1,0},{2,3},{3,2},{4,5},{5,4},{6,7},{7,6},{8,9},{9,8},{10,11... | collective-permute-start | bytes 30728 | tf_op jit(solution)/shard_map/ppermute | solution.py:174
  227.8 111.9 %copy-start.1 = (bf16[128,8,640]{2,1,0:T(8,128)(2,1)S(1)}, bf16[128,8,640]{2,1,0:T(8,128)(2,1)}, u32[]{:S(2)}) copy-start(bf16[128,8,640]{2,1,0:T(8,128)(2,1)} %param.13) | copy-start | bytes 3932164
Sparse Core Ops, SparseCore 0:
  9.1 98.0 all-gather.2
  109.0 88.5 all-gather.4
  227.9 111.6 reduce-scatter.1

commit v6 on v5

--- a/solution.py
+++ b/solution.py
@@ -159,8 +159,6 @@
     )
     step = jnp.arange(slots, dtype=jnp.int32)
     visit = jnp.where(odd == 0, slots - 1 - step, step)
-    own_visit = jnp.where(odd == 0, slots - 1 - jnp.minimum(step + other_count, slots - 1),
-                          jnp.minimum(step + other_count, slots - 1))
 
     own_span = jnp.stack([own_keys, own_values])[:, None]
     own_start = attend(
@@ -168,14 +166,25 @@
     )
     weight, own_start = lax.optimization_barrier((weight, own_start))
     weight = lax.all_gather(weight, "y", axis=1, tiled=True)
-    other_out, other_max, other_sum = attend(
-        partner_queries, arrived, visit, other_count.reshape(1)
-    )
+    meet = jnp.abs(slots - even_count)
+    before = jnp.clip(meet - other_count, 0, mine_count)
+    after = mine_count - before
+
+    def visits_from(first):
+        at = jnp.minimum(step + first, slots - 1)
+        return jnp.where(odd == 0, slots - 1 - at, at)
+
+    other_state = attend(partner_queries, arrived, visit, other_count.reshape(1))
+    own_state = attend(
+        own_queries, arrived, visits_from(other_count), before.reshape(1), own_start
+    )
+    other_state, own_state = lax.optimization_barrier((other_state, own_state))
+    other_out, other_max, other_sum = other_state
     got_max, got_sum, got_out = lax.ppermute(
         (other_max[:, ::HD], other_sum[:, ::HD], other_out), "x", swap
     )
     own_out, own_max, own_sum = attend(
-        own_queries, arrived, own_visit, mine_count.reshape(1), own_start
+        own_queries, arrived, visits_from(other_count + before), after.reshape(1), own_state
     )
     got_max = jnp.repeat(got_max, HD, axis=1)
     got_sum = jnp.repeat(got_sum, HD, axis=1)

time: 349 us -> 354 us (1.014)
  waiting for transfers between devices: 227 us -> 220 us
  starting transfers between devices: 23.4 us -> 29.5 us
  Pallas kernels: 37.2 us -> 43.1 us
    reduce_scatter x1, waiting for transfers between devices: 112 us -> 94.3 us  [local(): lax.psum_scatter(partial_value.astype(jnp.bfloat16), 'clip', scatter_dime...]
    ppermute x3, waiting for transfers between devices: 12.9 us -> 25.5 us  [local(): lax.ppermute((other_max[:, ::HD], other_sum[:, ::HD], other_out), 'x', swap)]
    ppermute x3, starting transfers between devices: 8.14 us -> 14.2 us  [local(): lax.ppermute((other_max[:, ::HD], other_sum[:, ::HD], other_out), 'x', swap)]
    pallas_call x3 -> x4, Pallas kernels: 37.2 us -> 43.1 us  [attend(): pl.pallas_call(lambda *refs: attend_kernel(*refs, with_init=with_init, he...]
  transfers between devices with their start and end apart: 8 -> 8, of which waited for: 4 -> 5; matrix products, arithmetic and copies ran while one was open for 9% -> 8% of each run, Pallas kernels for 11% -> 12%
where the time goes in v6:
time: 354 us; the launch traced here: 351 us
  waiting for transfers between devices  220 us (62%)
  Pallas kernels  43.1 us (12%)
  starting transfers between devices  29.5 us (8%)
  local copies, waits for them, and re-layouts  22.7 us (6%)
  between operations  15.9 us (4%)
  matrix products  11.7 us (3%)
  other arithmetic  8.04 us (2%)
    reduce_scatter x1, waiting for transfers between devices, local(): lax.psum_scatter(partial_value.astype(jnp.bfloat16), 'clip', scatter_dime...  94.3 us
    all_gather x1, waiting for transfers between devices, local(): weight = lax.all_gather(out_weight, ('zl', 'x'), axis=1, tiled=True)  62.7 us
    pallas_call x4, Pallas kernels, attend(): pl.pallas_call(lambda *refs: attend_kernel(*refs, with_init=with_init, he...  43.1 us
    all_to_all x1, waiting for transfers between devices, local(): lax.all_to_all(sent, FRAME_AXES, split_axis=2, concat_axis=2, tiled=True)  37.1 us
    ppermute x3, waiting for transfers between devices, local(): lax.ppermute((other_max[:, ::HD], other_sum[:, ::HD], other_out), 'x', swap)  25.5 us
    ppermute x3, starting transfers between devices, local(): lax.ppermute((other_max[:, ::HD], other_sum[:, ::HD], other_out), 'x', swap)  14.2 us
    all_to_all x1, starting transfers between devices, local(): lax.all_to_all(sent, FRAME_AXES, split_axis=2, concat_axis=2, tiled=True)  11.8 us
    dot_general x1, matrix products, local(): jnp.dot(attended, weight, preferred_element_type=jnp.float32)  11.7 us
  transfers between devices with their start and end apart: 8, of which 5 were waited for; matrix products, arithmetic and copies ran while one was open for 8% of the time, Pallas kernels for 12%

profile of v6, /device:TPU:50, one launch (start us, length us, event | category | flops | bytes accessed | tf_op | source)
XLA Modules:
  0.0 351.2 jit_solution(7528567042525405816)
XLA Ops:
  6.5 0.0 copy-start
  6.5 0.0 all-gather.3.cloned.1.call-start
  6.5 0.7 all-gather.3.cloned.1.call-update
  7.3 0.8 copy.31
  8.1 0.1 reshape.292
  8.2 0.8 select_reduce_fusion.3
  9.1 0.3 select_reduce_fusion
  9.4 0.9 select_reduce_fusion.2
  10.3 0.1 reshape.300
  10.4 0.0 copy-done
  10.4 0.0 copy-start.3
  10.4 2.5 gather_fusion
  12.9 0.0 copy-done.3
  12.9 2.4 gather_fusion.1
  15.3 3.1 pad_maximum_fusion
  18.4 3.2 copy.32
  21.6 0.0 copy-start.5
  21.6 0.0 copy-start.6
  21.6 11.8 %all-to-all-start = ((bf16[2,4,64,8,640]{4,3,1,0,2:T(8,128)(2,1)}), bf16[2,4,64,8,640]{4,3,1,0,2:T(8,128)(2,1)}, u32[]{:S(2)}, u32[]{:S(2)}) async-start(bf16[2,4,64,8,640]{4,3,1,0,2:T(8,128)(2,1)} %copy.32), calls=%async_computation | async-start | bytes 10485760 | tf_op jit(solution)/shard_map/all_to_all | solution.py:147
  33.5 0.0 all-gather.5.cloned.1.call-start
  33.5 0.0 copy-done.5
  33.5 0.0 copy-done.6
  33.5 1.2 maximum_bitcast_fusion.refs_3_.refs_4_
  34.7 9.5 %shard_map.92 = (f32[512,640]{1,0:T(8,128)}, f32[512,640]{1,0:T(8,128)}, f32[512,640]{1,0:T(8,128)}) custom-call(s32[1]{0:T(128)} %constant.76.clone.1.refs_0_, s32[1]{0:T(128)} %constant.77.clone.1.refs_1_, bf16[512,640]{1,0:T(8,128)(2,1)} %bitcast.25, bf16[2,1,512,640]{3,2,1,0:T(8,128)(2,1)} %maximum_bitcast_fusion.refs_3_.refs_4_, ...), custom_call_target="tpu_custom_call" | custom-call | flops 671088640 | bytes 9175040 | tf_op jit(solution)/shard_map/pallas_call | solution.py:79
  44.2 0.0 copy-start.2
  44.2 0.0 copy-start.7
  44.2 62.7 %all-gather.3.cloned.1.call-done = bf16[640,1280]{0,1:T(8,128)(2,1)} async-done(((bf16[640,80]{0,1:T(8,128)(2,1)}), bf16[640,1280]{0,1:T(8,128)(2,1)}) %all-gather.3.cloned.1.call-update) | async-done | bytes 1638416 | tf_op jit(solution)/shard_map/all_gather | solution.py:143
  106.9 0.0 all-gather.5.cloned.1.call-update
  106.9 0.0 reduce-scatter.2.cloned.1.call-start
  107.0 0.0 copy-done.2
  107.0 3.4 collective-permute-start
  110.3 0.0 copy-done.7
  110.3 0.6 fusion.3
  113.6 0.5 broadcast_select_fusion.1.refs_0_
  114.1 0.5 broadcast_select_fusion
  114.6 37.1 %all-to-all-done = bf16[2,4,64,8,640]{4,3,1,0,2:T(8,128)(2,1)} async-done(((bf16[2,4,64,8,640]{4,3,1,0,2:T(8,128)(2,1)}), bf16[2,4,64,8,640]{4,3,1,0,2:T(8,128)(2,1)}, u32[]{:S(2)}, u32[]{:S(2)}) %all-to-all-start) | async-done | bytes 5242912 | tf_op jit(solution)/shard_map/all_to_all | solution.py:147
  151.7 5.3 %copy.40 = bf16[2,4,64,8,640]{4,3,2,1,0:T(8,128)(2,1)} copy(bf16[2,4,64,8,640]{4,3,1,0,2:T(8,128)(2,1)} %all-to-all-done) | data formatting | bytes 10485760 | tf_op jit(solution)/shard_map/all_to_all | solution.py:147
  157.0 23.3 %shard_map.93 = (f32[512,640]{1,0:T(8,128)}, f32[512,640]{1,0:T(8,128)}, f32[512,640]{1,0:T(8,128)}) custom-call(s32[4]{0:T(128)} %get-tuple-element.53.refs_0_, s32[1]{0:T(128)} %bitcast.7.refs_1_, bf16[512,640]{1,0:T(8,128)(2,1)} %bitcast.26, bf16[2,4,512,640]{3,2,1,0:T(8,128)(2,1)} %bitcast.17, bf16[2,4,512,640]{3,2,1,0:T(8,128)(2,1)} %bitcast.18, ...), custom_call_target="tpu_custom_call" | custom-call | flops 2684354560 | bytes 13107200 | tf_op jit(solution)/shard_map/pallas_call | solution.py:79
  180.3 0.0 collective-permute-done.refs_2_
  180.3 0.0 copy-start.4
  180.3 0.8 copy-done.4
  181.1 4.6 %shard_map.91 = (f32[512,640]{1,0:T(8,128)}, f32[512,640]{1,0:T(8,128)}, f32[512,640]{1,0:T(8,128)}) custom-call(s32[4]{0:T(128)} %broadcast_select_fusion.1.refs_0_, s32[1]{0:T(128)} %bitcast.6.refs_1_, bf16[512,640]{1,0:T(8,128)(2,1)} %copy-done.4, bf16[2,4,512,640]{3,2,1,0:T(8,128)(2,1)} %bitcast.19, bf16[2,4,512,640]{3,2,1,0:T(8,128)(2,1)} %bitcast.20), custom_call_target="tpu_custom_call" | custom-call | flops 2684354560 | bytes 13107200 | tf_op jit(solution)/shard_map/pallas_call | solution.py:79
  185.7 11.8 %collective-permute-start.2 = (f32[512,640]{1,0:T(8,128)}, f32[512,640]{1,0:T(8,128)}, u32[]{:S(2)}, u32[]{:S(2)}) collective-permute-start(f32[512,640]{1,0:T(8,128)} %get-tuple-element.45), channel_id=1, source_target_pairs={{0,1},{1,0},{2,3},{3,2},{4,5},{5,4},{6,7},{7,6},{8,9},{9,8},{10,11... | collective-permute-start | bytes 3932168 | tf_op jit(solution)/shard_map/ppermute | solution.py:183
  197.5 2.4 slice.6
  199.9 0.1 collective-permute-start.1
  200.0 2.4 slice.7
  202.5 2.3 collective-permute-start.3
  204.8 5.8 %shard_map.94 = (f32[512,640]{1,0:T(8,128)}, f32[512,640]{1,0:T(8,128)}, f32[512,640]{1,0:T(8,128)}) custom-call(s32[4]{0:T(128)} %get-tuple-element.54.refs_0_, s32[1]{0:T(128)} %bitcast.refs_1_, bf16[512,640]{1,0:T(8,128)(2,1)} %bitcast.27, bf16[2,4,512,640]{3,2,1,0:T(8,128)(2,1)} %bitcast.21, bf16[2,4,512,640]{3,2,1,0:T(8,128)(2,1)} %bitcast.22, ...), custom_call_target="tpu_custom_call" | custom-call | flops 2684354560 | bytes 13107200 | tf_op jit(solution)/shard_map/pallas_call | solution.py:79
  210.6 22.3 %collective-permute-done.1 = f32[512,5]{1,0:T(8,128)S(1)} collective-permute-done((f32[512,5]{1,0:T(8,128)S(1)}, f32[512,5]{1,0:T(8,128)S(1)}, u32[]{:S(2)}, u32[]{:S(2)}) %collective-permute-start.1) | collective-permute-done | bytes 10272 | tf_op jit(solution)/shard_map/ppermute | solution.py:183
  232.9 0.1 copy.34
  233.1 0.2 broadcast_in_dim.66
  233.2 0.4 copy.35
  233.6 3.1 collective-permute-done.3
  236.8 0.1 copy.37
  236.9 0.2 broadcast_in_dim.67
  237.0 1.6 copy.38
  238.6 0.0 collective-permute-done.2
  238.6 0.0 all-gather.5.cloned.1.call-done
  238.6 11.7 %convolution_convert_fusion = bf16[512,5120]{1,0:T(8,128)(2,1)} fusion(bf16[640,5120]{0,1:T(8,128)(2,1)} %all-gather.5.cloned.1.call-done, f32[512,640]{1,0:T(8,128)} %copy.38, f32[512,640]{1,0:T(8,128)} %get-tuple-element.46, f32[512,640]{1,0:T(8,128)} %collective-permute-done.2, f32[512,640]{1,0:T(8,128)S(1)} %copy.35, f32[512,640]{1,0:T(8,128)} %get-tuple-element.43, ...), kind=kOutput, calls=%fused_computation.2 | convolution fusion | flops 3361669120 | bytes 19660800 | tf_op jit(solution)/shard_map/dot_general | solution.py:197
  250.3 0.0 reduce-scatter.2.cloned.1.call-update
  250.3 0.0 copy-start.1
  250.4 94.3 %reduce-scatter.2.cloned.1.call-done = bf16[128,5120]{1,0:T(8,128)(2,1)} async-done(((bf16[512,5120]{1,0:T(8,128)(2,1)}), bf16[128,5120]{1,0:T(8,128)(2,1)}) %reduce-scatter.2.cloned.1.call-update) | async-done | bytes 1310736 | tf_op jit(solution)/shard_map/reduce_scatter | solution.py:198
  344.6 0.0 copy-done.1
  (7 shorter events, 0.1 us)
Async XLA Ops:
  6.5 3.9 %copy-start = (bf16[128,8,640]{2,1,0:T(8,128)(2,1)S(1)}, bf16[128,8,640]{2,1,0:T(8,128)(2,1)}, u32[]{:S(2)}) copy-start(bf16[128,8,640]{2,1,0:T(8,128)(2,1)} %param.12) | copy-start | bytes 3932164
  6.5 100.3 %all-gather.3.cloned.1.call-start = ((), (), s32[]{:S(2)}) async-start(), calls=%async_computation.2 | async-start | bytes 1740800 | tf_op jit(solution)/shard_map/all_gather | solution.py:143
  10.4 2.5 copy-start.3
  21.6 11.9 %copy-start.5 = (bf16[1,512,640]{2,1,0:T(8,128)(2,1)S(1)}, bf16[1,512,640]{2,1,0:T(8,128)(2,1)}, u32[]{:S(2)}) copy-start(bf16[1,512,640]{2,1,0:T(8,128)(2,1)} %param.11) | copy-start | bytes 1966084
  21.6 11.9 %copy-start.6 = (bf16[1,512,640]{2,1,0:T(8,128)(2,1)S(1)}, bf16[1,512,640]{2,1,0:T(8,128)(2,1)}, u32[]{:S(2)}) copy-start(bf16[1,512,640]{2,1,0:T(8,128)(2,1)} %param.10) | copy-start | bytes 1966084
  21.6 130.1 %all-to-all-start = ((bf16[2,4,64,8,640]{4,3,1,0,2:T(8,128)(2,1)}), bf16[2,4,64,8,640]{4,3,1,0,2:T(8,128)(2,1)}, u32[]{:S(2)}, u32[]{:S(2)}) async-start(bf16[2,4,64,8,640]{4,3,1,0,2:T(8,128)(2,1)} %copy.32), calls=%async_computation | async-start | bytes 10485760 | tf_op jit(solution)/shard_map/all_to_all | solution.py:147
  33.5 205.2 %all-gather.5.cloned.1.call-start = ((), (), s32[]{:S(2)}) async-start(), calls=%async_computation.3 | async-start | bytes 8192000 | tf_op jit(solution)/shard_map/all_gather | solution.py:168
  44.2 62.7 %copy-start.2 = (bf16[1,512,640]{2,1,0:T(8,128)(2,1)S(1)}, bf16[1,512,640]{2,1,0:T(8,128)(2,1)}, u32[]{:S(2)}) copy-start(bf16[1,512,640]{2,1,0:T(8,128)(2,1)} %param.9) | copy-start | bytes 1966084
  44.2 66.1 %copy-start.7 = (s32[64]{0:T(128)S(1)}, s32[64]{0:T(128)}, u32[]{:S(2)}) copy-start(s32[64]{0:T(128)} %param.16) | copy-start | bytes 772
  106.9 237.7 %reduce-scatter.2.cloned.1.call-start = ((), (), s32[]{:S(2)}) async-start(), calls=%async_computation.4 | async-start | bytes 6553600 | tf_op jit(solution)/shard_map/reduce_scatter | solution.py:198
  107.0 73.3 %collective-permute-start = (bf16[512,640]{1,0:T(8,128)(2,1)S(1)}, bf16[512,640]{1,0:T(8,128)(2,1)S(1)}, u32[]{:S(2)}, u32[]{:S(2)}) collective-permute-start(bf16[512,640]{1,0:T(8,128)(2,1)S(1)} %bitcast.28), channel_id=1, source_target_pairs={{0,1},{1,0},{2,3},{3,2},{4,5},{5,4},{6,7},{7,6},{8,9},{9,8},{10,11... | collective-permute-start | bytes 1966088 | tf_op jit(solution)/shard_map/ppermute | solution.py:151
  180.3 0.9 copy-start.4
  185.7 52.9 %collective-permute-start.2 = (f32[512,640]{1,0:T(8,128)}, f32[512,640]{1,0:T(8,128)}, u32[]{:S(2)}, u32[]{:S(2)}) collective-permute-start(f32[512,640]{1,0:T(8,128)} %get-tuple-element.45), channel_id=1, source_target_pairs={{0,1},{1,0},{2,3},{3,2},{4,5},{5,4},{6,7},{7,6},{8,9},{9,8},{10,11... | collective-permute-start | bytes 3932168 | tf_op jit(solution)/shard_map/ppermute | solution.py:183
  199.9 33.0 %collective-permute-start.1 = (f32[512,5]{1,0:T(8,128)S(1)}, f32[512,5]{1,0:T(8,128)S(1)}, u32[]{:S(2)}, u32[]{:S(2)}) collective-permute-start(f32[512,5]{1,0:T(8,128)S(1)} %slice.6), channel_id=1, source_target_pairs={{0,1},{1,0},{2,3},{3,2},{4,5},{5,4},{6,7},{7,6},{8,9},{9,8},{10,11... | collective-permute-start | bytes 30728 | tf_op jit(solution)/shard_map/ppermute | solution.py:183
  202.5 34.3 %collective-permute-start.3 = (f32[512,5]{1,0:T(8,128)S(1)}, f32[512,5]{1,0:T(8,128)S(1)}, u32[]{:S(2)}, u32[]{:S(2)}) collective-permute-start(f32[512,5]{1,0:T(8,128)S(1)} %slice.7), channel_id=1, source_target_pairs={{0,1},{1,0},{2,3},{3,2},{4,5},{5,4},{6,7},{7,6},{8,9},{9,8},{10,11... | collective-permute-start | bytes 30728 | tf_op jit(solution)/shard_map/ppermute | solution.py:183
  250.3 94.3 %copy-start.1 = (bf16[128,8,640]{2,1,0:T(8,128)(2,1)S(1)}, bf16[128,8,640]{2,1,0:T(8,128)(2,1)}, u32[]{:S(2)}) copy-start(bf16[128,8,640]{2,1,0:T(8,128)(2,1)} %param.12) | copy-start | bytes 3932164
Sparse Core Ops, SparseCore 0:
  9.1 97.7 all-gather.2
  108.7 88.8 all-gather.4
  250.5 94.1 reduce-scatter.1

commit v7 on v6

--- a/solution.py
+++ b/solution.py
@@ -14,6 +14,7 @@
 NC = 16
 
 FRAME_AXES = ("y", "zl", "x")
+CLIP_AXES = ("zh", "core")
 
 neg_fill = -1e30
 
@@ -194,29 +195,48 @@
     total_sum = own_sum * own_scale + got_sum * got_scale
     total_out = own_out * own_scale + got_out * got_scale
     attended = (total_out / total_sum).astype(jnp.bfloat16)
+    quarters = lax.axis_size("zh") * lax.axis_size("core")
+    quarter_rows = tokens_here // quarters
+    attended = attended.reshape(lax.axis_size("zh"), lax.axis_size("core"), quarter_rows, row_width)
+    attended = attended.transpose(1, 0, 2, 3).reshape(tokens_here, row_width)
     partial_value = jnp.dot(attended, weight, preferred_element_type=jnp.float32)
-    own_rows = lax.psum_scatter(
-        partial_value.astype(jnp.bfloat16), "clip", scatter_dimension=0, tiled=True
-    )
+    on_chip = lax.psum_scatter(
+        partial_value.astype(jnp.bfloat16), "core", scatter_dimension=0, tiled=True
+    )
+    on_chip = on_chip.reshape(lax.axis_size("zh"), quarter_rows, -1)
+    chip_half = lax.axis_index("zh")
+    mine = lax.dynamic_index_in_dim(on_chip, chip_half, 0, keepdims=False)
+    theirs = lax.dynamic_index_in_dim(on_chip, 1 - chip_half, 0, keepdims=False)
+    ring = lax.axis_size("zh") * lax.axis_size("zl")
+    z_axes = ("zh", "zl")
+
+    def shifted(rows, by):
+        return lax.ppermute(rows, z_axes, [(i, (i + by) % ring) for i in range(ring)])
+
+    half = quarter_rows // 2
+    up = shifted(shifted(theirs[:half], 1), ring // 2 - 1)
+    down = shifted(shifted(theirs[half:], -1), 1 - ring // 2)
+    received = jnp.concatenate([up, down], axis=0)
+    own_rows = (mine.astype(jnp.float32) + received.astype(jnp.float32)).astype(jnp.bfloat16)
     return own_rows[None]
 
 
 def solution(mesh):
     frames = mesh.shape["fsdp"]
     fine = Mesh(
-        np.asarray(mesh.devices).reshape(mesh.shape["clip"], frames // 16, 4, 4),
-        ("clip",) + FRAME_AXES,
+        np.asarray(mesh.devices).reshape(2, mesh.shape["clip"] // 2, frames // 16, 4, 4),
+        CLIP_AXES + FRAME_AXES,
     )
     in_specs = (
-        P(FRAME_AXES, None, "clip"),
-        P(FRAME_AXES, None, "clip"),
-        P(FRAME_AXES, None, "clip"),
-        P(None, FRAME_AXES, "clip"),
-        P(None, FRAME_AXES, "clip"),
+        P(FRAME_AXES, None, CLIP_AXES),
+        P(FRAME_AXES, None, CLIP_AXES),
+        P(FRAME_AXES, None, CLIP_AXES),
+        P(None, FRAME_AXES, CLIP_AXES),
+        P(None, FRAME_AXES, CLIP_AXES),
         P(),
         P(),
         P(),
-        P("clip", FRAME_AXES),
-    )
-    out_specs = P(FRAME_AXES, "clip", None)
+        P(CLIP_AXES, FRAME_AXES),
+    )
+    out_specs = P(FRAME_AXES, CLIP_AXES, None)
     return jax.shard_map(local, mesh=fine, in_specs=in_specs, out_specs=out_specs, check_vma=False)

time: 354 us -> 353 us (level)
  waiting for transfers between devices: 220 us -> 208 us
  other arithmetic: 8.04 us -> 15.8 us
  starting transfers between devices: 29.5 us -> 36.6 us
    reduce_scatter x1, waiting for transfers between devices: 94.3 us -> 29.2 us  [local(): lax.psum_scatter(partial_value.astype(jnp.bfloat16), 'core', scatter_dime...]
    ppermute x0 -> x4, waiting for transfers between devices: none -> 61.7 us  [shifted(): lax.ppermute(rows, z_axes, [(i, (i + by) % ring) for i in range(ring)])]
    ppermute x3, waiting for transfers between devices: 25.5 us -> 14.4 us  [local(): lax.ppermute((other_max[:, ::HD], other_sum[:, ::HD], other_out), 'x', swap)]
    ppermute x0 -> x4, starting transfers between devices: none -> 8.06 us  [shifted(): lax.ppermute(rows, z_axes, [(i, (i + by) % ring) for i in range(ring)])]
    convert_element_type x0 -> x2, other arithmetic: none -> 6.35 us  [the longest x1 3.57 us: local(): attended = (total_out / total_sum).astype(jnp.bfloat16)]
    all_to_all x1, waiting for transfers between devices: 37.1 us -> 43 us  [local(): lax.all_to_all(sent, FRAME_AXES, split_axis=2, concat_axis=2, tiled=True)]
    all_gather x1, waiting for transfers between devices: 62.7 us -> 59.1 us  [local(): weight = lax.all_gather(out_weight, ('zl', 'x'), axis=1, tiled=True)]
  transfers between devices with their start and end apart: 8 -> 12, of which waited for: 5 -> 8; matrix products, arithmetic and copies ran while one was open for 8% -> 10% of each run, Pallas kernels for 12% -> 12%
where the time goes in v7:
time: 353 us
  waiting for transfers between devices  208 us (59%)
  Pallas kernels  43.1 us (12%)
  starting transfers between devices  36.6 us (10%)
  local copies, waits for them, and re-layouts  24.1 us (7%)
  between operations  16.1 us (5%)
  other arithmetic  15.8 us (4%)
  matrix products  8.83 us (3%)
    ppermute x4, waiting for transfers between devices, shifted(): lax.ppermute(rows, z_axes, [(i, (i + by) % ring) for i in range(ring)])  61.7 us
    all_gather x1, waiting for transfers between devices, local(): weight = lax.all_gather(out_weight, ('zl', 'x'), axis=1, tiled=True)  59.1 us
    pallas_call x4, Pallas kernels, attend(): pl.pallas_call(lambda *refs: attend_kernel(*refs, with_init=with_init, he...  43.1 us
    all_to_all x1, waiting for transfers between devices, local(): lax.all_to_all(sent, FRAME_AXES, split_axis=2, concat_axis=2, tiled=True)  43 us
    reduce_scatter x1, waiting for transfers between devices, local(): lax.psum_scatter(partial_value.astype(jnp.bfloat16), 'core', scatter_dime...  29.2 us
    ppermute x3, starting transfers between devices, local(): lax.ppermute((other_max[:, ::HD], other_sum[:, ::HD], other_out), 'x', swap)  15.7 us
    ppermute x3, waiting for transfers between devices, local(): lax.ppermute((other_max[:, ::HD], other_sum[:, ::HD], other_out), 'x', swap)  14.4 us
    all_to_all x1, starting transfers between devices, local(): lax.all_to_all(sent, FRAME_AXES, split_axis=2, concat_axis=2, tiled=True)  11.8 us
  transfers between devices with their start and end apart: 12, of which 8 were waited for; matrix products, arithmetic and copies ran while one was open for 10% of the time, Pallas kernels for 12%

profile of v7, /device:TPU:50, one launch (start us, length us, event | category | flops | bytes accessed | tf_op | source)
XLA Modules:
  0.0 352.7 jit_solution(17609156627497005719)
XLA Ops:
  6.5 0.0 copy-start
  6.5 0.0 all-gather.3.cloned.1.call-start
  6.5 0.7 all-gather.3.cloned.1.call-update
  7.3 1.4 iota_subtract_fusion
  8.7 0.8 select_reduce_fusion.3
  9.5 0.8 copy.34
  10.3 0.1 reshape.332
  10.5 0.3 select_reduce_fusion
  10.8 0.9 select_reduce_fusion.2
  11.7 0.1 reshape.343
  11.8 0.0 copy-start.3
  11.8 2.5 gather_fusion
  14.3 0.0 copy-done.3
  14.3 2.4 gather_fusion.1
  16.7 3.1 pad_maximum_fusion
  19.8 3.2 copy.35
  23.0 11.8 %all-to-all-start = ((bf16[2,4,64,8,640]{4,3,1,0,2:T(8,128)(2,1)}), bf16[2,4,64,8,640]{4,3,1,0,2:T(8,128)(2,1)}, u32[]{:S(2)}, u32[]{:S(2)}) async-start(bf16[2,4,64,8,640]{4,3,1,0,2:T(8,128)(2,1)} %copy.35), calls=%async_computation | async-start | bytes 10485760 | tf_op jit(solution)/shard_map/all_to_all | solution.py:148
  34.8 0.0 all-gather.5.cloned.1.call-start
  34.9 1.2 maximum_bitcast_fusion.refs_3_.refs_4_
  36.1 9.5 %shard_map.92 = (f32[512,640]{1,0:T(8,128)}, f32[512,640]{1,0:T(8,128)}, f32[512,640]{1,0:T(8,128)}) custom-call(s32[1]{0:T(128)} %constant.88.clone.1.refs_0_, s32[1]{0:T(128)} %constant.89.clone.1.refs_1_, bf16[512,640]{1,0:T(8,128)(2,1)} %bitcast.36, bf16[2,1,512,640]{3,2,1,0:T(8,128)(2,1)} %maximum_bitcast_fusion.refs_3_.refs_4_, ...), custom_call_target="tpu_custom_call" | custom-call | flops 671088640 | bytes 9175040 | tf_op jit(solution)/shard_map/pallas_call | solution.py:80
  45.6 59.1 %all-gather.3.cloned.1.call-done = bf16[640,1280]{0,1:T(8,128)(2,1)} async-done(((bf16[640,80]{0,1:T(8,128)(2,1)}), bf16[640,1280]{0,1:T(8,128)(2,1)}) %all-gather.3.cloned.1.call-update) | async-done | bytes 1638416 | tf_op jit(solution)/shard_map/all_gather | solution.py:144
  104.7 0.0 all-gather.5.cloned.1.call-update
  104.7 0.0 reduce-scatter.2.cloned.1.call-start
  104.8 0.9 collective-permute-start
  108.5 0.5 broadcast_select_fusion.refs_0_
  109.0 0.6 broadcast_select_fusion.1.refs_0_
  109.6 43.0 %all-to-all-done = bf16[2,4,64,8,640]{4,3,1,0,2:T(8,128)(2,1)} async-done(((bf16[2,4,64,8,640]{4,3,1,0,2:T(8,128)(2,1)}), bf16[2,4,64,8,640]{4,3,1,0,2:T(8,128)(2,1)}, u32[]{:S(2)}, u32[]{:S(2)}) %all-to-all-start) | async-done | bytes 5242912 | tf_op jit(solution)/shard_map/all_to_all | solution.py:148
  152.6 5.3 %copy.44 = bf16[2,4,64,8,640]{4,3,2,1,0:T(8,128)(2,1)} copy(bf16[2,4,64,8,640]{4,3,1,0,2:T(8,128)(2,1)} %all-to-all-done) | data formatting | bytes 10485760 | tf_op jit(solution)/shard_map/all_to_all | solution.py:148
  158.0 11.6 %shard_map.93 = (f32[512,640]{1,0:T(8,128)}, f32[512,640]{1,0:T(8,128)}, f32[512,640]{1,0:T(8,128)}) custom-call(s32[4]{0:T(128)} %broadcast_select_fusion.refs_0_, s32[1]{0:T(128)} %bitcast.7.refs_1_, bf16[512,640]{1,0:T(8,128)(2,1)} %bitcast.37, bf16[2,4,512,640]{3,2,1,0:T(8,128)(2,1)} %bitcast.28, bf16[2,4,512,640]{3,2,1,0:T(8,128)(2,1)} %bitcast.29, ...), custom_call_target="tpu_custom_call" | custom-call | flops 2684354560 | bytes 13107200 | tf_op jit(solution)/shard_map/pallas_call | solution.py:80
  169.6 0.0 collective-permute-done.refs_2_
  169.6 0.9 copy-done.4
  170.5 4.6 %shard_map.91 = (f32[512,640]{1,0:T(8,128)}, f32[512,640]{1,0:T(8,128)}, f32[512,640]{1,0:T(8,128)}) custom-call(s32[4]{0:T(128)} %broadcast_select_fusion.1.refs_0_, s32[1]{0:T(128)} %bitcast.6.refs_1_, bf16[512,640]{1,0:T(8,128)(2,1)} %copy-done.4, bf16[2,4,512,640]{3,2,1,0:T(8,128)(2,1)} %bitcast.30, bf16[2,4,512,640]{3,2,1,0:T(8,128)(2,1)} %bitcast.31), custom_call_target="tpu_custom_call" | custom-call | flops 2684354560 | bytes 13107200 | tf_op jit(solution)/shard_map/pallas_call | solution.py:80
  175.1 13.3 %collective-permute-start.2 = (f32[512,640]{1,0:T(8,128)}, f32[512,640]{1,0:T(8,128)}, u32[]{:S(2)}, u32[]{:S(2)}) collective-permute-start(f32[512,640]{1,0:T(8,128)} %get-tuple-element.45), channel_id=1, source_target_pairs={{0,1},{1,0},{2,3},{3,2},{4,5},{5,4},{6,7},{7,6},{8,9},{9,8},{10,11... | collective-permute-start | bytes 3932168 | tf_op jit(solution)/shard_map/ppermute | solution.py:184
  188.4 0.6 broadcast_select_fusion.2.refs_0_
  189.0 2.4 slice.18
  191.4 0.1 collective-permute-start.1
  191.5 2.4 slice.19
  194.0 2.3 collective-permute-start.3
  196.3 17.4 %shard_map.94 = (f32[512,640]{1,0:T(8,128)}, f32[512,640]{1,0:T(8,128)}, f32[512,640]{1,0:T(8,128)}) custom-call(s32[4]{0:T(128)} %broadcast_select_fusion.2.refs_0_, s32[1]{0:T(128)} %bitcast.refs_1_, bf16[512,640]{1,0:T(8,128)(2,1)} %bitcast.38, bf16[2,4,512,640]{3,2,1,0:T(8,128)(2,1)} %bitcast.32, bf16[2,4,512,640]{3,2,1,0:T(8,128)(2,1)} %bitcast.33, ...), custom_call_target="tpu_custom_call" | custom-call | flops 2684354560 | bytes 13107200 | tf_op jit(solution)/shard_map/pallas_call | solution.py:80
  213.7 10.1 %collective-permute-done.1 = f32[512,5]{1,0:T(8,128)S(1)} collective-permute-done((f32[512,5]{1,0:T(8,128)S(1)}, f32[512,5]{1,0:T(8,128)S(1)}, u32[]{:S(2)}, u32[]{:S(2)}) %collective-permute-start.1) | collective-permute-done | bytes 10272 | tf_op jit(solution)/shard_map/ppermute | solution.py:184
  223.8 0.1 copy.37
  223.9 0.2 broadcast_in_dim.64
  224.1 0.4 copy.38
  224.5 4.2 %collective-permute-done.3 = f32[512,5]{1,0:T(8,128)S(1)} collective-permute-done((f32[512,5]{1,0:T(8,128)S(1)}, f32[512,5]{1,0:T(8,128)S(1)}, u32[]{:S(2)}, u32[]{:S(2)}) %collective-permute-start.3) | collective-permute-done | bytes 10272 | tf_op jit(solution)/shard_map/ppermute | solution.py:184
  228.8 0.1 copy.40
  228.9 0.2 broadcast_in_dim.65
  229.0 1.5 copy.41
  230.5 0.0 collective-permute-done.2
  230.5 3.6 %divide_convert_fusion = bf16[512,640]{1,0:T(8,128)(2,1)S(1)} fusion(f32[512,640]{1,0:T(8,128)} %copy.41, f32[512,640]{1,0:T(8,128)} %get-tuple-element.46, f32[512,640]{1,0:T(8,128)} %collective-permute-done.2, f32[512,640]{1,0:T(8,128)S(1)} %copy.38, f32[512,640]{1,0:T(8,128)} %get-tuple-element.43, f32[512,640]{1,0:T(8,128)} %get-tuple-element.42), kind=kLoop, calls=%fused_computation.11 | loop fusion | flops 3604480 | bytes 8519680 | tf_op jit(solution)/shard_map/convert_element_type | solution.py:197
  234.1 0.1 copy.42
  234.2 0.0 all-gather.5.cloned.1.call-done
  234.2 8.8 %convolution_convert_fusion = bf16[512,5120]{1,0:T(8,128)(2,1)} fusion(bf16[512,640]{1,0:T(8,128)(2,1)S(1)} %bitcast.45, bf16[640,5120]{0,1:T(8,128)(2,1)} %all-gather.5.cloned.1.call-done), kind=kOutput, calls=%fused_computation.2 | convolution fusion | flops 3358064640 | bytes 12451840 | tf_op jit(solution)/shard_map/dot_general | solution.py:202
  243.0 0.0 reduce-scatter.2.cloned.1.call-update
  243.0 29.2 %reduce-scatter.2.cloned.1.call-done = bf16[256,5120]{1,0:T(8,128)(2,1)} async-done(((bf16[512,5120]{1,0:T(8,128)(2,1)}), bf16[256,5120]{1,0:T(8,128)(2,1)}) %reduce-scatter.2.cloned.1.call-update) | async-done | bytes 2621456 | tf_op jit(solution)/shard_map/reduce_scatter | solution.py:203
  272.2 1.4 dynamic-slice_bitcast_fusion.1
  273.6 1.6 collective-permute-start.4
  275.2 0.5 collective-permute-start.6
  275.7 14.8 %collective-permute-done.4 = bf16[64,5120]{1,0:T(8,128)(2,1)S(1)} collective-permute-done((bf16[64,5120]{1,0:T(8,128)(2,1)S(1)}, bf16[64,5120]{1,0:T(8,128)(2,1)S(1)}, u32[]{:S(2)}, u32[]{:S(2)}) %collective-permute-start.4) | collective-permute-done | bytes 655392 | tf_op jit(solution)/shard_map/ppermute | solution.py:214
  290.5 6.0 %collective-permute-start.5 = (bf16[64,5120]{1,0:T(8,128)(2,1)S(1)}, bf16[64,5120]{1,0:T(8,128)(2,1)S(1)}, u32[]{:S(2)}, u32[]{:S(2)}) collective-permute-start(bf16[64,5120]{1,0:T(8,128)(2,1)S(1)} %collective-permute-done.4), channel_id=1, source_target_pairs={{0,12},{4,128},{8,132},{12,136},{128,140},{132,0},{136,4},{140,8},... | collective-permute-start | bytes 1966088 | tf_op jit(solution)/shard_map/ppermute | solution.py:214
  296.4 0.0 collective-permute-done.6
  296.4 0.0 collective-permute-start.7
  296.4 40.8 %collective-permute-done.5 = bf16[64,5120]{1,0:T(8,128)(2,1)S(1)} collective-permute-done((bf16[64,5120]{1,0:T(8,128)(2,1)S(1)}, bf16[64,5120]{1,0:T(8,128)(2,1)S(1)}, u32[]{:S(2)}, u32[]{:S(2)}) %collective-permute-start.5) | collective-permute-done | bytes 655392 | tf_op jit(solution)/shard_map/ppermute | solution.py:214
  337.2 6.2 %collective-permute-done.7 = bf16[64,5120]{1,0:T(8,128)(2,1)S(1)} collective-permute-done((bf16[64,5120]{1,0:T(8,128)(2,1)}, bf16[64,5120]{1,0:T(8,128)(2,1)S(1)}, u32[]{:S(2)}, u32[]{:S(2)}) %collective-permute-start.7) | collective-permute-done | bytes 655392 | tf_op jit(solution)/shard_map/ppermute | solution.py:214
  343.4 2.8 add_convert_fusion
  (16 shorter events, 0.1 us)
Async XLA Ops:
  6.5 5.3 %copy-start = (bf16[128,8,640]{2,1,0:T(8,128)(2,1)S(1)}, bf16[128,8,640]{2,1,0:T(8,128)(2,1)}, u32[]{:S(2)}) copy-start(bf16[128,8,640]{2,1,0:T(8,128)(2,1)} %param.12) | copy-start | bytes 3932164
  6.5 98.2 %all-gather.3.cloned.1.call-start = ((), (), s32[]{:S(2)}) async-start(), calls=%async_computation.2 | async-start | bytes 1740800 | tf_op jit(solution)/shard_map/all_gather | solution.py:144
  11.8 2.5 copy-start.3
  23.0 11.9 %copy-start.5 = (bf16[1,512,640]{2,1,0:T(8,128)(2,1)S(1)}, bf16[1,512,640]{2,1,0:T(8,128)(2,1)}, u32[]{:S(2)}) copy-start(bf16[1,512,640]{2,1,0:T(8,128)(2,1)} %param.11) | copy-start | bytes 1966084
  23.0 11.9 %copy-start.6 = (bf16[1,512,640]{2,1,0:T(8,128)(2,1)S(1)}, bf16[1,512,640]{2,1,0:T(8,128)(2,1)}, u32[]{:S(2)}) copy-start(bf16[1,512,640]{2,1,0:T(8,128)(2,1)} %param.10) | copy-start | bytes 1966084
  23.0 129.6 %all-to-all-start = ((bf16[2,4,64,8,640]{4,3,1,0,2:T(8,128)(2,1)}), bf16[2,4,64,8,640]{4,3,1,0,2:T(8,128)(2,1)}, u32[]{:S(2)}, u32[]{:S(2)}) async-start(bf16[2,4,64,8,640]{4,3,1,0,2:T(8,128)(2,1)} %copy.35), calls=%async_computation | async-start | bytes 10485760 | tf_op jit(solution)/shard_map/all_to_all | solution.py:148
  34.8 199.3 %all-gather.5.cloned.1.call-start = ((), (), s32[]{:S(2)}) async-start(), calls=%async_computation.3 | async-start | bytes 8192000 | tf_op jit(solution)/shard_map/all_gather | solution.py:169
  45.6 59.2 %copy-start.2 = (bf16[1,512,640]{2,1,0:T(8,128)(2,1)S(1)}, bf16[1,512,640]{2,1,0:T(8,128)(2,1)}, u32[]{:S(2)}) copy-start(bf16[1,512,640]{2,1,0:T(8,128)(2,1)} %param.9) | copy-start | bytes 1966084
  104.7 167.5 %reduce-scatter.2.cloned.1.call-start = ((), (), s32[]{:S(2)}) async-start(), calls=%async_computation.4 | async-start | bytes 7864320 | tf_op jit(solution)/shard_map/reduce_scatter | solution.py:203
  104.8 64.8 %collective-permute-start = (bf16[512,640]{1,0:T(8,128)(2,1)S(1)}, bf16[512,640]{1,0:T(8,128)(2,1)S(1)}, u32[]{:S(2)}, u32[]{:S(2)}) collective-permute-start(bf16[512,640]{1,0:T(8,128)(2,1)S(1)} %bitcast.39), channel_id=1, source_target_pairs={{0,1},{1,0},{2,3},{3,2},{4,5},{5,4},{6,7},{7,6},{8,9},{9,8},{10,11... | collective-permute-start | bytes 1966088 | tf_op jit(solution)/shard_map/ppermute | solution.py:152
  169.6 0.9 copy-start.4
  175.1 55.5 %collective-permute-start.2 = (f32[512,640]{1,0:T(8,128)}, f32[512,640]{1,0:T(8,128)}, u32[]{:S(2)}, u32[]{:S(2)}) collective-permute-start(f32[512,640]{1,0:T(8,128)} %get-tuple-element.45), channel_id=1, source_target_pairs={{0,1},{1,0},{2,3},{3,2},{4,5},{5,4},{6,7},{7,6},{8,9},{9,8},{10,11... | collective-permute-start | bytes 3932168 | tf_op jit(solution)/shard_map/ppermute | solution.py:184
  191.4 32.4 %collective-permute-start.1 = (f32[512,5]{1,0:T(8,128)S(1)}, f32[512,5]{1,0:T(8,128)S(1)}, u32[]{:S(2)}, u32[]{:S(2)}) collective-permute-start(f32[512,5]{1,0:T(8,128)S(1)} %slice.18), channel_id=1, source_target_pairs={{0,1},{1,0},{2,3},{3,2},{4,5},{5,4},{6,7},{7,6},{8,9},{9,8},{10,11... | collective-permute-start | bytes 30728 | tf_op jit(solution)/shard_map/ppermute | solution.py:184
  194.0 34.8 %collective-permute-start.3 = (f32[512,5]{1,0:T(8,128)S(1)}, f32[512,5]{1,0:T(8,128)S(1)}, u32[]{:S(2)}, u32[]{:S(2)}) collective-permute-start(f32[512,5]{1,0:T(8,128)S(1)} %slice.19), channel_id=1, source_target_pairs={{0,1},{1,0},{2,3},{3,2},{4,5},{5,4},{6,7},{7,6},{8,9},{9,8},{10,11... | collective-permute-start | bytes 30728 | tf_op jit(solution)/shard_map/ppermute | solution.py:184
  273.6 16.9 %collective-permute-start.4 = (bf16[64,5120]{1,0:T(8,128)(2,1)S(1)}, bf16[64,5120]{1,0:T(8,128)(2,1)S(1)}, u32[]{:S(2)}, u32[]{:S(2)}) collective-permute-start(bf16[64,5120]{1,0:T(8,128)(2,1)S(1)} %get-tuple-element.51), channel_id=1, source_target_pairs={{0,4},{4,8},{8,12},{12,128},{128,132},{132,136},{136,140},{140,0},... | collective-permute-start | bytes 1966088 | tf_op jit(solution)/shard_map/ppermute | solution.py:214
  275.2 21.2 %collective-permute-start.6 = (bf16[64,5120]{1,0:T(8,128)(2,1)S(1)}, bf16[64,5120]{1,0:T(8,128)(2,1)}, u32[]{:S(2)}, u32[]{:S(2)}) collective-permute-start(bf16[64,5120]{1,0:T(8,128)(2,1)S(1)} %get-tuple-element.52), channel_id=1, source_target_pairs={{0,140},{4,0},{8,4},{12,8},{128,12},{132,128},{136,132},{140,136},... | collective-permute-start | bytes 1966088 | tf_op jit(solution)/shard_map/ppermute | solution.py:214
  290.5 46.7 %collective-permute-start.5 = (bf16[64,5120]{1,0:T(8,128)(2,1)S(1)}, bf16[64,5120]{1,0:T(8,128)(2,1)S(1)}, u32[]{:S(2)}, u32[]{:S(2)}) collective-permute-start(bf16[64,5120]{1,0:T(8,128)(2,1)S(1)} %collective-permute-done.4), channel_id=1, source_target_pairs={{0,12},{4,128},{8,132},{12,136},{128,140},{132,0},{136,4},{140,8},... | collective-permute-start | bytes 1966088 | tf_op jit(solution)/shard_map/ppermute | solution.py:214
  296.4 47.0 %collective-permute-start.7 = (bf16[64,5120]{1,0:T(8,128)(2,1)}, bf16[64,5120]{1,0:T(8,128)(2,1)S(1)}, u32[]{:S(2)}, u32[]{:S(2)}) collective-permute-start(bf16[64,5120]{1,0:T(8,128)(2,1)} %collective-permute-done.6), channel_id=1, source_target_pairs={{0,132},{4,136},{8,140},{12,0},{128,4},{132,8},{136,12},{140,128},... | collective-permute-start | bytes 1966088 | tf_op jit(solution)/shard_map/ppermute | solution.py:214
  343.4 2.8 copy-start.1
Sparse Core Ops, SparseCore 0:
  9.1 95.5 all-gather.2
  106.5 89.1 all-gather.4
  243.2 29.0 reduce-scatter.1

commit v8 on v7

--- a/solution.py
+++ b/solution.py
@@ -39,13 +39,13 @@
 
     @pl.when(step < count_ref[0])
     def _slot():
-        for head in range(heads):
-            cols = pl.ds(head * HD, HD)
+        def one_head(head, carry):
+            cols = pl.ds(pl.multiple_of(head * HD, HD), HD)
             scores = lax.dot_general(
                 q_ref[:, cols], k_ref[0, 0, :, cols], (((1,), (1,)), ((), ())),
                 preferred_element_type=jnp.float32,
             ) * (1.0 / math.sqrt(HD))
-            running_max = m_ref[:, pl.ds(head * HD, 1)]
+            running_max = m_ref[:, cols][:, :1]
             new_max = jnp.maximum(running_max, jnp.max(scores, axis=1, keepdims=True))
             shrink = jnp.exp(running_max - new_max)
             weights = jnp.exp(scores - new_max)
@@ -55,6 +55,9 @@
                 preferred_element_type=jnp.float32,
             )
             m_ref[:, cols] = jnp.broadcast_to(new_max, (new_max.shape[0], HD))
+            return carry
+
+        lax.fori_loop(0, heads, one_head, 0)
 
 
 def attend(queries, arrived, order, count, init=None):

time: 353 us -> 353 us (level)
  no operation moved by 1% of the time
where the time goes in v8:
time: 353 us
  waiting for transfers between devices  206 us (58%)
  Pallas kernels  43.8 us (12%)
  starting transfers between devices  38.1 us (11%)
  local copies, waits for them, and re-layouts  24.1 us (7%)
  between operations  16.1 us (5%)
  other arithmetic  15.8 us (4%)
  matrix products  8.83 us (3%)
    ppermute x4, waiting for transfers between devices, shifted(): lax.ppermute(rows, z_axes, [(i, (i + by) % ring) for i in range(ring)])  61.7 us
    all_gather x1, waiting for transfers between devices, local(): weight = lax.all_gather(out_weight, ('zl', 'x'), axis=1, tiled=True)  57.2 us
    pallas_call x4, Pallas kernels, attend(): pl.pallas_call(lambda *refs: attend_kernel(*refs, with_init=with_init, he...  43.8 us
    all_to_all x1, waiting for transfers between devices, local(): lax.all_to_all(sent, FRAME_AXES, split_axis=2, concat_axis=2, tiled=True)  43.2 us
    reduce_scatter x1, waiting for transfers between devices, local(): lax.psum_scatter(partial_value.astype(jnp.bfloat16), 'core', scatter_dime...  29.6 us
    ppermute x3, starting transfers between devices, local(): lax.ppermute((other_max[:, ::HD], other_sum[:, ::HD], other_out), 'x', swap)  15.8 us
    ppermute x3, waiting for transfers between devices, local(): lax.ppermute((other_max[:, ::HD], other_sum[:, ::HD], other_out), 'x', swap)  14 us
    all_to_all x1, starting transfers between devices, local(): lax.all_to_all(sent, FRAME_AXES, split_axis=2, concat_axis=2, tiled=True)  11.8 us
  transfers between devices with their start and end apart: 12, of which 8 were waited for; matrix products, arithmetic and copies ran while one was open for 10% of the time, Pallas kernels for 12%

profile of v8, /device:TPU:50, one launch (start us, length us, event | category | flops | bytes accessed | tf_op | source)
XLA Modules:
  0.0 353.2 jit_solution(9372732235937327365)
XLA Ops:
  6.5 0.0 copy-start
  6.5 0.0 all-gather.3.cloned.1.call-start
  6.5 0.7 all-gather.3.cloned.1.call-update
  7.3 1.4 iota_subtract_fusion
  8.7 0.8 select_reduce_fusion.3
  9.5 0.8 copy.34
  10.3 0.1 reshape.332
  10.5 0.3 select_reduce_fusion
  10.8 0.9 select_reduce_fusion.2
  11.7 0.1 reshape.343
  11.8 0.0 copy-done
  11.8 0.0 copy-start.3
  11.8 2.5 gather_fusion
  14.3 2.4 gather_fusion.1
  16.7 3.1 pad_maximum_fusion
  19.8 3.2 copy.35
  23.0 11.8 %all-to-all-start = ((bf16[2,4,64,8,640]{4,3,1,0,2:T(8,128)(2,1)}), bf16[2,4,64,8,640]{4,3,1,0,2:T(8,128)(2,1)}, u32[]{:S(2)}, u32[]{:S(2)}) async-start(bf16[2,4,64,8,640]{4,3,1,0,2:T(8,128)(2,1)} %copy.35), calls=%async_computation | async-start | bytes 10485760 | tf_op jit(solution)/shard_map/all_to_all | solution.py:151
  34.8 0.0 all-gather.5.cloned.1.call-start
  34.9 1.2 maximum_bitcast_fusion.refs_3_.refs_4_
  36.1 9.7 %shard_map.92 = (f32[512,640]{1,0:T(8,128)}, f32[512,640]{1,0:T(8,128)}, f32[512,640]{1,0:T(8,128)}) custom-call(s32[1]{0:T(128)} %constant.88.clone.1.refs_0_, s32[1]{0:T(128)} %constant.89.clone.1.refs_1_, bf16[512,640]{1,0:T(8,128)(2,1)} %bitcast.36, bf16[2,1,512,640]{3,2,1,0:T(8,128)(2,1)} %maximum_bitcast_fusion.refs_3_.refs_4_, ...), custom_call_target="tpu_custom_call" | custom-call | flops 671088640 | bytes 9175040 | tf_op jit(solution)/shard_map/pallas_call | solution.py:83
  45.8 57.2 %all-gather.3.cloned.1.call-done = bf16[640,1280]{0,1:T(8,128)(2,1)} async-done(((bf16[640,80]{0,1:T(8,128)(2,1)}), bf16[640,1280]{0,1:T(8,128)(2,1)}) %all-gather.3.cloned.1.call-update) | async-done | bytes 1638416 | tf_op jit(solution)/shard_map/all_gather | solution.py:147
  103.0 0.0 all-gather.5.cloned.1.call-update
  103.0 0.0 reduce-scatter.2.cloned.1.call-start
  103.1 2.4 collective-permute-start
  108.3 0.5 broadcast_select_fusion.refs_0_
  108.8 0.6 broadcast_select_fusion.1.refs_0_
  109.4 43.2 %all-to-all-done = bf16[2,4,64,8,640]{4,3,1,0,2:T(8,128)(2,1)} async-done(((bf16[2,4,64,8,640]{4,3,1,0,2:T(8,128)(2,1)}), bf16[2,4,64,8,640]{4,3,1,0,2:T(8,128)(2,1)}, u32[]{:S(2)}, u32[]{:S(2)}) %all-to-all-start) | async-done | bytes 5242912 | tf_op jit(solution)/shard_map/all_to_all | solution.py:151
  152.5 5.3 %copy.44 = bf16[2,4,64,8,640]{4,3,2,1,0:T(8,128)(2,1)} copy(bf16[2,4,64,8,640]{4,3,1,0,2:T(8,128)(2,1)} %all-to-all-done) | data formatting | bytes 10485760 | tf_op jit(solution)/shard_map/all_to_all | solution.py:151
  157.9 11.8 %shard_map.93 = (f32[512,640]{1,0:T(8,128)}, f32[512,640]{1,0:T(8,128)}, f32[512,640]{1,0:T(8,128)}) custom-call(s32[4]{0:T(128)} %broadcast_select_fusion.refs_0_, s32[1]{0:T(128)} %bitcast.7.refs_1_, bf16[512,640]{1,0:T(8,128)(2,1)} %bitcast.37, bf16[2,4,512,640]{3,2,1,0:T(8,128)(2,1)} %bitcast.28, bf16[2,4,512,640]{3,2,1,0:T(8,128)(2,1)} %bitcast.29, ...), custom_call_target="tpu_custom_call" | custom-call | flops 2684354560 | bytes 13107200 | tf_op jit(solution)/shard_map/pallas_call | solution.py:83
  169.7 0.0 collective-permute-done.refs_2_
  169.7 0.9 copy-done.4
  170.5 4.6 %shard_map.91 = (f32[512,640]{1,0:T(8,128)}, f32[512,640]{1,0:T(8,128)}, f32[512,640]{1,0:T(8,128)}) custom-call(s32[4]{0:T(128)} %broadcast_select_fusion.1.refs_0_, s32[1]{0:T(128)} %bitcast.6.refs_1_, bf16[512,640]{1,0:T(8,128)(2,1)} %copy-done.4, bf16[2,4,512,640]{3,2,1,0:T(8,128)(2,1)} %bitcast.30, bf16[2,4,512,640]{3,2,1,0:T(8,128)(2,1)} %bitcast.31), custom_call_target="tpu_custom_call" | custom-call | flops 2684354560 | bytes 13107200 | tf_op jit(solution)/shard_map/pallas_call | solution.py:83
  175.1 13.4 %collective-permute-start.2 = (f32[512,640]{1,0:T(8,128)}, f32[512,640]{1,0:T(8,128)}, u32[]{:S(2)}, u32[]{:S(2)}) collective-permute-start(f32[512,640]{1,0:T(8,128)} %get-tuple-element.45), channel_id=1, source_target_pairs={{0,1},{1,0},{2,3},{3,2},{4,5},{5,4},{6,7},{7,6},{8,9},{9,8},{10,11... | collective-permute-start | bytes 3932168 | tf_op jit(solution)/shard_map/ppermute | solution.py:187
  188.5 0.6 broadcast_select_fusion.2.refs_0_
  189.1 2.4 slice.18
  191.6 0.1 collective-permute-start.1
  191.7 2.4 slice.19
  194.1 2.3 collective-permute-start.3
  196.4 17.8 %shard_map.94 = (f32[512,640]{1,0:T(8,128)}, f32[512,640]{1,0:T(8,128)}, f32[512,640]{1,0:T(8,128)}) custom-call(s32[4]{0:T(128)} %broadcast_select_fusion.2.refs_0_, s32[1]{0:T(128)} %bitcast.refs_1_, bf16[512,640]{1,0:T(8,128)(2,1)} %bitcast.38, bf16[2,4,512,640]{3,2,1,0:T(8,128)(2,1)} %bitcast.32, bf16[2,4,512,640]{3,2,1,0:T(8,128)(2,1)} %bitcast.33, ...), custom_call_target="tpu_custom_call" | custom-call | flops 2684354560 | bytes 13107200 | tf_op jit(solution)/shard_map/pallas_call | solution.py:83
  214.2 9.8 %collective-permute-done.1 = f32[512,5]{1,0:T(8,128)S(1)} collective-permute-done((f32[512,5]{1,0:T(8,128)S(1)}, f32[512,5]{1,0:T(8,128)S(1)}, u32[]{:S(2)}, u32[]{:S(2)}) %collective-permute-start.1) | collective-permute-done | bytes 10272 | tf_op jit(solution)/shard_map/ppermute | solution.py:187
  224.0 0.1 copy.37
  224.1 0.2 broadcast_in_dim.64
  224.3 0.4 copy.38
  224.7 4.2 %collective-permute-done.3 = f32[512,5]{1,0:T(8,128)S(1)} collective-permute-done((f32[512,5]{1,0:T(8,128)S(1)}, f32[512,5]{1,0:T(8,128)S(1)}, u32[]{:S(2)}, u32[]{:S(2)}) %collective-permute-start.3) | collective-permute-done | bytes 10272 | tf_op jit(solution)/shard_map/ppermute | solution.py:187
  228.9 0.1 copy.40
  229.0 0.2 broadcast_in_dim.65
  229.2 1.5 copy.41
  230.7 0.0 collective-permute-done.2
  230.7 3.6 %divide_convert_fusion = bf16[512,640]{1,0:T(8,128)(2,1)S(1)} fusion(f32[512,640]{1,0:T(8,128)} %copy.41, f32[512,640]{1,0:T(8,128)} %get-tuple-element.46, f32[512,640]{1,0:T(8,128)} %collective-permute-done.2, f32[512,640]{1,0:T(8,128)S(1)} %copy.38, f32[512,640]{1,0:T(8,128)} %get-tuple-element.43, f32[512,640]{1,0:T(8,128)} %get-tuple-element.42), kind=kLoop, calls=%fused_computation.11 | loop fusion | flops 3604480 | bytes 8519680 | tf_op jit(solution)/shard_map/convert_element_type | solution.py:200
  234.3 0.1 copy.42
  234.3 0.0 all-gather.5.cloned.1.call-done
  234.3 8.8 %convolution_convert_fusion = bf16[512,5120]{1,0:T(8,128)(2,1)} fusion(bf16[512,640]{1,0:T(8,128)(2,1)S(1)} %bitcast.45, bf16[640,5120]{0,1:T(8,128)(2,1)} %all-gather.5.cloned.1.call-done), kind=kOutput, calls=%fused_computation.2 | convolution fusion | flops 3358064640 | bytes 12451840 | tf_op jit(solution)/shard_map/dot_general | solution.py:205
  243.2 0.0 reduce-scatter.2.cloned.1.call-update
  243.2 29.6 %reduce-scatter.2.cloned.1.call-done = bf16[256,5120]{1,0:T(8,128)(2,1)} async-done(((bf16[512,5120]{1,0:T(8,128)(2,1)}), bf16[256,5120]{1,0:T(8,128)(2,1)}) %reduce-scatter.2.cloned.1.call-update) | async-done | bytes 2621456 | tf_op jit(solution)/shard_map/reduce_scatter | solution.py:206
  272.8 1.4 dynamic-slice_bitcast_fusion.1
  274.2 1.6 collective-permute-start.4
  275.8 0.5 collective-permute-start.6
  276.3 14.8 %collective-permute-done.4 = bf16[64,5120]{1,0:T(8,128)(2,1)S(1)} collective-permute-done((bf16[64,5120]{1,0:T(8,128)(2,1)S(1)}, bf16[64,5120]{1,0:T(8,128)(2,1)S(1)}, u32[]{:S(2)}, u32[]{:S(2)}) %collective-permute-start.4) | collective-permute-done | bytes 655392 | tf_op jit(solution)/shard_map/ppermute | solution.py:217
  291.0 5.9 %collective-permute-start.5 = (bf16[64,5120]{1,0:T(8,128)(2,1)S(1)}, bf16[64,5120]{1,0:T(8,128)(2,1)S(1)}, u32[]{:S(2)}, u32[]{:S(2)}) collective-permute-start(bf16[64,5120]{1,0:T(8,128)(2,1)S(1)} %collective-permute-done.4), channel_id=1, source_target_pairs={{0,12},{4,128},{8,132},{12,136},{128,140},{132,0},{136,4},{140,8},... | collective-permute-start | bytes 1966088 | tf_op jit(solution)/shard_map/ppermute | solution.py:217
  297.0 0.0 collective-permute-done.6
  297.0 0.0 collective-permute-start.7
  297.0 40.7 %collective-permute-done.5 = bf16[64,5120]{1,0:T(8,128)(2,1)S(1)} collective-permute-done((bf16[64,5120]{1,0:T(8,128)(2,1)S(1)}, bf16[64,5120]{1,0:T(8,128)(2,1)S(1)}, u32[]{:S(2)}, u32[]{:S(2)}) %collective-permute-start.5) | collective-permute-done | bytes 655392 | tf_op jit(solution)/shard_map/ppermute | solution.py:217
  337.7 6.2 %collective-permute-done.7 = bf16[64,5120]{1,0:T(8,128)(2,1)S(1)} collective-permute-done((bf16[64,5120]{1,0:T(8,128)(2,1)}, bf16[64,5120]{1,0:T(8,128)(2,1)S(1)}, u32[]{:S(2)}, u32[]{:S(2)}) %collective-permute-start.7) | collective-permute-done | bytes 655392 | tf_op jit(solution)/shard_map/ppermute | solution.py:217
  343.9 2.8 add_convert_fusion
  (16 shorter events, 0.1 us)
Async XLA Ops:
  6.5 5.3 %copy-start = (bf16[128,8,640]{2,1,0:T(8,128)(2,1)S(1)}, bf16[128,8,640]{2,1,0:T(8,128)(2,1)}, u32[]{:S(2)}) copy-start(bf16[128,8,640]{2,1,0:T(8,128)(2,1)} %param.12) | copy-start | bytes 3932164
  6.5 96.4 %all-gather.3.cloned.1.call-start = ((), (), s32[]{:S(2)}) async-start(), calls=%async_computation.2 | async-start | bytes 1740800 | tf_op jit(solution)/shard_map/all_gather | solution.py:147
  11.8 2.5 copy-start.3
  23.0 11.9 %copy-start.5 = (bf16[1,512,640]{2,1,0:T(8,128)(2,1)S(1)}, bf16[1,512,640]{2,1,0:T(8,128)(2,1)}, u32[]{:S(2)}) copy-start(bf16[1,512,640]{2,1,0:T(8,128)(2,1)} %param.11) | copy-start | bytes 1966084
  23.0 11.9 %copy-start.6 = (bf16[1,512,640]{2,1,0:T(8,128)(2,1)S(1)}, bf16[1,512,640]{2,1,0:T(8,128)(2,1)}, u32[]{:S(2)}) copy-start(bf16[1,512,640]{2,1,0:T(8,128)(2,1)} %param.10) | copy-start | bytes 1966084
  23.0 129.5 %all-to-all-start = ((bf16[2,4,64,8,640]{4,3,1,0,2:T(8,128)(2,1)}), bf16[2,4,64,8,640]{4,3,1,0,2:T(8,128)(2,1)}, u32[]{:S(2)}, u32[]{:S(2)}) async-start(bf16[2,4,64,8,640]{4,3,1,0,2:T(8,128)(2,1)} %copy.35), calls=%async_computation | async-start | bytes 10485760 | tf_op jit(solution)/shard_map/all_to_all | solution.py:151
  34.8 199.5 %all-gather.5.cloned.1.call-start = ((), (), s32[]{:S(2)}) async-start(), calls=%async_computation.3 | async-start | bytes 8192000 | tf_op jit(solution)/shard_map/all_gather | solution.py:172
  45.8 57.3 %copy-start.2 = (bf16[1,512,640]{2,1,0:T(8,128)(2,1)S(1)}, bf16[1,512,640]{2,1,0:T(8,128)(2,1)}, u32[]{:S(2)}) copy-start(bf16[1,512,640]{2,1,0:T(8,128)(2,1)} %param.9) | copy-start | bytes 1966084
  103.0 169.8 %reduce-scatter.2.cloned.1.call-start = ((), (), s32[]{:S(2)}) async-start(), calls=%async_computation.4 | async-start | bytes 7864320 | tf_op jit(solution)/shard_map/reduce_scatter | solution.py:206
  103.1 66.6 %collective-permute-start = (bf16[512,640]{1,0:T(8,128)(2,1)S(1)}, bf16[512,640]{1,0:T(8,128)(2,1)S(1)}, u32[]{:S(2)}, u32[]{:S(2)}) collective-permute-start(bf16[512,640]{1,0:T(8,128)(2,1)S(1)} %bitcast.39), channel_id=1, source_target_pairs={{0,1},{1,0},{2,3},{3,2},{4,5},{5,4},{6,7},{7,6},{8,9},{9,8},{10,11... | collective-permute-start | bytes 1966088 | tf_op jit(solution)/shard_map/ppermute | solution.py:155
  169.7 0.9 copy-start.4
  175.1 55.6 %collective-permute-start.2 = (f32[512,640]{1,0:T(8,128)}, f32[512,640]{1,0:T(8,128)}, u32[]{:S(2)}, u32[]{:S(2)}) collective-permute-start(f32[512,640]{1,0:T(8,128)} %get-tuple-element.45), channel_id=1, source_target_pairs={{0,1},{1,0},{2,3},{3,2},{4,5},{5,4},{6,7},{7,6},{8,9},{9,8},{10,11... | collective-permute-start | bytes 3932168 | tf_op jit(solution)/shard_map/ppermute | solution.py:187
  191.6 32.4 %collective-permute-start.1 = (f32[512,5]{1,0:T(8,128)S(1)}, f32[512,5]{1,0:T(8,128)S(1)}, u32[]{:S(2)}, u32[]{:S(2)}) collective-permute-start(f32[512,5]{1,0:T(8,128)S(1)} %slice.18), channel_id=1, source_target_pairs={{0,1},{1,0},{2,3},{3,2},{4,5},{5,4},{6,7},{7,6},{8,9},{9,8},{10,11... | collective-permute-start | bytes 30728 | tf_op jit(solution)/shard_map/ppermute | solution.py:187
  194.1 34.8 %collective-permute-start.3 = (f32[512,5]{1,0:T(8,128)S(1)}, f32[512,5]{1,0:T(8,128)S(1)}, u32[]{:S(2)}, u32[]{:S(2)}) collective-permute-start(f32[512,5]{1,0:T(8,128)S(1)} %slice.19), channel_id=1, source_target_pairs={{0,1},{1,0},{2,3},{3,2},{4,5},{5,4},{6,7},{7,6},{8,9},{9,8},{10,11... | collective-permute-start | bytes 30728 | tf_op jit(solution)/shard_map/ppermute | solution.py:187
  274.2 16.9 %collective-permute-start.4 = (bf16[64,5120]{1,0:T(8,128)(2,1)S(1)}, bf16[64,5120]{1,0:T(8,128)(2,1)S(1)}, u32[]{:S(2)}, u32[]{:S(2)}) collective-permute-start(bf16[64,5120]{1,0:T(8,128)(2,1)S(1)} %get-tuple-element.51), channel_id=1, source_target_pairs={{0,4},{4,8},{8,12},{12,128},{128,132},{132,136},{136,140},{140,0},... | collective-permute-start | bytes 1966088 | tf_op jit(solution)/shard_map/ppermute | solution.py:217
  275.8 21.2 %collective-permute-start.6 = (bf16[64,5120]{1,0:T(8,128)(2,1)S(1)}, bf16[64,5120]{1,0:T(8,128)(2,1)}, u32[]{:S(2)}, u32[]{:S(2)}) collective-permute-start(bf16[64,5120]{1,0:T(8,128)(2,1)S(1)} %get-tuple-element.52), channel_id=1, source_target_pairs={{0,140},{4,0},{8,4},{12,8},{128,12},{132,128},{136,132},{140,136},... | collective-permute-start | bytes 1966088 | tf_op jit(solution)/shard_map/ppermute | solution.py:217
  291.0 46.7 %collective-permute-start.5 = (bf16[64,5120]{1,0:T(8,128)(2,1)S(1)}, bf16[64,5120]{1,0:T(8,128)(2,1)S(1)}, u32[]{:S(2)}, u32[]{:S(2)}) collective-permute-start(bf16[64,5120]{1,0:T(8,128)(2,1)S(1)} %collective-permute-done.4), channel_id=1, source_target_pairs={{0,12},{4,128},{8,132},{12,136},{128,140},{132,0},{136,4},{140,8},... | collective-permute-start | bytes 1966088 | tf_op jit(solution)/shard_map/ppermute | solution.py:217
  297.0 46.9 %collective-permute-start.7 = (bf16[64,5120]{1,0:T(8,128)(2,1)}, bf16[64,5120]{1,0:T(8,128)(2,1)S(1)}, u32[]{:S(2)}, u32[]{:S(2)}) collective-permute-start(bf16[64,5120]{1,0:T(8,128)(2,1)} %collective-permute-done.6), channel_id=1, source_target_pairs={{0,132},{4,136},{8,140},{12,0},{128,4},{132,8},{136,12},{140,128},... | collective-permute-start | bytes 1966088 | tf_op jit(solution)/shard_map/ppermute | solution.py:217
  343.9 2.8 copy-start.1
Sparse Core Ops, SparseCore 0:
  9.1 93.8 all-gather.2
  104.8 90.5 all-gather.4
  243.3 29.4 reduce-scatter.1

commit v9 on v7

--- a/solution.py
+++ b/solution.py
@@ -195,29 +195,40 @@
     total_sum = own_sum * own_scale + got_sum * got_scale
     total_out = own_out * own_scale + got_out * got_scale
     attended = (total_out / total_sum).astype(jnp.bfloat16)
+    partial_value = jnp.dot(attended, weight, preferred_element_type=jnp.float32)
+    partial_value = partial_value.astype(jnp.bfloat16)
     quarters = lax.axis_size("zh") * lax.axis_size("core")
     quarter_rows = tokens_here // quarters
-    attended = attended.reshape(lax.axis_size("zh"), lax.axis_size("core"), quarter_rows, row_width)
-    attended = attended.transpose(1, 0, 2, 3).reshape(tokens_here, row_width)
-    partial_value = jnp.dot(attended, weight, preferred_element_type=jnp.float32)
-    on_chip = lax.psum_scatter(
-        partial_value.astype(jnp.bfloat16), "core", scatter_dimension=0, tiled=True
-    )
-    on_chip = on_chip.reshape(lax.axis_size("zh"), quarter_rows, -1)
     chip_half = lax.axis_index("zh")
-    mine = lax.dynamic_index_in_dim(on_chip, chip_half, 0, keepdims=False)
-    theirs = lax.dynamic_index_in_dim(on_chip, 1 - chip_half, 0, keepdims=False)
+    core = lax.axis_index("core")
+    cores = lax.axis_size("core")
+    core_swap = [(i, cores - 1 - i) for i in range(cores)]
+
+    def quarter(zh, k):
+        return lax.dynamic_slice_in_dim(partial_value, (zh * cores + k) * quarter_rows, quarter_rows)
+
+    theirs = quarter(1 - chip_half, core).astype(jnp.float32) + lax.ppermute(
+        quarter(1 - chip_half, cores - 1 - core), "core", core_swap
+    ).astype(jnp.float32)
+    theirs = theirs.astype(jnp.bfloat16)
     ring = lax.axis_size("zh") * lax.axis_size("zl")
     z_axes = ("zh", "zl")
 
     def shifted(rows, by):
         return lax.ppermute(rows, z_axes, [(i, (i + by) % ring) for i in range(ring)])
 
-    half = quarter_rows // 2
-    up = shifted(shifted(theirs[:half], 1), ring // 2 - 1)
-    down = shifted(shifted(theirs[half:], -1), 1 - ring // 2)
-    received = jnp.concatenate([up, down], axis=0)
-    own_rows = (mine.astype(jnp.float32) + received.astype(jnp.float32)).astype(jnp.bfloat16)
+    pieces = 4
+    piece_rows = quarter_rows // pieces
+    received = []
+    for piece in range(pieces):
+        rows = theirs[piece * piece_rows:(piece + 1) * piece_rows]
+        first = 1 if piece < pieces // 2 else -1
+        received.append(shifted(shifted(rows, first), first * (ring // 2 - 1)))
+    received = jnp.concatenate(received, axis=0)
+    mine = quarter(chip_half, core).astype(jnp.float32) + lax.ppermute(
+        quarter(chip_half, cores - 1 - core), "core", core_swap
+    ).astype(jnp.float32)
+    own_rows = (mine + received.astype(jnp.float32)).astype(jnp.bfloat16)
     return own_rows[None]
 
 

time: 353 us -> 350 us (level)
  the two profiles are of different devices: /device:TPU:50 before, /device:TPU:24 now
where the time goes in v9:
time: 350 us; the launch traced here: 343 us
  waiting for transfers between devices  176 us (50%)
  starting transfers between devices  52.6 us (15%)
  Pallas kernels  48.7 us (14%)
  local copies, waits for them, and re-layouts  25.5 us (7%)
  between operations  16.6 us (5%)
  other arithmetic  14.3 us (4%)
  matrix products  9.36 us (3%)
    all_gather x1, waiting for transfers between devices, local(): weight = lax.all_gather(out_weight, ('zl', 'x'), axis=1, tiled=True)  63.3 us
    ppermute x8, waiting for transfers between devices, shifted(): lax.ppermute(rows, z_axes, [(i, (i + by) % ring) for i in range(ring)])  55.8 us
    pallas_call x4, Pallas kernels, attend(): pl.pallas_call(lambda *refs: attend_kernel(*refs, with_init=with_init, he...  48.7 us
    all_to_all x1, waiting for transfers between devices, local(): lax.all_to_all(sent, FRAME_AXES, split_axis=2, concat_axis=2, tiled=True)  45 us
    ppermute x8, starting transfers between devices, shifted(): lax.ppermute(rows, z_axes, [(i, (i + by) % ring) for i in range(ring)])  30.9 us
    all_to_all x1, starting transfers between devices, local(): lax.all_to_all(sent, FRAME_AXES, split_axis=2, concat_axis=2, tiled=True)  12.3 us
    dot_general x1, matrix products, local(): jnp.dot(attended, weight, preferred_element_type=jnp.float32)  9.36 us
    ppermute x3, waiting for transfers between devices, local(): lax.ppermute((other_max[:, ::HD], other_sum[:, ::HD], other_out), 'x', swap)  8.64 us
  transfers between devices with their start and end apart: 17, of which 11 were waited for; matrix products, arithmetic and copies ran while one was open for 10% of the time, Pallas kernels for 14%

profile of v9, /device:TPU:24, one launch (start us, length us, event | category | flops | bytes accessed | tf_op | source)
XLA Modules:
  0.0 343.0 jit_solution(726443656192946314)
XLA Ops:
  6.5 0.7 all-gather.3.cloned.1.call-update
  7.3 1.3 iota_subtract_fusion
  8.6 0.8 select_reduce_fusion.3
  9.5 0.8 copy.31
  10.2 0.1 reshape.292
  10.4 0.3 select_reduce_fusion
  10.8 0.9 select_reduce_fusion.2
  11.6 0.1 reshape.300
  11.7 0.0 copy-start.3
  11.8 2.5 gather_fusion
  14.2 2.4 gather_fusion.1
  16.7 3.1 pad_maximum_fusion
  19.7 3.2 copy.32
  22.9 12.3 %all-to-all-start = ((bf16[2,4,64,8,640]{4,3,1,0,2:T(8,128)(2,1)}), bf16[2,4,64,8,640]{4,3,1,0,2:T(8,128)(2,1)}, u32[]{:S(2)}, u32[]{:S(2)}) async-start(bf16[2,4,64,8,640]{4,3,1,0,2:T(8,128)(2,1)} %copy.32), calls=%async_computation | async-start | bytes 10485760 | tf_op jit(solution)/shard_map/all_to_all | solution.py:148
  35.2 0.0 all-gather.5.cloned.1.call-start
  35.3 1.2 maximum_bitcast_fusion.refs_3_.refs_4_
  36.5 9.5 %shard_map.92 = (f32[512,640]{1,0:T(8,128)}, f32[512,640]{1,0:T(8,128)}, f32[512,640]{1,0:T(8,128)}) custom-call(s32[1]{0:T(128)} %constant.86.clone.1.refs_0_, s32[1]{0:T(128)} %constant.87.clone.1.refs_1_, bf16[512,640]{1,0:T(8,128)(2,1)} %bitcast.26, bf16[2,1,512,640]{3,2,1,0:T(8,128)(2,1)} %maximum_bitcast_fusion.refs_3_.refs_4_, ...), custom_call_target="tpu_custom_call" | custom-call | flops 671088640 | bytes 9175040 | tf_op jit(solution)/shard_map/pallas_call | solution.py:80
  46.0 63.3 %all-gather.3.cloned.1.call-done = bf16[640,1280]{0,1:T(8,128)(2,1)} async-done(((bf16[640,80]{0,1:T(8,128)(2,1)}), bf16[640,1280]{0,1:T(8,128)(2,1)}) %all-gather.3.cloned.1.call-update) | async-done | bytes 1638416 | tf_op jit(solution)/shard_map/all_gather | solution.py:144
  109.2 0.0 all-gather.5.cloned.1.call-update
  109.3 0.3 collective-permute-start
  112.1 0.5 broadcast_select_fusion.refs_0_
  112.6 0.5 broadcast_select_fusion.1.refs_0_
  113.1 45.0 %all-to-all-done = bf16[2,4,64,8,640]{4,3,1,0,2:T(8,128)(2,1)} async-done(((bf16[2,4,64,8,640]{4,3,1,0,2:T(8,128)(2,1)}), bf16[2,4,64,8,640]{4,3,1,0,2:T(8,128)(2,1)}, u32[]{:S(2)}, u32[]{:S(2)}) %all-to-all-start) | async-done | bytes 5242912 | tf_op jit(solution)/shard_map/all_to_all | solution.py:148
  158.1 5.3 %copy.40 = bf16[2,4,64,8,640]{4,3,2,1,0:T(8,128)(2,1)} copy(bf16[2,4,64,8,640]{4,3,1,0,2:T(8,128)(2,1)} %all-to-all-done) | data formatting | bytes 10485760 | tf_op jit(solution)/shard_map/all_to_all | solution.py:148
  163.5 11.6 %shard_map.93 = (f32[512,640]{1,0:T(8,128)}, f32[512,640]{1,0:T(8,128)}, f32[512,640]{1,0:T(8,128)}) custom-call(s32[4]{0:T(128)} %broadcast_select_fusion.refs_0_, s32[1]{0:T(128)} %bitcast.7.refs_1_, bf16[512,640]{1,0:T(8,128)(2,1)} %bitcast.27, bf16[2,4,512,640]{3,2,1,0:T(8,128)(2,1)} %bitcast.18, bf16[2,4,512,640]{3,2,1,0:T(8,128)(2,1)} %bitcast.19, ...), custom_call_target="tpu_custom_call" | custom-call | flops 2684354560 | bytes 13107200 | tf_op jit(solution)/shard_map/pallas_call | solution.py:80
  175.1 0.9 copy-done.5
  175.9 4.6 %shard_map.91 = (f32[512,640]{1,0:T(8,128)}, f32[512,640]{1,0:T(8,128)}, f32[512,640]{1,0:T(8,128)}) custom-call(s32[4]{0:T(128)} %broadcast_select_fusion.1.refs_0_, s32[1]{0:T(128)} %bitcast.6.refs_1_, bf16[512,640]{1,0:T(8,128)(2,1)} %copy-done.5, bf16[2,4,512,640]{3,2,1,0:T(8,128)(2,1)} %bitcast.20, bf16[2,4,512,640]{3,2,1,0:T(8,128)(2,1)} %bitcast.21), custom_call_target="tpu_custom_call" | custom-call | flops 2684354560 | bytes 13107200 | tf_op jit(solution)/shard_map/pallas_call | solution.py:80
  180.5 6.2 %collective-permute-start.2 = (f32[512,640]{1,0:T(8,128)}, f32[512,640]{1,0:T(8,128)}, u32[]{:S(2)}, u32[]{:S(2)}) collective-permute-start(f32[512,640]{1,0:T(8,128)} %get-tuple-element.45), channel_id=1, source_target_pairs={{0,1},{1,0},{2,3},{3,2},{4,5},{5,4},{6,7},{7,6},{8,9},{9,8},{10,11... | collective-permute-start | bytes 3932168 | tf_op jit(solution)/shard_map/ppermute | solution.py:184
  186.7 0.5 broadcast_select_fusion.2.refs_0_
  187.2 2.4 slice.18
  189.7 0.1 collective-permute-start.1
  189.8 2.4 slice.19
  192.2 2.3 collective-permute-start.3
  194.5 23.1 %shard_map.94 = (f32[512,640]{1,0:T(8,128)}, f32[512,640]{1,0:T(8,128)}, f32[512,640]{1,0:T(8,128)}) custom-call(s32[4]{0:T(128)} %broadcast_select_fusion.2.refs_0_, s32[1]{0:T(128)} %bitcast.refs_1_, bf16[512,640]{1,0:T(8,128)(2,1)} %bitcast.28, bf16[2,4,512,640]{3,2,1,0:T(8,128)(2,1)} %bitcast.22, bf16[2,4,512,640]{3,2,1,0:T(8,128)(2,1)} %bitcast.23, ...), custom_call_target="tpu_custom_call" | custom-call | flops 2684354560 | bytes 13107200 | tf_op jit(solution)/shard_map/pallas_call | solution.py:80
  217.7 4.5 %collective-permute-done.1 = f32[512,5]{1,0:T(8,128)S(1)} collective-permute-done((f32[512,5]{1,0:T(8,128)S(1)}, f32[512,5]{1,0:T(8,128)S(1)}, u32[]{:S(2)}, u32[]{:S(2)}) %collective-permute-start.1) | collective-permute-done | bytes 10272 | tf_op jit(solution)/shard_map/ppermute | solution.py:184
  222.1 0.1 copy.34
  222.2 0.2 broadcast_in_dim.66
  222.4 0.4 copy.35
  222.8 4.2 %collective-permute-done.3 = f32[512,5]{1,0:T(8,128)S(1)} collective-permute-done((f32[512,5]{1,0:T(8,128)S(1)}, f32[512,5]{1,0:T(8,128)S(1)}, u32[]{:S(2)}, u32[]{:S(2)}) %collective-permute-start.3) | collective-permute-done | bytes 10272 | tf_op jit(solution)/shard_map/ppermute | solution.py:184
  227.0 0.1 copy.37
  227.1 0.2 broadcast_in_dim.67
  227.3 1.5 copy.38
  228.7 0.0 collective-permute-done.2
  228.7 9.4 %convolution_convert_fusion = bf16[512,5120]{1,0:T(8,128)(2,1)S(1)} fusion(bf16[640,5120]{0,1:T(8,128)(2,1)} %all-gather.5.cloned.1.call-done, f32[512,640]{1,0:T(8,128)} %copy.38, f32[512,640]{1,0:T(8,128)} %get-tuple-element.46, f32[512,640]{1,0:T(8,128)} %collective-permute-done.2, f32[512,640]{1,0:T(8,128)S(1)} %copy.35, ...), kind=kOutput, calls=%fused_computation.2 | convolution fusion | flops 3361669120 | bytes 19660800 | tf_op jit(solution)/shard_map/dot_general | solution.py:198
  238.1 1.4 constant_dynamic-slice_fusion.1
  239.5 1.4 copy-done.4
  240.9 0.5 collective-permute-start.4
  241.4 2.5 collective-permute-done.5
  243.9 1.6 add_convert_fusion.1
  245.5 0.1 fusion.6
  245.6 0.1 collective-permute-start.10
  245.7 7.3 %collective-permute-start.12 = (bf16[32,5120]{1,0:T(8,128)(2,1)S(1)}, bf16[32,5120]{1,0:T(8,128)(2,1)S(1)}, u32[]{:S(2)}, u32[]{:S(2)}) collective-permute-start(bf16[32,5120]{1,0:T(8,128)(2,1)S(1)} %get-tuple-element.54), channel_id=1, source_target_pairs={{0,140},{4,0},{8,4},{12,8},{128,12},{132,128},{136,132},{140,136},... | collective-permute-start | bytes 983048 | tf_op jit(solution)/shard_map/ppermute | solution.py:218
  253.0 8.9 %collective-permute-start.6 = (bf16[32,5120]{1,0:T(8,128)(2,1)S(1)}, bf16[32,5120]{1,0:T(8,128)(2,1)S(1)}, u32[]{:S(2)}, u32[]{:S(2)}) collective-permute-start(bf16[32,5120]{1,0:T(8,128)(2,1)S(1)} %get-tuple-element.53), channel_id=1, source_target_pairs={{0,4},{4,8},{8,12},{12,128},{128,132},{132,136},{136,140},{140,0},... | collective-permute-start | bytes 983048 | tf_op jit(solution)/shard_map/ppermute | solution.py:218
  261.9 1.9 collective-permute-start.8
  263.9 6.2 %collective-permute-done.10 = bf16[32,5120]{1,0:T(8,128)(2,1)S(1)} collective-permute-done((bf16[32,5120]{1,0:T(8,128)(2,1)S(1)}, bf16[32,5120]{1,0:T(8,128)(2,1)S(1)}, u32[]{:S(2)}, u32[]{:S(2)}) %collective-permute-start.10) | collective-permute-done | bytes 327712 | tf_op jit(solution)/shard_map/ppermute | solution.py:218
  270.1 3.1 collective-permute-start.11
  273.2 6.1 %collective-permute-done.12 = bf16[32,5120]{1,0:T(8,128)(2,1)S(1)} collective-permute-done((bf16[32,5120]{1,0:T(8,128)(2,1)S(1)}, bf16[32,5120]{1,0:T(8,128)(2,1)S(1)}, u32[]{:S(2)}, u32[]{:S(2)}) %collective-permute-start.12) | collective-permute-done | bytes 327712 | tf_op jit(solution)/shard_map/ppermute | solution.py:218
  279.2 9.1 %collective-permute-start.13 = (bf16[32,5120]{1,0:T(8,128)(2,1)S(1)}, bf16[32,5120]{1,0:T(8,128)(2,1)S(1)}, u32[]{:S(2)}, u32[]{:S(2)}) collective-permute-start(bf16[32,5120]{1,0:T(8,128)(2,1)S(1)} %collective-permute-done.12), channel_id=1, source_target_pairs={{0,132},{4,136},{8,140},{12,0},{128,4},{132,8},{136,12},{140,128},... | collective-permute-start | bytes 983048 | tf_op jit(solution)/shard_map/ppermute | solution.py:218
  288.4 0.4 collective-permute-start.9
  288.8 16.2 %collective-permute-done.11 = bf16[32,5120]{1,0:T(8,128)(2,1)S(1)} collective-permute-done((bf16[32,5120]{1,0:T(8,128)(2,1)S(1)}, bf16[32,5120]{1,0:T(8,128)(2,1)S(1)}, u32[]{:S(2)}, u32[]{:S(2)}) %collective-permute-start.11) | collective-permute-done | bytes 327712 | tf_op jit(solution)/shard_map/ppermute | solution.py:218
  305.1 10.6 %collective-permute-done.13 = bf16[32,5120]{1,0:T(8,128)(2,1)S(1)} collective-permute-done((bf16[32,5120]{1,0:T(8,128)(2,1)S(1)}, bf16[32,5120]{1,0:T(8,128)(2,1)S(1)}, u32[]{:S(2)}, u32[]{:S(2)}) %collective-permute-start.13) | collective-permute-done | bytes 327712 | tf_op jit(solution)/shard_map/ppermute | solution.py:218
  315.7 1.8 collective-permute-done.7
  317.5 14.8 %collective-permute-done.9 = bf16[32,5120]{1,0:T(8,128)(2,1)S(1)} collective-permute-done((bf16[32,5120]{1,0:T(8,128)(2,1)S(1)}, bf16[32,5120]{1,0:T(8,128)(2,1)S(1)}, u32[]{:S(2)}, u32[]{:S(2)}) %collective-permute-start.9) | collective-permute-done | bytes 327712 | tf_op jit(solution)/shard_map/ppermute | solution.py:218
  332.3 3.5 %fusion.2 = bf16[1,128,5120]{2,1,0:T(8,128)(2,1)} fusion(bf16[128,5120]{1,0:T(8,128)(2,1)} %collective-permute-done.4, bf16[32,5120]{1,0:T(8,128)(2,1)S(1)} %collective-permute-done.13, bf16[32,5120]{1,0:T(8,128)(2,1)S(1)} %collective-permute-done.11, bf16[32,5120]{1,0:T(8,128)(2,1)S(1)} %collective-permute-done.9, ...), kind=kLoop, calls=%fused_computation.11 | loop fusion | flops 8519680 | bytes 5242884 | tf_op jit(solution)/shard_map/broadcast_in_dim | solution.py:232
  (27 shorter events, 0.1 us)
Async XLA Ops:
  6.5 5.2 %copy-start = (bf16[128,8,640]{2,1,0:T(8,128)(2,1)S(1)}, bf16[128,8,640]{2,1,0:T(8,128)(2,1)}, u32[]{:S(2)}) copy-start(bf16[128,8,640]{2,1,0:T(8,128)(2,1)} %param.12) | copy-start | bytes 3932164
  6.5 102.7 %all-gather.3.cloned.1.call-start = ((), (), s32[]{:S(2)}) async-start(), calls=%async_computation.1 | async-start | bytes 1740800 | tf_op jit(solution)/shard_map/all_gather | solution.py:144
  11.7 2.5 copy-start.3
  22.9 12.3 %copy-start.6 = (bf16[1,512,640]{2,1,0:T(8,128)(2,1)S(1)}, bf16[1,512,640]{2,1,0:T(8,128)(2,1)}, u32[]{:S(2)}) copy-start(bf16[1,512,640]{2,1,0:T(8,128)(2,1)} %param.11) | copy-start | bytes 1966084
  22.9 12.3 %copy-start.7 = (bf16[1,512,640]{2,1,0:T(8,128)(2,1)S(1)}, bf16[1,512,640]{2,1,0:T(8,128)(2,1)}, u32[]{:S(2)}) copy-start(bf16[1,512,640]{2,1,0:T(8,128)(2,1)} %param.10) | copy-start | bytes 1966084
  22.9 135.2 %all-to-all-start = ((bf16[2,4,64,8,640]{4,3,1,0,2:T(8,128)(2,1)}), bf16[2,4,64,8,640]{4,3,1,0,2:T(8,128)(2,1)}, u32[]{:S(2)}, u32[]{:S(2)}) async-start(bf16[2,4,64,8,640]{4,3,1,0,2:T(8,128)(2,1)} %copy.32), calls=%async_computation | async-start | bytes 10485760 | tf_op jit(solution)/shard_map/all_to_all | solution.py:148
  35.2 193.5 %all-gather.5.cloned.1.call-start = ((), (), s32[]{:S(2)}) async-start(), calls=%async_computation.2 | async-start | bytes 8192000 | tf_op jit(solution)/shard_map/all_gather | solution.py:169
  45.9 63.3 %copy-start.2 = (bf16[1,512,640]{2,1,0:T(8,128)(2,1)S(1)}, bf16[1,512,640]{2,1,0:T(8,128)(2,1)}, u32[]{:S(2)}) copy-start(bf16[1,512,640]{2,1,0:T(8,128)(2,1)} %param.9) | copy-start | bytes 1966084
  109.3 65.8 %collective-permute-start = (bf16[512,640]{1,0:T(8,128)(2,1)S(1)}, bf16[512,640]{1,0:T(8,128)(2,1)S(1)}, u32[]{:S(2)}, u32[]{:S(2)}) collective-permute-start(bf16[512,640]{1,0:T(8,128)(2,1)S(1)} %bitcast.29), channel_id=1, source_target_pairs={{0,1},{1,0},{2,3},{3,2},{4,5},{5,4},{6,7},{7,6},{8,9},{9,8},{10,11... | collective-permute-start | bytes 1966088 | tf_op jit(solution)/shard_map/ppermute | solution.py:152
  175.1 0.9 copy-start.5
  180.5 48.3 %collective-permute-start.2 = (f32[512,640]{1,0:T(8,128)}, f32[512,640]{1,0:T(8,128)}, u32[]{:S(2)}, u32[]{:S(2)}) collective-permute-start(f32[512,640]{1,0:T(8,128)} %get-tuple-element.45), channel_id=1, source_target_pairs={{0,1},{1,0},{2,3},{3,2},{4,5},{5,4},{6,7},{7,6},{8,9},{9,8},{10,11... | collective-permute-start | bytes 3932168 | tf_op jit(solution)/shard_map/ppermute | solution.py:184
  189.7 32.5 %collective-permute-start.1 = (f32[512,5]{1,0:T(8,128)S(1)}, f32[512,5]{1,0:T(8,128)S(1)}, u32[]{:S(2)}, u32[]{:S(2)}) collective-permute-start(f32[512,5]{1,0:T(8,128)S(1)} %slice.18), channel_id=1, source_target_pairs={{0,1},{1,0},{2,3},{3,2},{4,5},{5,4},{6,7},{7,6},{8,9},{9,8},{10,11... | collective-permute-start | bytes 30728 | tf_op jit(solution)/shard_map/ppermute | solution.py:184
  192.2 34.8 %collective-permute-start.3 = (f32[512,5]{1,0:T(8,128)S(1)}, f32[512,5]{1,0:T(8,128)S(1)}, u32[]{:S(2)}, u32[]{:S(2)}) collective-permute-start(f32[512,5]{1,0:T(8,128)S(1)} %slice.19), channel_id=1, source_target_pairs={{0,1},{1,0},{2,3},{3,2},{4,5},{5,4},{6,7},{7,6},{8,9},{9,8},{10,11... | collective-permute-start | bytes 30728 | tf_op jit(solution)/shard_map/ppermute | solution.py:184
  238.1 2.8 copy-start.4
  240.9 3.0 collective-permute-start.5
  240.9 47.9 %collective-permute-start.4 = (bf16[128,5120]{1,0:T(8,128)(2,1)}, bf16[128,5120]{1,0:T(8,128)(2,1)}, u32[]{:S(2)}, u32[]{:S(2)}) collective-permute-start(bf16[128,5120]{1,0:T(8,128)(2,1)} %get-tuple-element.52), channel_id=1, source_target_pairs={{0,64},{64,0},{1,65},{65,1},{2,66},{66,2},{3,67},{67,3},{4,68},{68... | collective-permute-start | bytes 3932168 | tf_op jit(solution)/shard_map/ppermute | solution.py:228
  245.6 24.4 %collective-permute-start.10 = (bf16[32,5120]{1,0:T(8,128)(2,1)S(1)}, bf16[32,5120]{1,0:T(8,128)(2,1)S(1)}, u32[]{:S(2)}, u32[]{:S(2)}) collective-permute-start(bf16[32,5120]{1,0:T(8,128)(2,1)S(1)} %get-tuple-element.55), channel_id=1, source_target_pairs={{0,140},{4,0},{8,4},{12,8},{128,12},{132,128},{136,132},{140,136},... | collective-permute-start | bytes 983048 | tf_op jit(solution)/shard_map/ppermute | solution.py:218
  245.7 33.5 %collective-permute-start.12 = (bf16[32,5120]{1,0:T(8,128)(2,1)S(1)}, bf16[32,5120]{1,0:T(8,128)(2,1)S(1)}, u32[]{:S(2)}, u32[]{:S(2)}) collective-permute-start(bf16[32,5120]{1,0:T(8,128)(2,1)S(1)} %get-tuple-element.54), channel_id=1, source_target_pairs={{0,140},{4,0},{8,4},{12,8},{128,12},{132,128},{136,132},{140,136},... | collective-permute-start | bytes 983048 | tf_op jit(solution)/shard_map/ppermute | solution.py:218
  253.0 35.3 %collective-permute-start.6 = (bf16[32,5120]{1,0:T(8,128)(2,1)S(1)}, bf16[32,5120]{1,0:T(8,128)(2,1)S(1)}, u32[]{:S(2)}, u32[]{:S(2)}) collective-permute-start(bf16[32,5120]{1,0:T(8,128)(2,1)S(1)} %get-tuple-element.53), channel_id=1, source_target_pairs={{0,4},{4,8},{8,12},{12,128},{128,132},{132,136},{136,140},{140,0},... | collective-permute-start | bytes 983048 | tf_op jit(solution)/shard_map/ppermute | solution.py:218
  261.9 26.4 %collective-permute-start.8 = (bf16[32,5120]{1,0:T(8,128)(2,1)S(1)}, bf16[32,5120]{1,0:T(8,128)(2,1)S(1)}, u32[]{:S(2)}, u32[]{:S(2)}) collective-permute-start(bf16[32,5120]{1,0:T(8,128)(2,1)S(1)} %get-tuple-element.56), channel_id=1, source_target_pairs={{0,4},{4,8},{8,12},{12,128},{128,132},{132,136},{136,140},{140,0},... | collective-permute-start | bytes 983048 | tf_op jit(solution)/shard_map/ppermute | solution.py:218
  270.1 35.0 %collective-permute-start.11 = (bf16[32,5120]{1,0:T(8,128)(2,1)S(1)}, bf16[32,5120]{1,0:T(8,128)(2,1)S(1)}, u32[]{:S(2)}, u32[]{:S(2)}) collective-permute-start(bf16[32,5120]{1,0:T(8,128)(2,1)S(1)} %collective-permute-done.10), channel_id=1, source_target_pairs={{0,132},{4,136},{8,140},{12,0},{128,4},{132,8},{136,12},{140,128},... | collective-permute-start | bytes 983048 | tf_op jit(solution)/shard_map/ppermute | solution.py:218
  279.2 36.4 %collective-permute-start.13 = (bf16[32,5120]{1,0:T(8,128)(2,1)S(1)}, bf16[32,5120]{1,0:T(8,128)(2,1)S(1)}, u32[]{:S(2)}, u32[]{:S(2)}) collective-permute-start(bf16[32,5120]{1,0:T(8,128)(2,1)S(1)} %collective-permute-done.12), channel_id=1, source_target_pairs={{0,132},{4,136},{8,140},{12,0},{128,4},{132,8},{136,12},{140,128},... | collective-permute-start | bytes 983048 | tf_op jit(solution)/shard_map/ppermute | solution.py:218
  288.4 29.1 %collective-permute-start.7 = (bf16[32,5120]{1,0:T(8,128)(2,1)S(1)}, bf16[32,5120]{1,0:T(8,128)(2,1)S(1)}, u32[]{:S(2)}, u32[]{:S(2)}) collective-permute-start(bf16[32,5120]{1,0:T(8,128)(2,1)S(1)} %collective-permute-done.6), channel_id=1, source_target_pairs={{0,12},{4,128},{8,132},{12,136},{128,140},{132,0},{136,4},{140,8},... | collective-permute-start | bytes 983048 | tf_op jit(solution)/shard_map/ppermute | solution.py:218
  288.4 43.9 %collective-permute-start.9 = (bf16[32,5120]{1,0:T(8,128)(2,1)S(1)}, bf16[32,5120]{1,0:T(8,128)(2,1)S(1)}, u32[]{:S(2)}, u32[]{:S(2)}) collective-permute-start(bf16[32,5120]{1,0:T(8,128)(2,1)S(1)} %collective-permute-done.8), channel_id=1, source_target_pairs={{0,12},{4,128},{8,132},{12,136},{128,140},{132,0},{136,4},{140,8},... | collective-permute-start | bytes 983048 | tf_op jit(solution)/shard_map/ppermute | solution.py:218
  332.3 3.5 %copy-start.1 = (bf16[128,8,640]{2,1,0:T(8,128)(2,1)S(1)}, bf16[128,8,640]{2,1,0:T(8,128)(2,1)}, u32[]{:S(2)}) copy-start(bf16[128,8,640]{2,1,0:T(8,128)(2,1)} %param.12) | copy-start | bytes 3932164
Sparse Core Ops, SparseCore 0:
  9.1 100.0 all-gather.2
  111.0 77.1 all-gather.4

commit v10 on v9

--- a/solution.py
+++ b/solution.py
@@ -217,7 +217,7 @@
     def shifted(rows, by):
         return lax.ppermute(rows, z_axes, [(i, (i + by) % ring) for i in range(ring)])
 
-    pieces = 4
+    pieces = 2
     piece_rows = quarter_rows // pieces
     received = []
     for piece in range(pieces):

time: 350 us -> 336 us (0.960)
  the two profiles are of different devices: /device:TPU:24 before, /device:TPU:50 now
where the time goes in v10:
time: 336 us; the launch traced here: 333 us
  waiting for transfers between devices  189 us (56%)
  Pallas kernels  43.1 us (13%)
  starting transfers between devices  35.5 us (11%)
  local copies, waits for them, and re-layouts  25.4 us (8%)
  between operations  15.8 us (5%)
  other arithmetic  14.2 us (4%)
  matrix products  9.36 us (3%)
    all_gather x1, waiting for transfers between devices, local(): weight = lax.all_gather(out_weight, ('zl', 'x'), axis=1, tiled=True)  60.2 us
    ppermute x4, waiting for transfers between devices, shifted(): lax.ppermute(rows, z_axes, [(i, (i + by) % ring) for i in range(ring)])  56.5 us
    all_to_all x1, waiting for transfers between devices, local(): lax.all_to_all(sent, FRAME_AXES, split_axis=2, concat_axis=2, tiled=True)  43.3 us
    pallas_call x4, Pallas kernels, attend(): pl.pallas_call(lambda *refs: attend_kernel(*refs, with_init=with_init, he...  43.1 us
    ppermute x3, waiting for transfers between devices, local(): lax.ppermute((other_max[:, ::HD], other_sum[:, ::HD], other_out), 'x', swap)  26 us
    ppermute x3, starting transfers between devices, local(): lax.ppermute((other_max[:, ::HD], other_sum[:, ::HD], other_out), 'x', swap)  15.7 us
    all_to_all x1, starting transfers between devices, local(): lax.all_to_all(sent, FRAME_AXES, split_axis=2, concat_axis=2, tiled=True)  11.8 us
    dot_general x1, matrix products, local(): jnp.dot(attended, weight, preferred_element_type=jnp.float32)  9.36 us
  transfers between devices with their start and end apart: 13, of which 8 were waited for; matrix products, arithmetic and copies ran while one was open for 10% of the time, Pallas kernels for 13%

profile of v10, /device:TPU:50, one launch (start us, length us, event | category | flops | bytes accessed | tf_op | source)
XLA Modules:
  0.0 332.7 jit_solution(3104593868562192396)
XLA Ops:
  6.5 0.0 all-gather.3.cloned.1.call-start
  6.5 0.7 all-gather.3.cloned.1.call-update
  7.3 1.3 iota_subtract_fusion
  8.6 0.8 select_reduce_fusion.3
  9.4 0.8 copy.31
  10.2 0.1 reshape.292
  10.4 0.3 select_reduce_fusion
  10.7 0.9 select_reduce_fusion.2
  11.6 0.1 reshape.300
  11.7 0.0 copy-start.3
  11.7 2.5 gather_fusion
  14.2 0.0 copy-done.3
  14.2 2.4 gather_fusion.1
  16.6 3.1 pad_maximum_fusion
  19.7 3.2 copy.32
  22.9 11.8 %all-to-all-start = ((bf16[2,4,64,8,640]{4,3,1,0,2:T(8,128)(2,1)}), bf16[2,4,64,8,640]{4,3,1,0,2:T(8,128)(2,1)}, u32[]{:S(2)}, u32[]{:S(2)}) async-start(bf16[2,4,64,8,640]{4,3,1,0,2:T(8,128)(2,1)} %copy.32), calls=%async_computation | async-start | bytes 10485760 | tf_op jit(solution)/shard_map/all_to_all | solution.py:148
  34.7 0.0 all-gather.5.cloned.1.call-start
  34.8 1.2 maximum_bitcast_fusion.refs_3_.refs_4_
  36.0 9.5 %shard_map.92 = (f32[512,640]{1,0:T(8,128)}, f32[512,640]{1,0:T(8,128)}, f32[512,640]{1,0:T(8,128)}) custom-call(s32[1]{0:T(128)} %constant.86.clone.1.refs_0_, s32[1]{0:T(128)} %constant.87.clone.1.refs_1_, bf16[512,640]{1,0:T(8,128)(2,1)} %bitcast.26, bf16[2,1,512,640]{3,2,1,0:T(8,128)(2,1)} %maximum_bitcast_fusion.refs_3_.refs_4_, ...), custom_call_target="tpu_custom_call" | custom-call | flops 671088640 | bytes 9175040 | tf_op jit(solution)/shard_map/pallas_call | solution.py:80
  45.5 60.2 %all-gather.3.cloned.1.call-done = bf16[640,1280]{0,1:T(8,128)(2,1)} async-done(((bf16[640,80]{0,1:T(8,128)(2,1)}), bf16[640,1280]{0,1:T(8,128)(2,1)}) %all-gather.3.cloned.1.call-update) | async-done | bytes 1638416 | tf_op jit(solution)/shard_map/all_gather | solution.py:144
  105.7 0.0 all-gather.5.cloned.1.call-update
  105.7 0.3 collective-permute-start
  108.2 0.5 broadcast_select_fusion.refs_0_
  108.8 0.5 broadcast_select_fusion.1.refs_0_
  109.3 43.3 %all-to-all-done = bf16[2,4,64,8,640]{4,3,1,0,2:T(8,128)(2,1)} async-done(((bf16[2,4,64,8,640]{4,3,1,0,2:T(8,128)(2,1)}), bf16[2,4,64,8,640]{4,3,1,0,2:T(8,128)(2,1)}, u32[]{:S(2)}, u32[]{:S(2)}) %all-to-all-start) | async-done | bytes 5242912 | tf_op jit(solution)/shard_map/all_to_all | solution.py:148
  152.6 5.3 %copy.40 = bf16[2,4,64,8,640]{4,3,2,1,0:T(8,128)(2,1)} copy(bf16[2,4,64,8,640]{4,3,1,0,2:T(8,128)(2,1)} %all-to-all-done) | data formatting | bytes 10485760 | tf_op jit(solution)/shard_map/all_to_all | solution.py:148
  157.9 23.2 %shard_map.93 = (f32[512,640]{1,0:T(8,128)}, f32[512,640]{1,0:T(8,128)}, f32[512,640]{1,0:T(8,128)}) custom-call(s32[4]{0:T(128)} %broadcast_select_fusion.refs_0_, s32[1]{0:T(128)} %bitcast.7.refs_1_, bf16[512,640]{1,0:T(8,128)(2,1)} %bitcast.27, bf16[2,4,512,640]{3,2,1,0:T(8,128)(2,1)} %bitcast.18, bf16[2,4,512,640]{3,2,1,0:T(8,128)(2,1)} %bitcast.19, ...), custom_call_target="tpu_custom_call" | custom-call | flops 2684354560 | bytes 13107200 | tf_op jit(solution)/shard_map/pallas_call | solution.py:80
  181.1 0.0 collective-permute-done.refs_2_
  181.1 0.9 copy-done.5
  182.0 4.6 %shard_map.91 = (f32[512,640]{1,0:T(8,128)}, f32[512,640]{1,0:T(8,128)}, f32[512,640]{1,0:T(8,128)}) custom-call(s32[4]{0:T(128)} %broadcast_select_fusion.1.refs_0_, s32[1]{0:T(128)} %bitcast.6.refs_1_, bf16[512,640]{1,0:T(8,128)(2,1)} %copy-done.5, bf16[2,4,512,640]{3,2,1,0:T(8,128)(2,1)} %bitcast.20, bf16[2,4,512,640]{3,2,1,0:T(8,128)(2,1)} %bitcast.21), custom_call_target="tpu_custom_call" | custom-call | flops 2684354560 | bytes 13107200 | tf_op jit(solution)/shard_map/pallas_call | solution.py:80
  186.5 13.3 %collective-permute-start.2 = (f32[512,640]{1,0:T(8,128)}, f32[512,640]{1,0:T(8,128)}, u32[]{:S(2)}, u32[]{:S(2)}) collective-permute-start(f32[512,640]{1,0:T(8,128)} %get-tuple-element.45), channel_id=1, source_target_pairs={{0,1},{1,0},{2,3},{3,2},{4,5},{5,4},{6,7},{7,6},{8,9},{9,8},{10,11... | collective-permute-start | bytes 3932168 | tf_op jit(solution)/shard_map/ppermute | solution.py:184
  199.8 0.5 broadcast_select_fusion.2.refs_0_
  200.3 2.4 slice.12
  202.7 0.1 collective-permute-start.1
  202.8 2.4 slice.13
  205.3 2.3 collective-permute-start.3
  207.6 5.8 %shard_map.94 = (f32[512,640]{1,0:T(8,128)}, f32[512,640]{1,0:T(8,128)}, f32[512,640]{1,0:T(8,128)}) custom-call(s32[4]{0:T(128)} %broadcast_select_fusion.2.refs_0_, s32[1]{0:T(128)} %bitcast.refs_1_, bf16[512,640]{1,0:T(8,128)(2,1)} %bitcast.28, bf16[2,4,512,640]{3,2,1,0:T(8,128)(2,1)} %bitcast.22, bf16[2,4,512,640]{3,2,1,0:T(8,128)(2,1)} %bitcast.23, ...), custom_call_target="tpu_custom_call" | custom-call | flops 2684354560 | bytes 13107200 | tf_op jit(solution)/shard_map/pallas_call | solution.py:80
  213.4 21.8 %collective-permute-done.1 = f32[512,5]{1,0:T(8,128)S(1)} collective-permute-done((f32[512,5]{1,0:T(8,128)S(1)}, f32[512,5]{1,0:T(8,128)S(1)}, u32[]{:S(2)}, u32[]{:S(2)}) %collective-permute-start.1) | collective-permute-done | bytes 10272 | tf_op jit(solution)/shard_map/ppermute | solution.py:184
  235.3 0.1 copy.34
  235.4 0.2 broadcast_in_dim.66
  235.5 0.4 copy.35
  236.0 4.2 %collective-permute-done.3 = f32[512,5]{1,0:T(8,128)S(1)} collective-permute-done((f32[512,5]{1,0:T(8,128)S(1)}, f32[512,5]{1,0:T(8,128)S(1)}, u32[]{:S(2)}, u32[]{:S(2)}) %collective-permute-start.3) | collective-permute-done | bytes 10272 | tf_op jit(solution)/shard_map/ppermute | solution.py:184
  240.2 0.1 copy.37
  240.3 0.2 broadcast_in_dim.67
  240.4 1.5 copy.38
  241.9 0.0 collective-permute-done.2
  241.9 9.4 %convolution_convert_fusion = bf16[512,5120]{1,0:T(8,128)(2,1)S(1)} fusion(bf16[640,5120]{0,1:T(8,128)(2,1)} %all-gather.5.cloned.1.call-done, f32[512,640]{1,0:T(8,128)} %copy.38, f32[512,640]{1,0:T(8,128)} %get-tuple-element.46, f32[512,640]{1,0:T(8,128)} %collective-permute-done.2, f32[512,640]{1,0:T(8,128)S(1)} %copy.35, ...), kind=kOutput, calls=%fused_computation.2 | convolution fusion | flops 3361669120 | bytes 19660800 | tf_op jit(solution)/shard_map/dot_general | solution.py:198
  251.3 1.4 constant_dynamic-slice_fusion.1
  252.7 1.3 copy-done.4
  254.0 0.0 collective-permute-start.5
  254.0 0.5 collective-permute-start.4
  254.5 2.5 collective-permute-done.5
  257.0 1.6 add_convert_fusion.1
  258.7 0.1 fusion.6
  258.8 0.1 collective-permute-start.6
  258.9 2.0 collective-permute-start.8
  260.9 14.7 %collective-permute-done.6 = bf16[64,5120]{1,0:T(8,128)(2,1)S(1)} collective-permute-done((bf16[64,5120]{1,0:T(8,128)(2,1)S(1)}, bf16[64,5120]{1,0:T(8,128)(2,1)S(1)}, u32[]{:S(2)}, u32[]{:S(2)}) %collective-permute-start.6) | collective-permute-done | bytes 655392 | tf_op jit(solution)/shard_map/ppermute | solution.py:218
  275.6 1.8 collective-permute-start.7
  277.5 0.0 collective-permute-done.8
  277.5 3.2 collective-permute-start.9
  280.7 0.0 collective-permute-done.4
  280.7 38.3 %collective-permute-done.7 = bf16[64,5120]{1,0:T(8,128)(2,1)S(1)} collective-permute-done((bf16[64,5120]{1,0:T(8,128)(2,1)S(1)}, bf16[64,5120]{1,0:T(8,128)(2,1)S(1)}, u32[]{:S(2)}, u32[]{:S(2)}) %collective-permute-start.7) | collective-permute-done | bytes 655392 | tf_op jit(solution)/shard_map/ppermute | solution.py:218
  319.0 3.4 %collective-permute-done.9 = bf16[64,5120]{1,0:T(8,128)(2,1)S(1)} collective-permute-done((bf16[64,5120]{1,0:T(8,128)(2,1)S(1)}, bf16[64,5120]{1,0:T(8,128)(2,1)S(1)}, u32[]{:S(2)}, u32[]{:S(2)}) %collective-permute-start.9) | collective-permute-done | bytes 655392 | tf_op jit(solution)/shard_map/ppermute | solution.py:218
  322.4 3.5 %fusion.2 = bf16[1,128,5120]{2,1,0:T(8,128)(2,1)} fusion(bf16[128,5120]{1,0:T(8,128)(2,1)} %collective-permute-done.4, bf16[64,5120]{1,0:T(8,128)(2,1)S(1)} %collective-permute-done.9, bf16[64,5120]{1,0:T(8,128)(2,1)S(1)} %collective-permute-done.7, bf16[512,5120]{1,0:T(8,128)(2,1)} %copy-done.4, s32[]{:T(128)S(6)} %select_n.143), kind=kLoop, calls=%fused_computation.11 | loop fusion | flops 5898240 | bytes 5242884 | tf_op jit(solution)/shard_map/broadcast_in_dim | solution.py:232
  (19 shorter events, 0.1 us)
Async XLA Ops:
  6.5 5.2 %copy-start = (bf16[128,8,640]{2,1,0:T(8,128)(2,1)S(1)}, bf16[128,8,640]{2,1,0:T(8,128)(2,1)}, u32[]{:S(2)}) copy-start(bf16[128,8,640]{2,1,0:T(8,128)(2,1)} %param.12) | copy-start | bytes 3932164
  6.5 99.2 %all-gather.3.cloned.1.call-start = ((), (), s32[]{:S(2)}) async-start(), calls=%async_computation.1 | async-start | bytes 1740800 | tf_op jit(solution)/shard_map/all_gather | solution.py:144
  11.7 2.5 copy-start.3
  22.9 11.9 %copy-start.6 = (bf16[1,512,640]{2,1,0:T(8,128)(2,1)S(1)}, bf16[1,512,640]{2,1,0:T(8,128)(2,1)}, u32[]{:S(2)}) copy-start(bf16[1,512,640]{2,1,0:T(8,128)(2,1)} %param.11) | copy-start | bytes 1966084
  22.9 11.9 %copy-start.7 = (bf16[1,512,640]{2,1,0:T(8,128)(2,1)S(1)}, bf16[1,512,640]{2,1,0:T(8,128)(2,1)}, u32[]{:S(2)}) copy-start(bf16[1,512,640]{2,1,0:T(8,128)(2,1)} %param.10) | copy-start | bytes 1966084
  22.9 129.7 %all-to-all-start = ((bf16[2,4,64,8,640]{4,3,1,0,2:T(8,128)(2,1)}), bf16[2,4,64,8,640]{4,3,1,0,2:T(8,128)(2,1)}, u32[]{:S(2)}, u32[]{:S(2)}) async-start(bf16[2,4,64,8,640]{4,3,1,0,2:T(8,128)(2,1)} %copy.32), calls=%async_computation | async-start | bytes 10485760 | tf_op jit(solution)/shard_map/all_to_all | solution.py:148
  34.7 207.2 %all-gather.5.cloned.1.call-start = ((), (), s32[]{:S(2)}) async-start(), calls=%async_computation.2 | async-start | bytes 8192000 | tf_op jit(solution)/shard_map/all_gather | solution.py:169
  45.5 60.2 %copy-start.2 = (bf16[1,512,640]{2,1,0:T(8,128)(2,1)S(1)}, bf16[1,512,640]{2,1,0:T(8,128)(2,1)}, u32[]{:S(2)}) copy-start(bf16[1,512,640]{2,1,0:T(8,128)(2,1)} %param.9) | copy-start | bytes 1966084
  105.7 75.4 %collective-permute-start = (bf16[512,640]{1,0:T(8,128)(2,1)S(1)}, bf16[512,640]{1,0:T(8,128)(2,1)S(1)}, u32[]{:S(2)}, u32[]{:S(2)}) collective-permute-start(bf16[512,640]{1,0:T(8,128)(2,1)S(1)} %bitcast.29), channel_id=1, source_target_pairs={{0,1},{1,0},{2,3},{3,2},{4,5},{5,4},{6,7},{7,6},{8,9},{9,8},{10,11... | collective-permute-start | bytes 1966088 | tf_op jit(solution)/shard_map/ppermute | solution.py:152
  181.1 0.9 copy-start.5
  186.5 55.4 %collective-permute-start.2 = (f32[512,640]{1,0:T(8,128)}, f32[512,640]{1,0:T(8,128)}, u32[]{:S(2)}, u32[]{:S(2)}) collective-permute-start(f32[512,640]{1,0:T(8,128)} %get-tuple-element.45), channel_id=1, source_target_pairs={{0,1},{1,0},{2,3},{3,2},{4,5},{5,4},{6,7},{7,6},{8,9},{9,8},{10,11... | collective-permute-start | bytes 3932168 | tf_op jit(solution)/shard_map/ppermute | solution.py:184
  202.7 32.5 %collective-permute-start.1 = (f32[512,5]{1,0:T(8,128)S(1)}, f32[512,5]{1,0:T(8,128)S(1)}, u32[]{:S(2)}, u32[]{:S(2)}) collective-permute-start(f32[512,5]{1,0:T(8,128)S(1)} %slice.12), channel_id=1, source_target_pairs={{0,1},{1,0},{2,3},{3,2},{4,5},{5,4},{6,7},{7,6},{8,9},{9,8},{10,11... | collective-permute-start | bytes 30728 | tf_op jit(solution)/shard_map/ppermute | solution.py:184
  205.3 34.9 %collective-permute-start.3 = (f32[512,5]{1,0:T(8,128)S(1)}, f32[512,5]{1,0:T(8,128)S(1)}, u32[]{:S(2)}, u32[]{:S(2)}) collective-permute-start(f32[512,5]{1,0:T(8,128)S(1)} %slice.13), channel_id=1, source_target_pairs={{0,1},{1,0},{2,3},{3,2},{4,5},{5,4},{6,7},{7,6},{8,9},{9,8},{10,11... | collective-permute-start | bytes 30728 | tf_op jit(solution)/shard_map/ppermute | solution.py:184
  251.3 2.7 copy-start.4
  254.0 3.0 collective-permute-start.5
  254.0 26.7 %collective-permute-start.4 = (bf16[128,5120]{1,0:T(8,128)(2,1)}, bf16[128,5120]{1,0:T(8,128)(2,1)}, u32[]{:S(2)}, u32[]{:S(2)}) collective-permute-start(bf16[128,5120]{1,0:T(8,128)(2,1)} %get-tuple-element.52), channel_id=1, source_target_pairs={{0,64},{64,0},{1,65},{65,1},{2,66},{66,2},{3,67},{67,3},{4,68},{68... | collective-permute-start | bytes 3932168 | tf_op jit(solution)/shard_map/ppermute | solution.py:228
  258.8 16.9 %collective-permute-start.6 = (bf16[64,5120]{1,0:T(8,128)(2,1)S(1)}, bf16[64,5120]{1,0:T(8,128)(2,1)S(1)}, u32[]{:S(2)}, u32[]{:S(2)}) collective-permute-start(bf16[64,5120]{1,0:T(8,128)(2,1)S(1)} %get-tuple-element.53), channel_id=1, source_target_pairs={{0,4},{4,8},{8,12},{12,128},{128,132},{132,136},{136,140},{140,0},... | collective-permute-start | bytes 1966088 | tf_op jit(solution)/shard_map/ppermute | solution.py:218
  258.9 18.6 %collective-permute-start.8 = (bf16[64,5120]{1,0:T(8,128)(2,1)S(1)}, bf16[64,5120]{1,0:T(8,128)(2,1)S(1)}, u32[]{:S(2)}, u32[]{:S(2)}) collective-permute-start(bf16[64,5120]{1,0:T(8,128)(2,1)S(1)} %get-tuple-element.54), channel_id=1, source_target_pairs={{0,140},{4,0},{8,4},{12,8},{128,12},{132,128},{136,132},{140,136},... | collective-permute-start | bytes 1966088 | tf_op jit(solution)/shard_map/ppermute | solution.py:218
  275.6 43.4 %collective-permute-start.7 = (bf16[64,5120]{1,0:T(8,128)(2,1)S(1)}, bf16[64,5120]{1,0:T(8,128)(2,1)S(1)}, u32[]{:S(2)}, u32[]{:S(2)}) collective-permute-start(bf16[64,5120]{1,0:T(8,128)(2,1)S(1)} %collective-permute-done.6), channel_id=1, source_target_pairs={{0,12},{4,128},{8,132},{12,136},{128,140},{132,0},{136,4},{140,8},... | collective-permute-start | bytes 1966088 | tf_op jit(solution)/shard_map/ppermute | solution.py:218
  277.5 45.0 %collective-permute-start.9 = (bf16[64,5120]{1,0:T(8,128)(2,1)S(1)}, bf16[64,5120]{1,0:T(8,128)(2,1)S(1)}, u32[]{:S(2)}, u32[]{:S(2)}) collective-permute-start(bf16[64,5120]{1,0:T(8,128)(2,1)S(1)} %collective-permute-done.8), channel_id=1, source_target_pairs={{0,132},{4,136},{8,140},{12,0},{128,4},{132,8},{136,12},{140,128},... | collective-permute-start | bytes 1966088 | tf_op jit(solution)/shard_map/ppermute | solution.py:218
  322.4 3.5 %copy-start.1 = (bf16[128,8,640]{2,1,0:T(8,128)(2,1)S(1)}, bf16[128,8,640]{2,1,0:T(8,128)(2,1)}, u32[]{:S(2)}) copy-start(bf16[128,8,640]{2,1,0:T(8,128)(2,1)} %param.12) | copy-start | bytes 3932164
Sparse Core Ops, SparseCore 0:
  9.1 96.5 all-gather.2
  107.5 88.2 all-gather.4

commit v11 on v10

--- a/solution.py
+++ b/solution.py
@@ -39,13 +39,13 @@
 
     @pl.when(step < count_ref[0])
     def _slot():
-        for head in range(heads):
-            cols = pl.ds(head * HD, HD)
+        def one_head(head, carry):
+            cols = pl.ds(pl.multiple_of(head * HD, HD), HD)
             scores = lax.dot_general(
                 q_ref[:, cols], k_ref[0, 0, :, cols], (((1,), (1,)), ((), ())),
                 preferred_element_type=jnp.float32,
             ) * (1.0 / math.sqrt(HD))
-            running_max = m_ref[:, pl.ds(head * HD, 1)]
+            running_max = m_ref[:, cols][:, :1]
             new_max = jnp.maximum(running_max, jnp.max(scores, axis=1, keepdims=True))
             shrink = jnp.exp(running_max - new_max)
             weights = jnp.exp(scores - new_max)
@@ -55,6 +55,9 @@
                 preferred_element_type=jnp.float32,
             )
             m_ref[:, cols] = jnp.broadcast_to(new_max, (new_max.shape[0], HD))
+            return carry
+
+        lax.fori_loop(0, heads, one_head, 0)
 
 
 def attend(queries, arrived, order, count, init=None):

time: 336 us -> 336 us (level)
  starting transfers between devices: 35.5 us -> 39.9 us
  waiting for transfers between devices: 189 us -> 185 us
    ppermute x3, waiting for transfers between devices: 26 us -> 20.1 us  [local(): lax.ppermute((other_max[:, ::HD], other_sum[:, ::HD], other_out), 'x', swap)]
    ppermute x4, starting transfers between devices: 7.13 us -> 11.8 us  [shifted(): lax.ppermute(rows, z_axes, [(i, (i + by) % ring) for i in range(ring)])]
where the time goes in v11:
time: 336 us; the launch traced here: 334 us
  waiting for transfers between devices  185 us (55%)
  Pallas kernels  43.9 us (13%)
  starting transfers between devices  39.9 us (12%)
  local copies, waits for them, and re-layouts  25.4 us (8%)
  between operations  15.8 us (5%)
  other arithmetic  14.2 us (4%)
  matrix products  9.36 us (3%)
    all_gather x1, waiting for transfers between devices, local(): weight = lax.all_gather(out_weight, ('zl', 'x'), axis=1, tiled=True)  60 us
    ppermute x4, waiting for transfers between devices, shifted(): lax.ppermute(rows, z_axes, [(i, (i + by) % ring) for i in range(ring)])  58 us
    pallas_call x4, Pallas kernels, attend(): pl.pallas_call(lambda *refs: attend_kernel(*refs, with_init=with_init, he...  43.9 us
    all_to_all x1, waiting for transfers between devices, local(): lax.all_to_all(sent, FRAME_AXES, split_axis=2, concat_axis=2, tiled=True)  43.5 us
    ppermute x3, waiting for transfers between devices, local(): lax.ppermute((other_max[:, ::HD], other_sum[:, ::HD], other_out), 'x', swap)  20.1 us
    ppermute x3, starting transfers between devices, local(): lax.ppermute((other_max[:, ::HD], other_sum[:, ::HD], other_out), 'x', swap)  15.6 us
    all_to_all x1, starting transfers between devices, local(): lax.all_to_all(sent, FRAME_AXES, split_axis=2, concat_axis=2, tiled=True)  11.8 us
    ppermute x4, starting transfers between devices, shifted(): lax.ppermute(rows, z_axes, [(i, (i + by) % ring) for i in range(ring)])  11.8 us
  transfers between devices with their start and end apart: 13, of which 8 were waited for; matrix products, arithmetic and copies ran while one was open for 10% of the time, Pallas kernels for 13%

profile of v11, /device:TPU:50, one launch (start us, length us, event | category | flops | bytes accessed | tf_op | source)
XLA Modules:
  0.0 333.5 jit_solution(10900604016929703569)
XLA Ops:
  6.5 0.7 all-gather.3.cloned.1.call-update
  7.3 1.3 iota_subtract_fusion
  8.6 0.8 select_reduce_fusion.3
  9.4 0.8 copy.31
  10.2 0.1 reshape.292
  10.4 0.3 select_reduce_fusion
  10.7 0.9 select_reduce_fusion.2
  11.6 0.1 reshape.300
  11.7 0.0 copy-start.3
  11.7 2.5 gather_fusion
  14.2 0.0 copy-done.3
  14.2 2.4 gather_fusion.1
  16.6 3.1 pad_maximum_fusion
  19.7 3.2 copy.32
  22.9 11.8 %all-to-all-start = ((bf16[2,4,64,8,640]{4,3,1,0,2:T(8,128)(2,1)}), bf16[2,4,64,8,640]{4,3,1,0,2:T(8,128)(2,1)}, u32[]{:S(2)}, u32[]{:S(2)}) async-start(bf16[2,4,64,8,640]{4,3,1,0,2:T(8,128)(2,1)} %copy.32), calls=%async_computation | async-start | bytes 10485760 | tf_op jit(solution)/shard_map/all_to_all | solution.py:151
  34.7 0.0 all-gather.5.cloned.1.call-start
  34.8 1.2 maximum_bitcast_fusion.refs_3_.refs_4_
  36.0 9.7 %shard_map.92 = (f32[512,640]{1,0:T(8,128)}, f32[512,640]{1,0:T(8,128)}, f32[512,640]{1,0:T(8,128)}) custom-call(s32[1]{0:T(128)} %constant.86.clone.1.refs_0_, s32[1]{0:T(128)} %constant.87.clone.1.refs_1_, bf16[512,640]{1,0:T(8,128)(2,1)} %bitcast.26, bf16[2,1,512,640]{3,2,1,0:T(8,128)(2,1)} %maximum_bitcast_fusion.refs_3_.refs_4_, ...), custom_call_target="tpu_custom_call" | custom-call | flops 671088640 | bytes 9175040 | tf_op jit(solution)/shard_map/pallas_call | solution.py:83
  45.7 60.0 %all-gather.3.cloned.1.call-done = bf16[640,1280]{0,1:T(8,128)(2,1)} async-done(((bf16[640,80]{0,1:T(8,128)(2,1)}), bf16[640,1280]{0,1:T(8,128)(2,1)}) %all-gather.3.cloned.1.call-update) | async-done | bytes 1638416 | tf_op jit(solution)/shard_map/all_gather | solution.py:147
  105.7 0.0 all-gather.5.cloned.1.call-update
  105.8 0.1 collective-permute-start
  108.1 0.5 broadcast_select_fusion.refs_0_
  108.6 0.5 broadcast_select_fusion.1.refs_0_
  109.1 43.5 %all-to-all-done = bf16[2,4,64,8,640]{4,3,1,0,2:T(8,128)(2,1)} async-done(((bf16[2,4,64,8,640]{4,3,1,0,2:T(8,128)(2,1)}), bf16[2,4,64,8,640]{4,3,1,0,2:T(8,128)(2,1)}, u32[]{:S(2)}, u32[]{:S(2)}) %all-to-all-start) | async-done | bytes 5242912 | tf_op jit(solution)/shard_map/all_to_all | solution.py:151
  152.6 5.3 %copy.40 = bf16[2,4,64,8,640]{4,3,2,1,0:T(8,128)(2,1)} copy(bf16[2,4,64,8,640]{4,3,1,0,2:T(8,128)(2,1)} %all-to-all-done) | data formatting | bytes 10485760 | tf_op jit(solution)/shard_map/all_to_all | solution.py:151
  157.9 5.8 %shard_map.93 = (f32[512,640]{1,0:T(8,128)}, f32[512,640]{1,0:T(8,128)}, f32[512,640]{1,0:T(8,128)}) custom-call(s32[4]{0:T(128)} %broadcast_select_fusion.refs_0_, s32[1]{0:T(128)} %bitcast.7.refs_1_, bf16[512,640]{1,0:T(8,128)(2,1)} %bitcast.27, bf16[2,4,512,640]{3,2,1,0:T(8,128)(2,1)} %bitcast.18, bf16[2,4,512,640]{3,2,1,0:T(8,128)(2,1)} %bitcast.19, ...), custom_call_target="tpu_custom_call" | custom-call | flops 2684354560 | bytes 13107200 | tf_op jit(solution)/shard_map/pallas_call | solution.py:83
  163.8 0.0 collective-permute-done.refs_2_
  163.8 0.9 copy-done.5
  164.6 16.6 %shard_map.91 = (f32[512,640]{1,0:T(8,128)}, f32[512,640]{1,0:T(8,128)}, f32[512,640]{1,0:T(8,128)}) custom-call(s32[4]{0:T(128)} %broadcast_select_fusion.1.refs_0_, s32[1]{0:T(128)} %bitcast.6.refs_1_, bf16[512,640]{1,0:T(8,128)(2,1)} %copy-done.5, bf16[2,4,512,640]{3,2,1,0:T(8,128)(2,1)} %bitcast.20, bf16[2,4,512,640]{3,2,1,0:T(8,128)(2,1)} %bitcast.21), custom_call_target="tpu_custom_call" | custom-call | flops 2684354560 | bytes 13107200 | tf_op jit(solution)/shard_map/pallas_call | solution.py:83
  181.2 13.2 %collective-permute-start.2 = (f32[512,640]{1,0:T(8,128)}, f32[512,640]{1,0:T(8,128)}, u32[]{:S(2)}, u32[]{:S(2)}) collective-permute-start(f32[512,640]{1,0:T(8,128)} %get-tuple-element.45), channel_id=1, source_target_pairs={{0,1},{1,0},{2,3},{3,2},{4,5},{5,4},{6,7},{7,6},{8,9},{9,8},{10,11... | collective-permute-start | bytes 3932168 | tf_op jit(solution)/shard_map/ppermute | solution.py:187
  194.4 0.5 broadcast_select_fusion.2.refs_0_
  194.9 2.4 slice.12
  197.3 0.1 collective-permute-start.1
  197.4 2.4 slice.13
  199.9 2.3 collective-permute-start.3
  202.2 11.8 %shard_map.94 = (f32[512,640]{1,0:T(8,128)}, f32[512,640]{1,0:T(8,128)}, f32[512,640]{1,0:T(8,128)}) custom-call(s32[4]{0:T(128)} %broadcast_select_fusion.2.refs_0_, s32[1]{0:T(128)} %bitcast.refs_1_, bf16[512,640]{1,0:T(8,128)(2,1)} %bitcast.28, bf16[2,4,512,640]{3,2,1,0:T(8,128)(2,1)} %bitcast.22, bf16[2,4,512,640]{3,2,1,0:T(8,128)(2,1)} %bitcast.23, ...), custom_call_target="tpu_custom_call" | custom-call | flops 2684354560 | bytes 13107200 | tf_op jit(solution)/shard_map/pallas_call | solution.py:83
  214.0 15.9 %collective-permute-done.1 = f32[512,5]{1,0:T(8,128)S(1)} collective-permute-done((f32[512,5]{1,0:T(8,128)S(1)}, f32[512,5]{1,0:T(8,128)S(1)}, u32[]{:S(2)}, u32[]{:S(2)}) %collective-permute-start.1) | collective-permute-done | bytes 10272 | tf_op jit(solution)/shard_map/ppermute | solution.py:187
  229.9 0.1 copy.34
  230.0 0.2 broadcast_in_dim.66
  230.1 0.4 copy.35
  230.5 4.2 %collective-permute-done.3 = f32[512,5]{1,0:T(8,128)S(1)} collective-permute-done((f32[512,5]{1,0:T(8,128)S(1)}, f32[512,5]{1,0:T(8,128)S(1)}, u32[]{:S(2)}, u32[]{:S(2)}) %collective-permute-start.3) | collective-permute-done | bytes 10272 | tf_op jit(solution)/shard_map/ppermute | solution.py:187
  234.8 0.1 copy.37
  234.9 0.2 broadcast_in_dim.67
  235.0 1.5 copy.38
  236.5 0.0 collective-permute-done.2
  236.5 9.4 %convolution_convert_fusion = bf16[512,5120]{1,0:T(8,128)(2,1)S(1)} fusion(bf16[640,5120]{0,1:T(8,128)(2,1)} %all-gather.5.cloned.1.call-done, f32[512,640]{1,0:T(8,128)} %copy.38, f32[512,640]{1,0:T(8,128)} %get-tuple-element.46, f32[512,640]{1,0:T(8,128)} %collective-permute-done.2, f32[512,640]{1,0:T(8,128)S(1)} %copy.35, ...), kind=kOutput, calls=%fused_computation.2 | convolution fusion | flops 3361669120 | bytes 19660800 | tf_op jit(solution)/shard_map/dot_general | solution.py:201
  245.9 0.0 copy-start.4
  245.9 1.4 constant_dynamic-slice_fusion.1
  247.3 1.3 copy-done.4
  248.6 0.0 collective-permute-start.5
  248.6 0.5 collective-permute-start.4
  249.1 2.5 collective-permute-done.5
  251.6 1.6 add_convert_fusion.1
  253.3 0.1 fusion.6
  253.4 0.1 collective-permute-start.6
  253.5 2.0 collective-permute-start.8
  255.5 14.7 %collective-permute-done.6 = bf16[64,5120]{1,0:T(8,128)(2,1)S(1)} collective-permute-done((bf16[64,5120]{1,0:T(8,128)(2,1)S(1)}, bf16[64,5120]{1,0:T(8,128)(2,1)S(1)}, u32[]{:S(2)}, u32[]{:S(2)}) %collective-permute-start.6) | collective-permute-done | bytes 655392 | tf_op jit(solution)/shard_map/ppermute | solution.py:221
  270.2 7.8 %collective-permute-start.7 = (bf16[64,5120]{1,0:T(8,128)(2,1)S(1)}, bf16[64,5120]{1,0:T(8,128)(2,1)S(1)}, u32[]{:S(2)}, u32[]{:S(2)}) collective-permute-start(bf16[64,5120]{1,0:T(8,128)(2,1)S(1)} %collective-permute-done.6), channel_id=1, source_target_pairs={{0,12},{4,128},{8,132},{12,136},{128,140},{132,0},{136,4},{140,8},... | collective-permute-start | bytes 1966088 | tf_op jit(solution)/shard_map/ppermute | solution.py:221
  278.0 0.0 collective-permute-done.8
  278.0 1.9 collective-permute-start.9
  279.9 0.0 collective-permute-done.4
  279.9 39.9 %collective-permute-done.7 = bf16[64,5120]{1,0:T(8,128)(2,1)S(1)} collective-permute-done((bf16[64,5120]{1,0:T(8,128)(2,1)S(1)}, bf16[64,5120]{1,0:T(8,128)(2,1)S(1)}, u32[]{:S(2)}, u32[]{:S(2)}) %collective-permute-start.7) | collective-permute-done | bytes 655392 | tf_op jit(solution)/shard_map/ppermute | solution.py:221
  319.8 3.4 %collective-permute-done.9 = bf16[64,5120]{1,0:T(8,128)(2,1)S(1)} collective-permute-done((bf16[64,5120]{1,0:T(8,128)(2,1)S(1)}, bf16[64,5120]{1,0:T(8,128)(2,1)S(1)}, u32[]{:S(2)}, u32[]{:S(2)}) %collective-permute-start.9) | collective-permute-done | bytes 655392 | tf_op jit(solution)/shard_map/ppermute | solution.py:221
  323.2 3.5 %fusion.2 = bf16[1,128,5120]{2,1,0:T(8,128)(2,1)} fusion(bf16[128,5120]{1,0:T(8,128)(2,1)} %collective-permute-done.4, bf16[64,5120]{1,0:T(8,128)(2,1)S(1)} %collective-permute-done.9, bf16[64,5120]{1,0:T(8,128)(2,1)S(1)} %collective-permute-done.7, bf16[512,5120]{1,0:T(8,128)(2,1)} %copy-done.4, s32[]{:T(128)S(6)} %select_n.143), kind=kLoop, calls=%fused_computation.11 | loop fusion | flops 5898240 | bytes 5242884 | tf_op jit(solution)/shard_map/broadcast_in_dim | solution.py:235
  (19 shorter events, 0.1 us)
Async XLA Ops:
  6.5 5.2 %copy-start = (bf16[128,8,640]{2,1,0:T(8,128)(2,1)S(1)}, bf16[128,8,640]{2,1,0:T(8,128)(2,1)}, u32[]{:S(2)}) copy-start(bf16[128,8,640]{2,1,0:T(8,128)(2,1)} %param.12) | copy-start | bytes 3932164
  6.5 99.2 %all-gather.3.cloned.1.call-start = ((), (), s32[]{:S(2)}) async-start(), calls=%async_computation.1 | async-start | bytes 1740800 | tf_op jit(solution)/shard_map/all_gather | solution.py:147
  11.7 2.5 copy-start.3
  22.9 11.9 %copy-start.6 = (bf16[1,512,640]{2,1,0:T(8,128)(2,1)S(1)}, bf16[1,512,640]{2,1,0:T(8,128)(2,1)}, u32[]{:S(2)}) copy-start(bf16[1,512,640]{2,1,0:T(8,128)(2,1)} %param.11) | copy-start | bytes 1966084
  22.9 11.9 %copy-start.7 = (bf16[1,512,640]{2,1,0:T(8,128)(2,1)S(1)}, bf16[1,512,640]{2,1,0:T(8,128)(2,1)}, u32[]{:S(2)}) copy-start(bf16[1,512,640]{2,1,0:T(8,128)(2,1)} %param.10) | copy-start | bytes 1966084
  22.9 129.7 %all-to-all-start = ((bf16[2,4,64,8,640]{4,3,1,0,2:T(8,128)(2,1)}), bf16[2,4,64,8,640]{4,3,1,0,2:T(8,128)(2,1)}, u32[]{:S(2)}, u32[]{:S(2)}) async-start(bf16[2,4,64,8,640]{4,3,1,0,2:T(8,128)(2,1)} %copy.32), calls=%async_computation | async-start | bytes 10485760 | tf_op jit(solution)/shard_map/all_to_all | solution.py:151
  34.7 201.8 %all-gather.5.cloned.1.call-start = ((), (), s32[]{:S(2)}) async-start(), calls=%async_computation.2 | async-start | bytes 8192000 | tf_op jit(solution)/shard_map/all_gather | solution.py:172
  45.7 60.0 %copy-start.2 = (bf16[1,512,640]{2,1,0:T(8,128)(2,1)S(1)}, bf16[1,512,640]{2,1,0:T(8,128)(2,1)}, u32[]{:S(2)}) copy-start(bf16[1,512,640]{2,1,0:T(8,128)(2,1)} %param.9) | copy-start | bytes 1966084
  105.8 58.0 %collective-permute-start = (bf16[512,640]{1,0:T(8,128)(2,1)S(1)}, bf16[512,640]{1,0:T(8,128)(2,1)S(1)}, u32[]{:S(2)}, u32[]{:S(2)}) collective-permute-start(bf16[512,640]{1,0:T(8,128)(2,1)S(1)} %bitcast.29), channel_id=1, source_target_pairs={{0,1},{1,0},{2,3},{3,2},{4,5},{5,4},{6,7},{7,6},{8,9},{9,8},{10,11... | collective-permute-start | bytes 1966088 | tf_op jit(solution)/shard_map/ppermute | solution.py:155
  163.8 0.9 copy-start.5
  181.2 55.3 %collective-permute-start.2 = (f32[512,640]{1,0:T(8,128)}, f32[512,640]{1,0:T(8,128)}, u32[]{:S(2)}, u32[]{:S(2)}) collective-permute-start(f32[512,640]{1,0:T(8,128)} %get-tuple-element.45), channel_id=1, source_target_pairs={{0,1},{1,0},{2,3},{3,2},{4,5},{5,4},{6,7},{7,6},{8,9},{9,8},{10,11... | collective-permute-start | bytes 3932168 | tf_op jit(solution)/shard_map/ppermute | solution.py:187
  197.3 32.5 %collective-permute-start.1 = (f32[512,5]{1,0:T(8,128)S(1)}, f32[512,5]{1,0:T(8,128)S(1)}, u32[]{:S(2)}, u32[]{:S(2)}) collective-permute-start(f32[512,5]{1,0:T(8,128)S(1)} %slice.12), channel_id=1, source_target_pairs={{0,1},{1,0},{2,3},{3,2},{4,5},{5,4},{6,7},{7,6},{8,9},{9,8},{10,11... | collective-permute-start | bytes 30728 | tf_op jit(solution)/shard_map/ppermute | solution.py:187
  199.9 34.9 %collective-permute-start.3 = (f32[512,5]{1,0:T(8,128)S(1)}, f32[512,5]{1,0:T(8,128)S(1)}, u32[]{:S(2)}, u32[]{:S(2)}) collective-permute-start(f32[512,5]{1,0:T(8,128)S(1)} %slice.13), channel_id=1, source_target_pairs={{0,1},{1,0},{2,3},{3,2},{4,5},{5,4},{6,7},{7,6},{8,9},{9,8},{10,11... | collective-permute-start | bytes 30728 | tf_op jit(solution)/shard_map/ppermute | solution.py:187
  245.9 2.7 copy-start.4
  248.6 3.0 collective-permute-start.5
  248.6 31.3 %collective-permute-start.4 = (bf16[128,5120]{1,0:T(8,128)(2,1)}, bf16[128,5120]{1,0:T(8,128)(2,1)}, u32[]{:S(2)}, u32[]{:S(2)}) collective-permute-start(bf16[128,5120]{1,0:T(8,128)(2,1)} %get-tuple-element.52), channel_id=1, source_target_pairs={{0,64},{64,0},{1,65},{65,1},{2,66},{66,2},{3,67},{67,3},{4,68},{68... | collective-permute-start | bytes 3932168 | tf_op jit(solution)/shard_map/ppermute | solution.py:231
  253.4 16.9 %collective-permute-start.6 = (bf16[64,5120]{1,0:T(8,128)(2,1)S(1)}, bf16[64,5120]{1,0:T(8,128)(2,1)S(1)}, u32[]{:S(2)}, u32[]{:S(2)}) collective-permute-start(bf16[64,5120]{1,0:T(8,128)(2,1)S(1)} %get-tuple-element.53), channel_id=1, source_target_pairs={{0,4},{4,8},{8,12},{12,128},{128,132},{132,136},{136,140},{140,0},... | collective-permute-start | bytes 1966088 | tf_op jit(solution)/shard_map/ppermute | solution.py:221
  253.5 24.6 %collective-permute-start.8 = (bf16[64,5120]{1,0:T(8,128)(2,1)S(1)}, bf16[64,5120]{1,0:T(8,128)(2,1)S(1)}, u32[]{:S(2)}, u32[]{:S(2)}) collective-permute-start(bf16[64,5120]{1,0:T(8,128)(2,1)S(1)} %get-tuple-element.54), channel_id=1, source_target_pairs={{0,140},{4,0},{8,4},{12,8},{128,12},{132,128},{136,132},{140,136},... | collective-permute-start | bytes 1966088 | tf_op jit(solution)/shard_map/ppermute | solution.py:221
  270.2 49.6 %collective-permute-start.7 = (bf16[64,5120]{1,0:T(8,128)(2,1)S(1)}, bf16[64,5120]{1,0:T(8,128)(2,1)S(1)}, u32[]{:S(2)}, u32[]{:S(2)}) collective-permute-start(bf16[64,5120]{1,0:T(8,128)(2,1)S(1)} %collective-permute-done.6), channel_id=1, source_target_pairs={{0,12},{4,128},{8,132},{12,136},{128,140},{132,0},{136,4},{140,8},... | collective-permute-start | bytes 1966088 | tf_op jit(solution)/shard_map/ppermute | solution.py:221
  278.0 45.2 %collective-permute-start.9 = (bf16[64,5120]{1,0:T(8,128)(2,1)S(1)}, bf16[64,5120]{1,0:T(8,128)(2,1)S(1)}, u32[]{:S(2)}, u32[]{:S(2)}) collective-permute-start(bf16[64,5120]{1,0:T(8,128)(2,1)S(1)} %collective-permute-done.8), channel_id=1, source_target_pairs={{0,132},{4,136},{8,140},{12,0},{128,4},{132,8},{136,12},{140,128},... | collective-permute-start | bytes 1966088 | tf_op jit(solution)/shard_map/ppermute | solution.py:221
  323.2 3.5 %copy-start.1 = (bf16[128,8,640]{2,1,0:T(8,128)(2,1)S(1)}, bf16[128,8,640]{2,1,0:T(8,128)(2,1)}, u32[]{:S(2)}) copy-start(bf16[128,8,640]{2,1,0:T(8,128)(2,1)} %param.12) | copy-start | bytes 3932164
Sparse Core Ops, SparseCore 0:
  9.1 96.5 all-gather.2
  107.5 88.2 all-gather.4

commit v12 on v11

--- a/solution.py
+++ b/solution.py
@@ -42,7 +42,7 @@
         def one_head(head, carry):
             cols = pl.ds(pl.multiple_of(head * HD, HD), HD)
             scores = lax.dot_general(
-                q_ref[:, cols], k_ref[0, 0, :, cols], (((1,), (1,)), ((), ())),
+                q_ref[:, cols], k_ref[:, 0, 0, :, cols].reshape(-1, HD), (((1,), (1,)), ((), ())),
                 preferred_element_type=jnp.float32,
             ) * (1.0 / math.sqrt(HD))
             running_max = m_ref[:, cols][:, :1]
@@ -51,7 +51,7 @@
             weights = jnp.exp(scores - new_max)
             l_ref[:, cols] = l_ref[:, cols] * shrink + jnp.sum(weights, axis=1, keepdims=True)
             o_ref[:, cols] = o_ref[:, cols] * shrink + jnp.dot(
-                weights.astype(jnp.bfloat16), v_ref[0, 0, :, cols],
+                weights.astype(jnp.bfloat16), v_ref[:, 0, 0, :, cols].reshape(-1, HD),
                 preferred_element_type=jnp.float32,
             )
             m_ref[:, cols] = jnp.broadcast_to(new_max, (new_max.shape[0], HD))
@@ -62,8 +62,8 @@
 
 def attend(queries, arrived, order, count, init=None):
     tokens, width = queries.shape
-    slots = arrived.shape[1]
-    keys_each = arrived.shape[2]
+    senders, _, slots, rows_each, _ = arrived.shape
+    keys_each = senders * rows_each
     heads = width // HD
     with_init = init is not None
 
@@ -71,8 +71,8 @@
         return order_ref[jnp.clip(s, 0, jnp.maximum(count_ref[0] - 1, 0))]
 
     q_spec = pl.BlockSpec((tokens, width), lambda s, o, c: (0, 0))
-    k_spec = pl.BlockSpec((1, 1, keys_each, width), lambda s, o, c: (0, slot_at(s, o, c), 0, 0))
-    v_spec = pl.BlockSpec((1, 1, keys_each, width), lambda s, o, c: (1, slot_at(s, o, c), 0, 0))
+    k_spec = pl.BlockSpec((senders, 1, 1, rows_each, width), lambda s, o, c: (0, 0, slot_at(s, o, c), 0, 0))
+    v_spec = pl.BlockSpec((senders, 1, 1, rows_each, width), lambda s, o, c: (0, 1, slot_at(s, o, c), 0, 0))
     in_specs = [q_spec, k_spec, v_spec]
     operands = [queries, arrived, arrived]
     state_spec = pl.BlockSpec((tokens, width), lambda s, o, c: (0, 0))
@@ -147,9 +147,8 @@
     weight = lax.all_gather(out_weight, ("zl", "x"), axis=1, tiled=True)
 
     blocks = pair_schedule(frames, slots, page_table, frame_lists, list_counts).T
-    sent = jnp.stack([cache_keys[blocks], cache_values[blocks]], axis=0)
-    arrived = lax.all_to_all(sent, FRAME_AXES, split_axis=2, concat_axis=2, tiled=True)
-    arrived = arrived.reshape(2, slots, tokens_here, row_width)
+    sent = jnp.stack([cache_keys[blocks.T], cache_values[blocks.T]], axis=1)
+    arrived = lax.all_to_all(sent, FRAME_AXES, split_axis=0, concat_axis=0, tiled=True)
 
     swap = [(i, i ^ 1) for i in range(lax.axis_size("x"))]
     partner_queries = lax.ppermute(own_queries, "x", swap)
@@ -164,7 +163,7 @@
     step = jnp.arange(slots, dtype=jnp.int32)
     visit = jnp.where(odd == 0, slots - 1 - step, step)
 
-    own_span = jnp.stack([own_keys, own_values])[:, None]
+    own_span = jnp.stack([own_keys, own_values]).reshape(2, 1, -1, cache_keys.shape[1], row_width).transpose(2, 0, 1, 3, 4)
     own_start = attend(
         own_queries, own_span, jnp.zeros((1,), jnp.int32), jnp.ones((1,), jnp.int32)
     )

time: 336 us -> 326 us (0.970)
  waiting for transfers between devices: 185 us -> 170 us
  starting transfers between devices: 39.9 us -> 50.5 us
  local copies, waits for them, and re-layouts: 25.4 us -> 16.1 us
    all_to_all x1, waiting for transfers between devices: 43.5 us -> 26.9 us  [local(): lax.all_to_all(sent, FRAME_AXES, split_axis=0, concat_axis=0, tiled=True)]
    ppermute x1, waiting for transfers between devices: 0.01 us -> 14.2 us  [local(): partner_queries = lax.ppermute(own_queries, 'x', swap)]
    ppermute x3, waiting for transfers between devices: 20.1 us -> 6.97 us  [local(): lax.ppermute((other_max[:, ::HD], other_sum[:, ::HD], other_out), 'x', swap)]
    ppermute x4, starting transfers between devices: 11.8 us -> 21 us  [shifted(): lax.ppermute(rows, z_axes, [(i, (i + by) % ring) for i in range(ring)])]
    all_to_all x1 -> x0, local copies, waits for them, and re-layouts: 5.33 us -> none  [local(): lax.all_to_all(sent, FRAME_AXES, split_axis=2, concat_axis=2, tiled=True)]
  transfers between devices with their start and end apart: 13 -> 13, of which waited for: 8 -> 9; matrix products, arithmetic and copies ran while one was open for 10% -> 8% of each run, Pallas kernels for 13% -> 14%
where the time goes in v12:
time: 326 us; the launch traced here: 322 us
  waiting for transfers between devices  170 us (52%)
  starting transfers between devices  50.5 us (15%)
  Pallas kernels  43.9 us (13%)
  other arithmetic  16.7 us (5%)
  local copies, waits for them, and re-layouts  16.1 us (5%)
  between operations  15.8 us (5%)
  matrix products  9.36 us (3%)
    all_gather x1, waiting for transfers between devices, local(): weight = lax.all_gather(out_weight, ('zl', 'x'), axis=1, tiled=True)  60.5 us
    ppermute x4, waiting for transfers between devices, shifted(): lax.ppermute(rows, z_axes, [(i, (i + by) % ring) for i in range(ring)])  58 us
    pallas_call x4, Pallas kernels, attend(): pl.pallas_call(lambda *refs: attend_kernel(*refs, with_init=with_init, he...  43.9 us
    all_to_all x1, waiting for transfers between devices, local(): lax.all_to_all(sent, FRAME_AXES, split_axis=0, concat_axis=0, tiled=True)  26.9 us
    ppermute x4, starting transfers between devices, shifted(): lax.ppermute(rows, z_axes, [(i, (i + by) % ring) for i in range(ring)])  21 us
    ppermute x3, starting transfers between devices, local(): lax.ppermute((other_max[:, ::HD], other_sum[:, ::HD], other_out), 'x', swap)  15 us
    ppermute x1, waiting for transfers between devices, local(): partner_queries = lax.ppermute(own_queries, 'x', swap)  14.2 us
    all_to_all x1, starting transfers between devices, local(): lax.all_to_all(sent, FRAME_AXES, split_axis=0, concat_axis=0, tiled=True)  11.8 us
  transfers between devices with their start and end apart: 13, of which 9 were waited for; matrix products, arithmetic and copies ran while one was open for 8% of the time, Pallas kernels for 14%

profile of v12, /device:TPU:50, one launch (start us, length us, event | category | flops | bytes accessed | tf_op | source)
XLA Modules:
  0.0 322.2 jit_solution(3239098027800292023)
XLA Ops:
  6.5 0.0 copy-start
  6.5 0.0 all-gather.3.cloned.1.call-start
  6.5 0.7 all-gather.3.cloned.1.call-update
  7.3 1.3 iota_subtract_fusion
  8.6 0.8 select_reduce_fusion.3
  9.4 0.8 copy.17
  10.2 0.1 reshape.305
  10.4 0.3 select_reduce_fusion
  10.7 0.9 select_reduce_fusion.2
  11.6 0.1 copy.18
  11.7 0.1 reshape.313
  11.8 0.0 copy-done
  11.8 0.0 copy-start.3
  11.8 2.5 gather_fusion
  14.3 0.0 copy-done.3
  14.3 2.4 gather_fusion.1
  16.7 5.3 %pad_maximum_fusion = bf16[64,2,4,8,640]{4,3,2,1,0:T(8,128)(2,1)} fusion(bf16[64,1,4,8,640]{4,3,2,1,0:T(8,128)(2,1)} %bitcast.21, bf16[64,1,4,8,640]{4,3,2,1,0:T(8,128)(2,1)} %bitcast.20), kind=kLoop, calls=%fused_computation.3 | loop fusion | flops 2621440 | bytes 10485760 | tf_op jit(solution)/shard_map/stack | solution.py:150
  22.1 11.8 %all-to-all-start = ((bf16[64,2,4,8,640]{4,3,2,1,0:T(8,128)(2,1)}), bf16[64,2,4,8,640]{4,3,2,1,0:T(8,128)(2,1)}, u32[]{:S(2)}, u32[]{:S(2)}) async-start(bf16[64,2,4,8,640]{4,3,2,1,0:T(8,128)(2,1)} %pad_maximum_fusion), calls=%async_computation | async-start | bytes 10485760 | tf_op jit(solution)/shard_map/all_to_all | solution.py:151
  33.9 0.0 all-gather.5.cloned.1.call-start
  34.0 1.2 copy_bitcast_fusion.refs_3_.refs_4_
  35.2 9.7 %shard_map.92 = (f32[512,640]{1,0:T(8,128)}, f32[512,640]{1,0:T(8,128)}, f32[512,640]{1,0:T(8,128)}) custom-call(s32[1]{0:T(128)} %constant.86.clone.1.refs_0_, s32[1]{0:T(128)} %constant.87.clone.1.refs_1_, bf16[512,640]{1,0:T(8,128)(2,1)} %bitcast.22, bf16[64,2,1,8,640]{4,3,2,1,0:T(8,128)(2,1)} %copy_bitcast_fusion.refs_3_.refs_4_, ...), custom_call_target="tpu_custom_call" | custom-call | flops 671088640 | bytes 9175040 | tf_op jit(solution)/shard_map/pallas_call | solution.py:83
  44.8 60.5 %all-gather.3.cloned.1.call-done = bf16[640,1280]{0,1:T(8,128)(2,1)} async-done(((bf16[640,80]{0,1:T(8,128)(2,1)}), bf16[640,1280]{0,1:T(8,128)(2,1)}) %all-gather.3.cloned.1.call-update) | async-done | bytes 1638416 | tf_op jit(solution)/shard_map/all_gather | solution.py:147
  105.3 0.0 all-gather.5.cloned.1.call-update
  105.3 2.1 collective-permute-start
  109.6 0.6 broadcast_select_fusion.refs_0_
  110.2 0.6 broadcast_select_fusion.1.refs_0_
  110.8 14.2 %collective-permute-done.refs_2_ = bf16[512,640]{1,0:T(8,128)(2,1)S(1)} collective-permute-done((bf16[512,640]{1,0:T(8,128)(2,1)S(1)}, bf16[512,640]{1,0:T(8,128)(2,1)S(1)}, u32[]{:S(2)}, u32[]{:S(2)}) %collective-permute-start) | collective-permute-done | bytes 655392 | tf_op jit(solution)/shard_map/ppermute | solution.py:154
  125.0 26.9 %all-to-all-done.refs_3_.refs_4_ = bf16[64,2,4,8,640]{4,3,2,1,0:T(8,128)(2,1)} async-done(((bf16[64,2,4,8,640]{4,3,2,1,0:T(8,128)(2,1)}), bf16[64,2,4,8,640]{4,3,2,1,0:T(8,128)(2,1)}, u32[]{:S(2)}, u32[]{:S(2)}) %all-to-all-start) | async-done | bytes 5242912 | tf_op jit(solution)/shard_map/all_to_all | solution.py:151
  151.9 4.7 %shard_map.91 = (f32[512,640]{1,0:T(8,128)}, f32[512,640]{1,0:T(8,128)}, f32[512,640]{1,0:T(8,128)}) custom-call(s32[4]{0:T(128)} %broadcast_select_fusion.1.refs_0_, s32[1]{0:T(128)} %bitcast.5.refs_1_, bf16[512,640]{1,0:T(8,128)(2,1)} %copy-done.5, bf16[64,2,4,8,640]{4,3,2,1,0:T(8,128)(2,1)} %all-to-all-done.refs_3_.refs_4_, ...), custom_call_target="tpu_custom_call" | custom-call | flops 2684354560 | bytes 13107200 | tf_op jit(solution)/shard_map/pallas_call | solution.py:83
  156.6 5.8 %shard_map.93 = (f32[512,640]{1,0:T(8,128)}, f32[512,640]{1,0:T(8,128)}, f32[512,640]{1,0:T(8,128)}) custom-call(s32[4]{0:T(128)} %broadcast_select_fusion.refs_0_, s32[1]{0:T(128)} %bitcast.6.refs_1_, bf16[512,640]{1,0:T(8,128)(2,1)} %bitcast.23, bf16[64,2,4,8,640]{4,3,2,1,0:T(8,128)(2,1)} %all-to-all-done.refs_3_.refs_4_, ...), custom_call_target="tpu_custom_call" | custom-call | flops 2684354560 | bytes 13107200 | tf_op jit(solution)/shard_map/pallas_call | solution.py:83
  162.4 12.6 %collective-permute-start.2 = (f32[512,640]{1,0:T(8,128)}, f32[512,640]{1,0:T(8,128)}, u32[]{:S(2)}, u32[]{:S(2)}) collective-permute-start(f32[512,640]{1,0:T(8,128)} %get-tuple-element.45), channel_id=1, source_target_pairs={{0,1},{1,0},{2,3},{3,2},{4,5},{5,4},{6,7},{7,6},{8,9},{9,8},{10,11... | collective-permute-start | bytes 3932168 | tf_op jit(solution)/shard_map/ppermute | solution.py:186
  175.0 0.6 broadcast_select_fusion.2.refs_0_
  175.6 2.4 slice.12
  178.0 0.1 collective-permute-start.1
  178.1 2.5 slice.13
  180.6 2.3 collective-permute-start.3
  182.8 23.8 %shard_map.94 = (f32[512,640]{1,0:T(8,128)}, f32[512,640]{1,0:T(8,128)}, f32[512,640]{1,0:T(8,128)}) custom-call(s32[4]{0:T(128)} %broadcast_select_fusion.2.refs_0_, s32[1]{0:T(128)} %bitcast.refs_1_, bf16[512,640]{1,0:T(8,128)(2,1)} %bitcast.24, bf16[64,2,4,8,640]{4,3,2,1,0:T(8,128)(2,1)} %all-to-all-done.refs_3_.refs_4_, ...), custom_call_target="tpu_custom_call" | custom-call | flops 2684354560 | bytes 13107200 | tf_op jit(solution)/shard_map/pallas_call | solution.py:83
  206.6 3.8 %collective-permute-done.1 = f32[512,5]{1,0:T(8,128)S(1)} collective-permute-done((f32[512,5]{1,0:T(8,128)S(1)}, f32[512,5]{1,0:T(8,128)S(1)}, u32[]{:S(2)}, u32[]{:S(2)}) %collective-permute-start.1) | collective-permute-done | bytes 10272 | tf_op jit(solution)/shard_map/ppermute | solution.py:186
  210.4 0.1 copy.20
  210.6 0.2 broadcast_in_dim.59
  210.7 0.4 copy.21
  211.1 3.2 collective-permute-done.3
  214.3 0.1 copy.23
  214.4 0.2 broadcast_in_dim.60
  214.6 1.5 copy.24
  216.1 0.0 collective-permute-done.2
  216.1 9.4 %convolution_convert_fusion = bf16[512,5120]{1,0:T(8,128)(2,1)S(1)} fusion(bf16[640,5120]{0,1:T(8,128)(2,1)} %all-gather.5.cloned.1.call-done, f32[512,640]{1,0:T(8,128)} %copy.24, f32[512,640]{1,0:T(8,128)} %get-tuple-element.46, f32[512,640]{1,0:T(8,128)} %collective-permute-done.2, f32[512,640]{1,0:T(8,128)S(1)} %copy.21, ...), kind=kOutput, calls=%fused_computation.2 | convolution fusion | flops 3361669120 | bytes 19660800 | tf_op jit(solution)/shard_map/dot_general | solution.py:200
  225.4 1.4 constant_dynamic-slice_fusion.1
  226.8 1.4 copy-done.4
  228.1 0.0 collective-permute-start.5
  228.2 0.5 collective-permute-start.4
  228.7 2.5 collective-permute-done.5
  231.2 1.6 add_convert_fusion.1
  232.8 0.1 fusion.6
  232.9 15.5 %collective-permute-start.6 = (bf16[64,5120]{1,0:T(8,128)(2,1)S(1)}, bf16[64,5120]{1,0:T(8,128)(2,1)S(1)}, u32[]{:S(2)}, u32[]{:S(2)}) collective-permute-start(bf16[64,5120]{1,0:T(8,128)(2,1)S(1)} %get-tuple-element.53), channel_id=1, source_target_pairs={{0,4},{4,8},{8,12},{12,128},{128,132},{132,136},{136,140},{140,0},... | collective-permute-start | bytes 1966088 | tf_op jit(solution)/shard_map/ppermute | solution.py:220
  248.4 0.0 collective-permute-start.8
  248.4 14.3 %collective-permute-done.6 = bf16[64,5120]{1,0:T(8,128)(2,1)S(1)} collective-permute-done((bf16[64,5120]{1,0:T(8,128)(2,1)S(1)}, bf16[64,5120]{1,0:T(8,128)(2,1)S(1)}, u32[]{:S(2)}, u32[]{:S(2)}) %collective-permute-start.6) | collective-permute-done | bytes 655392 | tf_op jit(solution)/shard_map/ppermute | solution.py:220
  262.7 2.2 collective-permute-start.7
  264.9 0.0 collective-permute-done.8
  264.9 3.3 %collective-permute-start.9 = (bf16[64,5120]{1,0:T(8,128)(2,1)S(1)}, bf16[64,5120]{1,0:T(8,128)(2,1)S(1)}, u32[]{:S(2)}, u32[]{:S(2)}) collective-permute-start(bf16[64,5120]{1,0:T(8,128)(2,1)S(1)} %collective-permute-done.8), channel_id=1, source_target_pairs={{0,132},{4,136},{8,140},{12,0},{128,4},{132,8},{136,12},{140,128},... | collective-permute-start | bytes 1966088 | tf_op jit(solution)/shard_map/ppermute | solution.py:220
  268.2 0.0 collective-permute-done.4
  268.2 42.3 %collective-permute-done.7 = bf16[64,5120]{1,0:T(8,128)(2,1)S(1)} collective-permute-done((bf16[64,5120]{1,0:T(8,128)(2,1)S(1)}, bf16[64,5120]{1,0:T(8,128)(2,1)S(1)}, u32[]{:S(2)}, u32[]{:S(2)}) %collective-permute-start.7) | collective-permute-done | bytes 655392 | tf_op jit(solution)/shard_map/ppermute | solution.py:220
  310.5 1.4 collective-permute-done.9
  311.9 3.5 %fusion.2 = bf16[1,128,5120]{2,1,0:T(8,128)(2,1)} fusion(bf16[128,5120]{1,0:T(8,128)(2,1)} %collective-permute-done.4, bf16[64,5120]{1,0:T(8,128)(2,1)S(1)} %collective-permute-done.9, bf16[64,5120]{1,0:T(8,128)(2,1)S(1)} %collective-permute-done.7, bf16[512,5120]{1,0:T(8,128)(2,1)} %copy-done.4, s32[]{:T(128)S(6)} %select_n.150), kind=kLoop, calls=%fused_computation.10 | loop fusion | flops 5898240 | bytes 5242884 | tf_op jit(solution)/shard_map/broadcast_in_dim | solution.py:234
  (18 shorter events, 0.1 us)
Async XLA Ops:
  6.5 5.3 %copy-start = (bf16[128,8,640]{2,1,0:T(8,128)(2,1)S(1)}, bf16[128,8,640]{2,1,0:T(8,128)(2,1)}, u32[]{:S(2)}) copy-start(bf16[128,8,640]{2,1,0:T(8,128)(2,1)} %param.12) | copy-start | bytes 3932164
  6.5 98.8 %all-gather.3.cloned.1.call-start = ((), (), s32[]{:S(2)}) async-start(), calls=%async_computation.1 | async-start | bytes 1740800 | tf_op jit(solution)/shard_map/all_gather | solution.py:147
  11.8 2.5 copy-start.3
  22.1 11.9 %copy-start.6 = (bf16[1,512,640]{2,1,0:T(8,128)(2,1)S(1)}, bf16[1,512,640]{2,1,0:T(8,128)(2,1)}, u32[]{:S(2)}) copy-start(bf16[1,512,640]{2,1,0:T(8,128)(2,1)} %param.11) | copy-start | bytes 1966084
  22.1 11.9 %copy-start.7 = (bf16[1,512,640]{2,1,0:T(8,128)(2,1)S(1)}, bf16[1,512,640]{2,1,0:T(8,128)(2,1)}, u32[]{:S(2)}) copy-start(bf16[1,512,640]{2,1,0:T(8,128)(2,1)} %param.10) | copy-start | bytes 1966084
  22.1 129.8 %all-to-all-start = ((bf16[64,2,4,8,640]{4,3,2,1,0:T(8,128)(2,1)}), bf16[64,2,4,8,640]{4,3,2,1,0:T(8,128)(2,1)}, u32[]{:S(2)}, u32[]{:S(2)}) async-start(bf16[64,2,4,8,640]{4,3,2,1,0:T(8,128)(2,1)} %pad_maximum_fusion), calls=%async_computation | async-start | bytes 10485760 | tf_op jit(solution)/shard_map/all_to_all | solution.py:151
  33.9 182.1 %all-gather.5.cloned.1.call-start = ((), (), s32[]{:S(2)}) async-start(), calls=%async_computation.2 | async-start | bytes 8192000 | tf_op jit(solution)/shard_map/all_gather | solution.py:171
  44.8 60.5 %copy-start.2 = (bf16[1,512,640]{2,1,0:T(8,128)(2,1)S(1)}, bf16[1,512,640]{2,1,0:T(8,128)(2,1)}, u32[]{:S(2)}) copy-start(bf16[1,512,640]{2,1,0:T(8,128)(2,1)} %param.9) | copy-start | bytes 1966084
  105.3 19.7 %collective-permute-start = (bf16[512,640]{1,0:T(8,128)(2,1)S(1)}, bf16[512,640]{1,0:T(8,128)(2,1)S(1)}, u32[]{:S(2)}, u32[]{:S(2)}) collective-permute-start(bf16[512,640]{1,0:T(8,128)(2,1)S(1)} %bitcast.25), channel_id=1, source_target_pairs={{0,1},{1,0},{2,3},{3,2},{4,5},{5,4},{6,7},{7,6},{8,9},{9,8},{10,11... | collective-permute-start | bytes 1966088 | tf_op jit(solution)/shard_map/ppermute | solution.py:154
  125.0 26.9 %copy-start.5 = (bf16[512,640]{1,0:T(8,128)(2,1)}, bf16[512,640]{1,0:T(8,128)(2,1)S(1)}, u32[]{:S(2)}) copy-start(bf16[512,640]{1,0:T(8,128)(2,1)S(1)} %collective-permute-done.refs_2_) | copy-start | bytes 1966084
  162.4 53.7 %collective-permute-start.2 = (f32[512,640]{1,0:T(8,128)}, f32[512,640]{1,0:T(8,128)}, u32[]{:S(2)}, u32[]{:S(2)}) collective-permute-start(f32[512,640]{1,0:T(8,128)} %get-tuple-element.45), channel_id=1, source_target_pairs={{0,1},{1,0},{2,3},{3,2},{4,5},{5,4},{6,7},{7,6},{8,9},{9,8},{10,11... | collective-permute-start | bytes 3932168 | tf_op jit(solution)/shard_map/ppermute | solution.py:186
  178.0 32.4 %collective-permute-start.1 = (f32[512,5]{1,0:T(8,128)S(1)}, f32[512,5]{1,0:T(8,128)S(1)}, u32[]{:S(2)}, u32[]{:S(2)}) collective-permute-start(f32[512,5]{1,0:T(8,128)S(1)} %slice.12), channel_id=1, source_target_pairs={{0,1},{1,0},{2,3},{3,2},{4,5},{5,4},{6,7},{7,6},{8,9},{9,8},{10,11... | collective-permute-start | bytes 30728 | tf_op jit(solution)/shard_map/ppermute | solution.py:186
  180.6 33.7 %collective-permute-start.3 = (f32[512,5]{1,0:T(8,128)S(1)}, f32[512,5]{1,0:T(8,128)S(1)}, u32[]{:S(2)}, u32[]{:S(2)}) collective-permute-start(f32[512,5]{1,0:T(8,128)S(1)} %slice.13), channel_id=1, source_target_pairs={{0,1},{1,0},{2,3},{3,2},{4,5},{5,4},{6,7},{7,6},{8,9},{9,8},{10,11... | collective-permute-start | bytes 30728 | tf_op jit(solution)/shard_map/ppermute | solution.py:186
  225.4 2.7 copy-start.4
  228.1 3.0 collective-permute-start.5
  228.2 40.1 %collective-permute-start.4 = (bf16[128,5120]{1,0:T(8,128)(2,1)}, bf16[128,5120]{1,0:T(8,128)(2,1)}, u32[]{:S(2)}, u32[]{:S(2)}) collective-permute-start(bf16[128,5120]{1,0:T(8,128)(2,1)} %get-tuple-element.52), channel_id=1, source_target_pairs={{0,64},{64,0},{1,65},{65,1},{2,66},{66,2},{3,67},{67,3},{4,68},{68... | collective-permute-start | bytes 3932168 | tf_op jit(solution)/shard_map/ppermute | solution.py:230
  232.9 29.8 %collective-permute-start.6 = (bf16[64,5120]{1,0:T(8,128)(2,1)S(1)}, bf16[64,5120]{1,0:T(8,128)(2,1)S(1)}, u32[]{:S(2)}, u32[]{:S(2)}) collective-permute-start(bf16[64,5120]{1,0:T(8,128)(2,1)S(1)} %get-tuple-element.53), channel_id=1, source_target_pairs={{0,4},{4,8},{8,12},{12,128},{128,132},{132,136},{136,140},{140,0},... | collective-permute-start | bytes 1966088 | tf_op jit(solution)/shard_map/ppermute | solution.py:220
  248.4 16.5 %collective-permute-start.8 = (bf16[64,5120]{1,0:T(8,128)(2,1)S(1)}, bf16[64,5120]{1,0:T(8,128)(2,1)S(1)}, u32[]{:S(2)}, u32[]{:S(2)}) collective-permute-start(bf16[64,5120]{1,0:T(8,128)(2,1)S(1)} %get-tuple-element.54), channel_id=1, source_target_pairs={{0,140},{4,0},{8,4},{12,8},{128,12},{132,128},{136,132},{140,136},... | collective-permute-start | bytes 1966088 | tf_op jit(solution)/shard_map/ppermute | solution.py:220
  262.7 47.8 %collective-permute-start.7 = (bf16[64,5120]{1,0:T(8,128)(2,1)S(1)}, bf16[64,5120]{1,0:T(8,128)(2,1)S(1)}, u32[]{:S(2)}, u32[]{:S(2)}) collective-permute-start(bf16[64,5120]{1,0:T(8,128)(2,1)S(1)} %collective-permute-done.6), channel_id=1, source_target_pairs={{0,12},{4,128},{8,132},{12,136},{128,140},{132,0},{136,4},{140,8},... | collective-permute-start | bytes 1966088 | tf_op jit(solution)/shard_map/ppermute | solution.py:220
  264.9 47.0 %collective-permute-start.9 = (bf16[64,5120]{1,0:T(8,128)(2,1)S(1)}, bf16[64,5120]{1,0:T(8,128)(2,1)S(1)}, u32[]{:S(2)}, u32[]{:S(2)}) collective-permute-start(bf16[64,5120]{1,0:T(8,128)(2,1)S(1)} %collective-permute-done.8), channel_id=1, source_target_pairs={{0,132},{4,136},{8,140},{12,0},{128,4},{132,8},{136,12},{140,128},... | collective-permute-start | bytes 1966088 | tf_op jit(solution)/shard_map/ppermute | solution.py:220
  311.9 3.5 %copy-start.1 = (bf16[128,8,640]{2,1,0:T(8,128)(2,1)S(1)}, bf16[128,8,640]{2,1,0:T(8,128)(2,1)}, u32[]{:S(2)}) copy-start(bf16[128,8,640]{2,1,0:T(8,128)(2,1)} %param.12) | copy-start | bytes 3932164
Sparse Core Ops, SparseCore 0:
  9.1 96.1 all-gather.2
  107.1 87.3 all-gather.4

commit v13 on v12

--- a/solution.py
+++ b/solution.py
@@ -183,14 +183,16 @@
     )
     other_state, own_state = lax.optimization_barrier((other_state, own_state))
     other_out, other_max, other_sum = other_state
-    got_max, got_sum, got_out = lax.ppermute(
-        (other_max[:, ::HD], other_sum[:, ::HD], other_out), "x", swap
+    other_mean = jnp.where(other_sum > 0, other_out / jnp.maximum(other_sum, 1e-30), 0.0)
+    got_max, got_sum, got_mean = lax.ppermute(
+        (other_max[:, ::HD], other_sum[:, ::HD], other_mean.astype(jnp.bfloat16)), "x", swap
     )
     own_out, own_max, own_sum = attend(
         own_queries, arrived, visits_from(other_count + before), after.reshape(1), own_state
     )
     got_max = jnp.repeat(got_max, HD, axis=1)
     got_sum = jnp.repeat(got_sum, HD, axis=1)
+    got_out = got_mean.astype(jnp.float32) * got_sum
     top = jnp.maximum(own_max, got_max)
     own_scale = jnp.exp(own_max - top)
     got_scale = jnp.exp(got_max - top)

time: 326 us -> 317 us (0.972)
  starting transfers between devices: 50.5 us -> 33.8 us
  waiting for transfers between devices: 170 us -> 175 us
    ppermute x4, starting transfers between devices: 21 us -> 7.13 us  [shifted(): lax.ppermute(rows, z_axes, [(i, (i + by) % ring) for i in range(ring)])]
    ppermute x3, waiting for transfers between devices: 6.97 us -> 12.5 us  [local(): lax.ppermute((other_max[:, ::HD], other_sum[:, ::HD], other_mean.astype(j...]
    all_to_all x1, waiting for transfers between devices: 26.9 us -> 21.4 us  [local(): lax.all_to_all(sent, FRAME_AXES, split_axis=0, concat_axis=0, tiled=True)]
    all_gather x1, waiting for transfers between devices: 60.5 us -> 64.9 us  [local(): weight = lax.all_gather(out_weight, ('zl', 'x'), axis=1, tiled=True)]
  transfers between devices with their start and end apart: 13 -> 13, of which waited for: 9 -> 9; matrix products, arithmetic and copies ran while one was open for 8% -> 9% of each run, Pallas kernels for 14% -> 14%
where the time goes in v13:
time: 317 us; the launch traced here: 311 us
  waiting for transfers between devices  175 us (55%)
  Pallas kernels  43.9 us (14%)
  starting transfers between devices  33.8 us (11%)
  other arithmetic  16.9 us (5%)
  between operations  16.2 us (5%)
  local copies, waits for them, and re-layouts  16.1 us (5%)
  matrix products  9.23 us (3%)
    all_gather x1, waiting for transfers between devices, local(): weight = lax.all_gather(out_weight, ('zl', 'x'), axis=1, tiled=True)  64.9 us
    ppermute x4, waiting for transfers between devices, shifted(): lax.ppermute(rows, z_axes, [(i, (i + by) % ring) for i in range(ring)])  55.6 us
    pallas_call x4, Pallas kernels, attend(): pl.pallas_call(lambda *refs: attend_kernel(*refs, with_init=with_init, he...  43.9 us
    all_to_all x1, waiting for transfers between devices, local(): lax.all_to_all(sent, FRAME_AXES, split_axis=0, concat_axis=0, tiled=True)  21.4 us
    ppermute x1, waiting for transfers between devices, local(): partner_queries = lax.ppermute(own_queries, 'x', swap)  16.9 us
    ppermute x3, starting transfers between devices, local(): lax.ppermute((other_max[:, ::HD], other_sum[:, ::HD], other_mean.astype(j...  14.2 us
    ppermute x3, waiting for transfers between devices, local(): lax.ppermute((other_max[:, ::HD], other_sum[:, ::HD], other_mean.astype(j...  12.5 us
    all_to_all x1, starting transfers between devices, local(): lax.all_to_all(sent, FRAME_AXES, split_axis=0, concat_axis=0, tiled=True)  11.8 us
  transfers between devices with their start and end apart: 13, of which 9 were waited for; matrix products, arithmetic and copies ran while one was open for 9% of the time, Pallas kernels for 14%

profile of v13, /device:TPU:50, one launch (start us, length us, event | category | flops | bytes accessed | tf_op | source)
XLA Modules:
  0.0 310.7 jit_solution(16881810009582583378)
XLA Ops:
  6.5 0.0 all-gather.3.cloned.1.call-start
  6.5 0.7 all-gather.3.cloned.1.call-update
  7.3 1.3 iota_subtract_fusion
  8.6 0.8 select_reduce_fusion.3
  9.5 0.8 copy.18
  10.3 0.1 reshape.305
  10.4 0.3 select_reduce_fusion
  10.7 0.9 select_reduce_fusion.2
  11.6 0.1 copy.19
  11.7 0.1 reshape.313
  11.9 0.0 copy-start.3
  11.9 2.5 gather_fusion
  14.4 0.0 copy-done.3
  14.4 2.4 gather_fusion.1
  16.8 5.3 %pad_maximum_fusion = bf16[64,2,4,8,640]{4,3,2,1,0:T(8,128)(2,1)} fusion(bf16[64,1,4,8,640]{4,3,2,1,0:T(8,128)(2,1)} %bitcast.21, bf16[64,1,4,8,640]{4,3,2,1,0:T(8,128)(2,1)} %bitcast.20), kind=kLoop, calls=%fused_computation.3 | loop fusion | flops 2621440 | bytes 10485760 | tf_op jit(solution)/shard_map/stack | solution.py:150
  22.2 11.8 %all-to-all-start = ((bf16[64,2,4,8,640]{4,3,2,1,0:T(8,128)(2,1)}), bf16[64,2,4,8,640]{4,3,2,1,0:T(8,128)(2,1)}, u32[]{:S(2)}, u32[]{:S(2)}) async-start(bf16[64,2,4,8,640]{4,3,2,1,0:T(8,128)(2,1)} %pad_maximum_fusion), calls=%async_computation | async-start | bytes 10485760 | tf_op jit(solution)/shard_map/all_to_all | solution.py:151
  34.0 0.0 all-gather.5.cloned.1.call-start
  34.1 1.2 copy_bitcast_fusion.refs_3_.refs_4_
  35.2 9.7 %shard_map.92 = (f32[512,640]{1,0:T(8,128)}, f32[512,640]{1,0:T(8,128)}, f32[512,640]{1,0:T(8,128)}) custom-call(s32[1]{0:T(128)} %constant.89.clone.1.refs_0_, s32[1]{0:T(128)} %constant.90.clone.1.refs_1_, bf16[512,640]{1,0:T(8,128)(2,1)} %bitcast.22, bf16[64,2,1,8,640]{4,3,2,1,0:T(8,128)(2,1)} %copy_bitcast_fusion.refs_3_.refs_4_, ...), custom_call_target="tpu_custom_call" | custom-call | flops 671088640 | bytes 9175040 | tf_op jit(solution)/shard_map/pallas_call | solution.py:83
  44.9 64.9 %all-gather.3.cloned.1.call-done = bf16[640,1280]{0,1:T(8,128)(2,1)} async-done(((bf16[640,80]{0,1:T(8,128)(2,1)}), bf16[640,1280]{0,1:T(8,128)(2,1)}) %all-gather.3.cloned.1.call-update) | async-done | bytes 1638416 | tf_op jit(solution)/shard_map/all_gather | solution.py:147
  109.8 0.0 all-gather.5.cloned.1.call-update
  109.9 0.1 collective-permute-start
  112.5 0.5 broadcast_select_fusion.refs_0_
  113.0 0.6 broadcast_select_fusion.1.refs_0_
  113.6 16.9 %collective-permute-done.refs_2_ = bf16[512,640]{1,0:T(8,128)(2,1)S(1)} collective-permute-done((bf16[512,640]{1,0:T(8,128)(2,1)S(1)}, bf16[512,640]{1,0:T(8,128)(2,1)S(1)}, u32[]{:S(2)}, u32[]{:S(2)}) %collective-permute-start) | collective-permute-done | bytes 655392 | tf_op jit(solution)/shard_map/ppermute | solution.py:154
  130.5 21.4 %all-to-all-done.refs_3_.refs_4_ = bf16[64,2,4,8,640]{4,3,2,1,0:T(8,128)(2,1)} async-done(((bf16[64,2,4,8,640]{4,3,2,1,0:T(8,128)(2,1)}), bf16[64,2,4,8,640]{4,3,2,1,0:T(8,128)(2,1)}, u32[]{:S(2)}, u32[]{:S(2)}) %all-to-all-start) | async-done | bytes 5242912 | tf_op jit(solution)/shard_map/all_to_all | solution.py:151
  151.9 4.6 %shard_map.91 = (f32[512,640]{1,0:T(8,128)}, f32[512,640]{1,0:T(8,128)}, f32[512,640]{1,0:T(8,128)}) custom-call(s32[4]{0:T(128)} %broadcast_select_fusion.1.refs_0_, s32[1]{0:T(128)} %bitcast.5.refs_1_, bf16[512,640]{1,0:T(8,128)(2,1)} %copy-done.7, bf16[64,2,4,8,640]{4,3,2,1,0:T(8,128)(2,1)} %all-to-all-done.refs_3_.refs_4_, ...), custom_call_target="tpu_custom_call" | custom-call | flops 2684354560 | bytes 13107200 | tf_op jit(solution)/shard_map/pallas_call | solution.py:83
  156.5 23.9 %shard_map.93 = (f32[512,640]{1,0:T(8,128)}, f32[512,640]{1,0:T(8,128)}, f32[512,640]{1,0:T(8,128)}) custom-call(s32[4]{0:T(128)} %broadcast_select_fusion.refs_0_, s32[1]{0:T(128)} %bitcast.6.refs_1_, bf16[512,640]{1,0:T(8,128)(2,1)} %bitcast.23, bf16[64,2,4,8,640]{4,3,2,1,0:T(8,128)(2,1)} %all-to-all-done.refs_3_.refs_4_, ...), custom_call_target="tpu_custom_call" | custom-call | flops 2684354560 | bytes 13107200 | tf_op jit(solution)/shard_map/pallas_call | solution.py:83
  180.4 0.0 copy-done.5
  180.4 0.2 select_convert_fusion
  180.6 12.1 %collective-permute-start.2 = (bf16[512,640]{1,0:T(8,128)(2,1)S(1)}, bf16[512,640]{1,0:T(8,128)(2,1)}, u32[]{:S(2)}, u32[]{:S(2)}) collective-permute-start(bf16[512,640]{1,0:T(8,128)(2,1)S(1)} %select_convert_fusion), channel_id=1, source_target_pairs={{0,1},{1,0},{2,3},{3,2},{4,5},{5,4},{6,7},{7,6},{8,9},{9,8},{10,11... | collective-permute-start | bytes 1966088 | tf_op jit(solution)/shard_map/ppermute | solution.py:187
  192.7 0.5 broadcast_select_fusion.2.refs_0_
  193.2 1.4 slice.13
  194.6 2.4 slice.12
  197.1 0.1 collective-permute-start.1
  197.2 2.0 collective-permute-start.3
  199.2 5.8 %shard_map.94 = (f32[512,640]{1,0:T(8,128)}, f32[512,640]{1,0:T(8,128)}, f32[512,640]{1,0:T(8,128)}) custom-call(s32[4]{0:T(128)} %broadcast_select_fusion.2.refs_0_, s32[1]{0:T(128)} %bitcast.refs_1_, bf16[512,640]{1,0:T(8,128)(2,1)} %bitcast.24, bf16[64,2,4,8,640]{4,3,2,1,0:T(8,128)(2,1)} %all-to-all-done.refs_3_.refs_4_, ...), custom_call_target="tpu_custom_call" | custom-call | flops 2684354560 | bytes 13107200 | tf_op jit(solution)/shard_map/pallas_call | solution.py:83
  205.0 8.9 %collective-permute-done.1 = f32[512,5]{1,0:T(8,128)S(1)} collective-permute-done((f32[512,5]{1,0:T(8,128)S(1)}, f32[512,5]{1,0:T(8,128)S(1)}, u32[]{:S(2)}, u32[]{:S(2)}) %collective-permute-start.1) | collective-permute-done | bytes 10272 | tf_op jit(solution)/shard_map/ppermute | solution.py:187
  213.9 0.1 copy.21
  214.0 0.2 broadcast_in_dim.61
  214.2 0.4 copy.22
  214.6 3.6 %collective-permute-done.3 = f32[512,5]{1,0:T(8,128)} collective-permute-done((f32[512,5]{1,0:T(8,128)S(1)}, f32[512,5]{1,0:T(8,128)}, u32[]{:S(2)}, u32[]{:S(2)}) %collective-permute-start.3) | collective-permute-done | bytes 10272 | tf_op jit(solution)/shard_map/ppermute | solution.py:187
  218.2 1.1 copy.23
  219.3 0.2 broadcast_in_dim.62
  219.4 1.5 copy.24
  220.9 0.0 collective-permute-done.2
  220.9 9.2 %convolution_convert_fusion = bf16[512,5120]{1,0:T(8,128)(2,1)S(1)} fusion(bf16[640,5120]{0,1:T(8,128)(2,1)} %all-gather.5.cloned.1.call-done, f32[512,640]{1,0:T(8,128)} %copy.24, f32[512,640]{1,0:T(8,128)} %get-tuple-element.47, f32[512,640]{1,0:T(8,128)S(1)} %copy.22, f32[512,640]{1,0:T(8,128)} %get-tuple-element.43, ...), kind=kOutput, calls=%fused_computation.2 | convolution fusion | flops 3362324480 | bytes 19005440 | tf_op jit(solution)/shard_map/dot_general | solution.py:202
  230.1 1.4 constant_dynamic-slice_fusion.1
  231.5 1.4 copy-done.4
  232.9 0.0 collective-permute-start.5
  232.9 0.5 collective-permute-start.4
  233.4 2.5 collective-permute-done.5
  235.9 1.6 add_convert_fusion.1
  237.6 0.1 fusion.6
  237.7 0.1 collective-permute-start.6
  237.7 2.0 collective-permute-start.8
  239.8 15.1 %collective-permute-done.6 = bf16[64,5120]{1,0:T(8,128)(2,1)S(1)} collective-permute-done((bf16[64,5120]{1,0:T(8,128)(2,1)S(1)}, bf16[64,5120]{1,0:T(8,128)(2,1)S(1)}, u32[]{:S(2)}, u32[]{:S(2)}) %collective-permute-start.6) | collective-permute-done | bytes 655392 | tf_op jit(solution)/shard_map/ppermute | solution.py:222
  254.8 1.5 collective-permute-start.7
  256.3 0.0 collective-permute-done.8
  256.4 3.5 %collective-permute-start.9 = (bf16[64,5120]{1,0:T(8,128)(2,1)S(1)}, bf16[64,5120]{1,0:T(8,128)(2,1)S(1)}, u32[]{:S(2)}, u32[]{:S(2)}) collective-permute-start(bf16[64,5120]{1,0:T(8,128)(2,1)S(1)} %collective-permute-done.8), channel_id=1, source_target_pairs={{0,132},{4,136},{8,140},{12,0},{128,4},{132,8},{136,12},{140,128},... | collective-permute-start | bytes 1966088 | tf_op jit(solution)/shard_map/ppermute | solution.py:222
  259.9 0.0 collective-permute-done.4
  259.9 39.7 %collective-permute-done.7 = bf16[64,5120]{1,0:T(8,128)(2,1)S(1)} collective-permute-done((bf16[64,5120]{1,0:T(8,128)(2,1)S(1)}, bf16[64,5120]{1,0:T(8,128)(2,1)S(1)}, u32[]{:S(2)}, u32[]{:S(2)}) %collective-permute-start.7) | collective-permute-done | bytes 655392 | tf_op jit(solution)/shard_map/ppermute | solution.py:222
  299.6 0.8 collective-permute-done.9
  300.4 3.5 %fusion.2 = bf16[1,128,5120]{2,1,0:T(8,128)(2,1)} fusion(bf16[128,5120]{1,0:T(8,128)(2,1)} %collective-permute-done.4, bf16[64,5120]{1,0:T(8,128)(2,1)S(1)} %collective-permute-done.9, bf16[64,5120]{1,0:T(8,128)(2,1)S(1)} %collective-permute-done.7, bf16[512,5120]{1,0:T(8,128)(2,1)} %copy-done.4, s32[]{:T(128)S(6)} %select_n.155), kind=kLoop, calls=%fused_computation.10 | loop fusion | flops 5898240 | bytes 5242884 | tf_op jit(solution)/shard_map/broadcast_in_dim | solution.py:236
  (23 shorter events, 0.1 us)
Async XLA Ops:
  6.5 5.3 %copy-start = (bf16[128,8,640]{2,1,0:T(8,128)(2,1)S(1)}, bf16[128,8,640]{2,1,0:T(8,128)(2,1)}, u32[]{:S(2)}) copy-start(bf16[128,8,640]{2,1,0:T(8,128)(2,1)} %param.12) | copy-start | bytes 3932164
  6.5 103.3 %all-gather.3.cloned.1.call-start = ((), (), s32[]{:S(2)}) async-start(), calls=%async_computation.1 | async-start | bytes 1740800 | tf_op jit(solution)/shard_map/all_gather | solution.py:147
  11.9 2.5 copy-start.3
  22.1 11.9 %copy-start.8 = (bf16[1,512,640]{2,1,0:T(8,128)(2,1)S(1)}, bf16[1,512,640]{2,1,0:T(8,128)(2,1)}, u32[]{:S(2)}) copy-start(bf16[1,512,640]{2,1,0:T(8,128)(2,1)} %param.11) | copy-start | bytes 1966084
  22.2 11.9 %copy-start.9 = (bf16[1,512,640]{2,1,0:T(8,128)(2,1)S(1)}, bf16[1,512,640]{2,1,0:T(8,128)(2,1)}, u32[]{:S(2)}) copy-start(bf16[1,512,640]{2,1,0:T(8,128)(2,1)} %param.10) | copy-start | bytes 1966084
  22.2 129.7 %all-to-all-start = ((bf16[64,2,4,8,640]{4,3,2,1,0:T(8,128)(2,1)}), bf16[64,2,4,8,640]{4,3,2,1,0:T(8,128)(2,1)}, u32[]{:S(2)}, u32[]{:S(2)}) async-start(bf16[64,2,4,8,640]{4,3,2,1,0:T(8,128)(2,1)} %pad_maximum_fusion), calls=%async_computation | async-start | bytes 10485760 | tf_op jit(solution)/shard_map/all_to_all | solution.py:151
  34.0 186.9 %all-gather.5.cloned.1.call-start = ((), (), s32[]{:S(2)}) async-start(), calls=%async_computation.2 | async-start | bytes 8192000 | tf_op jit(solution)/shard_map/all_gather | solution.py:171
  44.9 65.0 %copy-start.2 = (bf16[1,512,640]{2,1,0:T(8,128)(2,1)S(1)}, bf16[1,512,640]{2,1,0:T(8,128)(2,1)}, u32[]{:S(2)}) copy-start(bf16[1,512,640]{2,1,0:T(8,128)(2,1)} %param.9) | copy-start | bytes 1966084
  109.9 20.6 %collective-permute-start = (bf16[512,640]{1,0:T(8,128)(2,1)S(1)}, bf16[512,640]{1,0:T(8,128)(2,1)S(1)}, u32[]{:S(2)}, u32[]{:S(2)}) collective-permute-start(bf16[512,640]{1,0:T(8,128)(2,1)S(1)} %bitcast.25), channel_id=1, source_target_pairs={{0,1},{1,0},{2,3},{3,2},{4,5},{5,4},{6,7},{7,6},{8,9},{9,8},{10,11... | collective-permute-start | bytes 1966088 | tf_op jit(solution)/shard_map/ppermute | solution.py:154
  130.5 21.4 %copy-start.7 = (bf16[512,640]{1,0:T(8,128)(2,1)}, bf16[512,640]{1,0:T(8,128)(2,1)S(1)}, u32[]{:S(2)}) copy-start(bf16[512,640]{1,0:T(8,128)(2,1)S(1)} %collective-permute-done.refs_2_) | copy-start | bytes 1966084
  156.5 23.9 %copy-start.5 = (f32[512,640]{1,0:T(8,128)S(1)}, f32[512,640]{1,0:T(8,128)}, u32[]{:S(2)}) copy-start(f32[512,640]{1,0:T(8,128)} %get-tuple-element.45) | copy-start | bytes 3932164
  156.5 23.9 %copy-start.6 = (f32[512,640]{1,0:T(8,128)S(1)}, f32[512,640]{1,0:T(8,128)}, u32[]{:S(2)}) copy-start(f32[512,640]{1,0:T(8,128)} %get-tuple-element.46) | copy-start | bytes 3932164
  180.6 40.3 %collective-permute-start.2 = (bf16[512,640]{1,0:T(8,128)(2,1)S(1)}, bf16[512,640]{1,0:T(8,128)(2,1)}, u32[]{:S(2)}, u32[]{:S(2)}) collective-permute-start(bf16[512,640]{1,0:T(8,128)(2,1)S(1)} %select_convert_fusion), channel_id=1, source_target_pairs={{0,1},{1,0},{2,3},{3,2},{4,5},{5,4},{6,7},{7,6},{8,9},{9,8},{10,11... | collective-permute-start | bytes 1966088 | tf_op jit(solution)/shard_map/ppermute | solution.py:187
  197.1 16.8 %collective-permute-start.1 = (f32[512,5]{1,0:T(8,128)S(1)}, f32[512,5]{1,0:T(8,128)S(1)}, u32[]{:S(2)}, u32[]{:S(2)}) collective-permute-start(f32[512,5]{1,0:T(8,128)S(1)} %slice.12), channel_id=1, source_target_pairs={{0,1},{1,0},{2,3},{3,2},{4,5},{5,4},{6,7},{7,6},{8,9},{9,8},{10,11... | collective-permute-start | bytes 30728 | tf_op jit(solution)/shard_map/ppermute | solution.py:187
  197.2 21.0 %collective-permute-start.3 = (f32[512,5]{1,0:T(8,128)S(1)}, f32[512,5]{1,0:T(8,128)}, u32[]{:S(2)}, u32[]{:S(2)}) collective-permute-start(f32[512,5]{1,0:T(8,128)S(1)} %slice.13), channel_id=1, source_target_pairs={{0,1},{1,0},{2,3},{3,2},{4,5},{5,4},{6,7},{7,6},{8,9},{9,8},{10,11... | collective-permute-start | bytes 30728 | tf_op jit(solution)/shard_map/ppermute | solution.py:187
  230.1 2.8 copy-start.4
  232.9 3.0 collective-permute-start.5
  232.9 27.0 %collective-permute-start.4 = (bf16[128,5120]{1,0:T(8,128)(2,1)}, bf16[128,5120]{1,0:T(8,128)(2,1)}, u32[]{:S(2)}, u32[]{:S(2)}) collective-permute-start(bf16[128,5120]{1,0:T(8,128)(2,1)} %get-tuple-element.52), channel_id=1, source_target_pairs={{0,64},{64,0},{1,65},{65,1},{2,66},{66,2},{3,67},{67,3},{4,68},{68... | collective-permute-start | bytes 3932168 | tf_op jit(solution)/shard_map/ppermute | solution.py:232
  237.7 17.2 %collective-permute-start.6 = (bf16[64,5120]{1,0:T(8,128)(2,1)S(1)}, bf16[64,5120]{1,0:T(8,128)(2,1)S(1)}, u32[]{:S(2)}, u32[]{:S(2)}) collective-permute-start(bf16[64,5120]{1,0:T(8,128)(2,1)S(1)} %get-tuple-element.53), channel_id=1, source_target_pairs={{0,4},{4,8},{8,12},{12,128},{128,132},{132,136},{136,140},{140,0},... | collective-permute-start | bytes 1966088 | tf_op jit(solution)/shard_map/ppermute | solution.py:222
  237.7 18.6 %collective-permute-start.8 = (bf16[64,5120]{1,0:T(8,128)(2,1)S(1)}, bf16[64,5120]{1,0:T(8,128)(2,1)S(1)}, u32[]{:S(2)}, u32[]{:S(2)}) collective-permute-start(bf16[64,5120]{1,0:T(8,128)(2,1)S(1)} %get-tuple-element.54), channel_id=1, source_target_pairs={{0,140},{4,0},{8,4},{12,8},{128,12},{132,128},{136,132},{140,136},... | collective-permute-start | bytes 1966088 | tf_op jit(solution)/shard_map/ppermute | solution.py:222
  254.8 44.8 %collective-permute-start.7 = (bf16[64,5120]{1,0:T(8,128)(2,1)S(1)}, bf16[64,5120]{1,0:T(8,128)(2,1)S(1)}, u32[]{:S(2)}, u32[]{:S(2)}) collective-permute-start(bf16[64,5120]{1,0:T(8,128)(2,1)S(1)} %collective-permute-done.6), channel_id=1, source_target_pairs={{0,12},{4,128},{8,132},{12,136},{128,140},{132,0},{136,4},{140,8},... | collective-permute-start | bytes 1966088 | tf_op jit(solution)/shard_map/ppermute | solution.py:222
  256.4 44.1 %collective-permute-start.9 = (bf16[64,5120]{1,0:T(8,128)(2,1)S(1)}, bf16[64,5120]{1,0:T(8,128)(2,1)S(1)}, u32[]{:S(2)}, u32[]{:S(2)}) collective-permute-start(bf16[64,5120]{1,0:T(8,128)(2,1)S(1)} %collective-permute-done.8), channel_id=1, source_target_pairs={{0,132},{4,136},{8,140},{12,0},{128,4},{132,8},{136,12},{140,128},... | collective-permute-start | bytes 1966088 | tf_op jit(solution)/shard_map/ppermute | solution.py:222
  300.4 3.5 %copy-start.1 = (bf16[128,8,640]{2,1,0:T(8,128)(2,1)S(1)}, bf16[128,8,640]{2,1,0:T(8,128)(2,1)}, u32[]{:S(2)}) copy-start(bf16[128,8,640]{2,1,0:T(8,128)(2,1)} %param.12) | copy-start | bytes 3932164
Sparse Core Ops, SparseCore 0:
  9.1 100.6 all-gather.2
  111.7 82.0 all-gather.4

commit v14 on v13

--- a/solution.py
+++ b/solution.py
@@ -184,9 +184,10 @@
     other_state, own_state = lax.optimization_barrier((other_state, own_state))
     other_out, other_max, other_sum = other_state
     other_mean = jnp.where(other_sum > 0, other_out / jnp.maximum(other_sum, 1e-30), 0.0)
-    got_max, got_sum, got_mean = lax.ppermute(
-        (other_max[:, ::HD], other_sum[:, ::HD], other_mean.astype(jnp.bfloat16)), "x", swap
-    )
+    got_stats, got_mean = lax.ppermute(
+        (jnp.stack([other_max, other_sum])[:, :, ::HD], other_mean.astype(jnp.bfloat16)), "x", swap
+    )
+    got_max, got_sum = got_stats[0], got_stats[1]
     own_out, own_max, own_sum = attend(
         own_queries, arrived, visits_from(other_count + before), after.reshape(1), own_state
     )

time: 317 us -> 316 us (level)
  the two profiles are of different devices: /device:TPU:50 before, /device:TPU:34 now
where the time goes in v14:
time: 316 us
  waiting for transfers between devices  174 us (55%)
  Pallas kernels  44 us (14%)
  starting transfers between devices  38.8 us (12%)
  other arithmetic  18.7 us (6%)
  between operations  16.2 us (5%)
  local copies, waits for them, and re-layouts  15.4 us (5%)
  matrix products  9.23 us (3%)
    all_gather x1, waiting for transfers between devices, local(): weight = lax.all_gather(out_weight, ('zl', 'x'), axis=1, tiled=True)  62.8 us
    ppermute x4, waiting for transfers between devices, shifted(): lax.ppermute(rows, z_axes, [(i, (i + by) % ring) for i in range(ring)])  61.3 us
    pallas_call x4, Pallas kernels, attend(): pl.pallas_call(lambda *refs: attend_kernel(*refs, with_init=with_init, he...  44 us
    all_to_all x1, waiting for transfers between devices, local(): lax.all_to_all(sent, FRAME_AXES, split_axis=0, concat_axis=0, tiled=True)  27.4 us
    ppermute x4, starting transfers between devices, shifted(): lax.ppermute(rows, z_axes, [(i, (i + by) % ring) for i in range(ring)])  13.1 us
    ppermute x2, starting transfers between devices, local(): lax.ppermute((jnp.stack([other_max, other_sum])[:, :, ::HD], other_mean.a...  13 us
    ppermute x1, waiting for transfers between devices, local(): partner_queries = lax.ppermute(own_queries, 'x', swap)  12.7 us
    all_to_all x1, starting transfers between devices, local(): lax.all_to_all(sent, FRAME_AXES, split_axis=0, concat_axis=0, tiled=True)  11.9 us
  transfers between devices with their start and end apart: 12, of which 8 were waited for; matrix products, arithmetic and copies ran while one was open for 9% of the time, Pallas kernels for 14%

profile of v14, /device:TPU:34, one launch (start us, length us, event | category | flops | bytes accessed | tf_op | source)
XLA Modules:
  0.0 316.1 jit_solution(16232392875255578699)
XLA Ops:
  6.5 0.0 copy-start
  6.5 0.7 all-gather.3.cloned.1.call-update
  7.3 1.3 iota_subtract_fusion
  8.7 0.8 select_reduce_fusion.3
  9.5 0.8 copy.18
  10.3 0.1 reshape.305
  10.4 0.3 select_reduce_fusion
  10.8 0.9 select_reduce_fusion.2
  11.7 0.1 copy.19
  11.8 0.1 reshape.313
  11.9 0.0 copy-done
  11.9 0.0 copy-start.4
  11.9 2.5 gather_fusion
  14.4 2.4 gather_fusion.1
  16.8 5.3 %pad_maximum_fusion = bf16[64,2,4,8,640]{4,3,2,1,0:T(8,128)(2,1)} fusion(bf16[64,1,4,8,640]{4,3,2,1,0:T(8,128)(2,1)} %bitcast.27, bf16[64,1,4,8,640]{4,3,2,1,0:T(8,128)(2,1)} %bitcast.26), kind=kLoop, calls=%fused_computation.3 | loop fusion | flops 2621440 | bytes 10485760 | tf_op jit(solution)/shard_map/stack | solution.py:150
  22.2 11.9 %all-to-all-start = ((bf16[64,2,4,8,640]{4,3,2,1,0:T(8,128)(2,1)}), bf16[64,2,4,8,640]{4,3,2,1,0:T(8,128)(2,1)}, u32[]{:S(2)}, u32[]{:S(2)}) async-start(bf16[64,2,4,8,640]{4,3,2,1,0:T(8,128)(2,1)} %pad_maximum_fusion), calls=%async_computation | async-start | bytes 10485760 | tf_op jit(solution)/shard_map/all_to_all | solution.py:151
  34.1 0.0 all-gather.5.cloned.1.call-start
  34.2 1.2 copy_bitcast_fusion.refs_3_.refs_4_
  35.3 9.6 %shard_map.92 = (f32[512,640]{1,0:T(8,128)}, f32[512,640]{1,0:T(8,128)}, f32[512,640]{1,0:T(8,128)}) custom-call(s32[1]{0:T(128)} %constant.89.clone.1.refs_0_, s32[1]{0:T(128)} %constant.90.clone.1.refs_1_, bf16[512,640]{1,0:T(8,128)(2,1)} %bitcast.28, bf16[64,2,1,8,640]{4,3,2,1,0:T(8,128)(2,1)} %copy_bitcast_fusion.refs_3_.refs_4_, ...), custom_call_target="tpu_custom_call" | custom-call | flops 671088640 | bytes 9175040 | tf_op jit(solution)/shard_map/pallas_call | solution.py:83
  45.0 62.8 %all-gather.3.cloned.1.call-done = bf16[640,1280]{0,1:T(8,128)(2,1)} async-done(((bf16[640,80]{0,1:T(8,128)(2,1)}), bf16[640,1280]{0,1:T(8,128)(2,1)}) %all-gather.3.cloned.1.call-update) | async-done | bytes 1638416 | tf_op jit(solution)/shard_map/all_gather | solution.py:147
  107.8 0.0 all-gather.5.cloned.1.call-update
  107.8 0.3 collective-permute-start
  110.6 0.6 broadcast_select_fusion.refs_0_
  111.2 0.6 broadcast_select_fusion.1.refs_0_
  111.8 0.6 broadcast_select_fusion.2.refs_0_
  112.4 12.7 %collective-permute-done.refs_2_ = bf16[512,640]{1,0:T(8,128)(2,1)S(1)} collective-permute-done((bf16[512,640]{1,0:T(8,128)(2,1)S(1)}, bf16[512,640]{1,0:T(8,128)(2,1)S(1)}, u32[]{:S(2)}, u32[]{:S(2)}) %collective-permute-start) | collective-permute-done | bytes 655392 | tf_op jit(solution)/shard_map/ppermute | solution.py:154
  125.1 27.4 %all-to-all-done.refs_3_.refs_4_ = bf16[64,2,4,8,640]{4,3,2,1,0:T(8,128)(2,1)} async-done(((bf16[64,2,4,8,640]{4,3,2,1,0:T(8,128)(2,1)}), bf16[64,2,4,8,640]{4,3,2,1,0:T(8,128)(2,1)}, u32[]{:S(2)}, u32[]{:S(2)}) %all-to-all-start) | async-done | bytes 5242912 | tf_op jit(solution)/shard_map/all_to_all | solution.py:151
  152.5 0.0 copy-done.8
  152.5 16.5 %shard_map.91 = (f32[512,640]{1,0:T(8,128)}, f32[512,640]{1,0:T(8,128)}, f32[512,640]{1,0:T(8,128)}) custom-call(s32[4]{0:T(128)} %broadcast_select_fusion.1.refs_0_, s32[1]{0:T(128)} %bitcast.5.refs_1_, bf16[512,640]{1,0:T(8,128)(2,1)} %copy-done.8, bf16[64,2,4,8,640]{4,3,2,1,0:T(8,128)(2,1)} %all-to-all-done.refs_3_.refs_4_, ...), custom_call_target="tpu_custom_call" | custom-call | flops 2684354560 | bytes 13107200 | tf_op jit(solution)/shard_map/pallas_call | solution.py:83
  169.1 6.0 %shard_map.93 = (f32[512,640]{1,0:T(8,128)}, f32[512,640]{1,0:T(8,128)}, f32[512,640]{1,0:T(8,128)}) custom-call(s32[4]{0:T(128)} %broadcast_select_fusion.refs_0_, s32[1]{0:T(128)} %bitcast.6.refs_1_, bf16[512,640]{1,0:T(8,128)(2,1)} %bitcast.29, bf16[64,2,4,8,640]{4,3,2,1,0:T(8,128)(2,1)} %all-to-all-done.refs_3_.refs_4_, ...), custom_call_target="tpu_custom_call" | custom-call | flops 2684354560 | bytes 13107200 | tf_op jit(solution)/shard_map/pallas_call | solution.py:83
  175.1 0.0 copy-done.7
  175.1 0.0 copy-start.6
  175.1 0.2 select_convert_fusion
  175.4 11.7 %collective-permute-start.2 = (bf16[512,640]{1,0:T(8,128)(2,1)S(1)}, bf16[512,640]{1,0:T(8,128)(2,1)}, u32[]{:S(2)}, u32[]{:S(2)}) collective-permute-start(bf16[512,640]{1,0:T(8,128)(2,1)S(1)} %select_convert_fusion), channel_id=1, source_target_pairs={{0,1},{1,0},{2,3},{3,2},{4,5},{5,4},{6,7},{7,6},{8,9},{9,8},{10,11... | collective-permute-start | bytes 1966088 | tf_op jit(solution)/shard_map/ppermute | solution.py:187
  187.1 1.7 pad_maximum_fusion.1
  188.8 4.0 %slice.15 = f32[2,512,5]{2,1,0:T(8,128)S(1)} slice(f32[2,512,640]{2,1,0:T(8,128)} %pad_maximum_fusion.1), slice={[0:2:1], [0:512:1], [0:640:128]} | slice | bytes 40960 | tf_op jit(solution)/shard_map/slice | solution.py:188
  192.8 1.2 collective-permute-start.1
  194.0 11.8 %shard_map.94 = (f32[512,640]{1,0:T(8,128)}, f32[512,640]{1,0:T(8,128)}, f32[512,640]{1,0:T(8,128)}) custom-call(s32[4]{0:T(128)} %broadcast_select_fusion.2.refs_0_, s32[1]{0:T(128)} %bitcast.refs_1_, bf16[512,640]{1,0:T(8,128)(2,1)} %bitcast.30, bf16[64,2,4,8,640]{4,3,2,1,0:T(8,128)(2,1)} %all-to-all-done.refs_3_.refs_4_, ...), custom_call_target="tpu_custom_call" | custom-call | flops 2684354560 | bytes 13107200 | tf_op jit(solution)/shard_map/pallas_call | solution.py:83
  205.8 6.3 %collective-permute-done.1 = f32[2,512,5]{2,1,0:T(8,128)S(1)} collective-permute-done((f32[2,512,5]{2,1,0:T(8,128)S(1)}, f32[2,512,5]{2,1,0:T(8,128)S(1)}, u32[]{:S(2)}, u32[]{:S(2)}) %collective-permute-start.1) | collective-permute-done | bytes 20512 | tf_op jit(solution)/shard_map/ppermute | solution.py:187
  212.1 0.1 copy.21
  212.3 0.2 broadcast_in_dim.61
  212.4 0.4 copy.22
  212.8 0.1 copy.23
  212.9 0.2 broadcast_in_dim.62
  213.1 1.5 copy.24
  214.6 0.0 collective-permute-done.2
  214.6 9.2 %convolution_convert_fusion = bf16[512,5120]{1,0:T(8,128)(2,1)S(1)} fusion(bf16[640,5120]{0,1:T(8,128)(2,1)} %all-gather.5.cloned.1.call-done, f32[512,640]{1,0:T(8,128)} %copy.24, f32[512,640]{1,0:T(8,128)} %get-tuple-element.47, f32[512,640]{1,0:T(8,128)S(1)} %copy.22, f32[512,640]{1,0:T(8,128)} %get-tuple-element.43, ...), kind=kOutput, calls=%fused_computation.2 | convolution fusion | flops 3362324480 | bytes 19005440 | tf_op jit(solution)/shard_map/dot_general | solution.py:203
  223.8 1.4 constant_dynamic-slice_fusion.1
  225.2 1.4 copy-done.5
  226.6 0.0 collective-permute-start.4
  226.6 0.5 collective-permute-start.3
  227.1 2.5 collective-permute-done.4
  229.6 1.6 add_convert_fusion.1
  231.3 0.1 fusion.6
  231.3 0.1 collective-permute-start.5
  231.4 7.2 %collective-permute-start.7 = (bf16[64,5120]{1,0:T(8,128)(2,1)S(1)}, bf16[64,5120]{1,0:T(8,128)(2,1)S(1)}, u32[]{:S(2)}, u32[]{:S(2)}) collective-permute-start(bf16[64,5120]{1,0:T(8,128)(2,1)S(1)} %get-tuple-element.54), channel_id=1, source_target_pairs={{0,140},{4,0},{8,4},{12,8},{128,12},{132,128},{136,132},{140,136},... | collective-permute-start | bytes 1966088 | tf_op jit(solution)/shard_map/ppermute | solution.py:223
  238.6 14.9 %collective-permute-done.5 = bf16[64,5120]{1,0:T(8,128)(2,1)S(1)} collective-permute-done((bf16[64,5120]{1,0:T(8,128)(2,1)S(1)}, bf16[64,5120]{1,0:T(8,128)(2,1)S(1)}, u32[]{:S(2)}, u32[]{:S(2)}) %collective-permute-start.5) | collective-permute-done | bytes 655392 | tf_op jit(solution)/shard_map/ppermute | solution.py:223
  253.5 5.8 %collective-permute-start.6 = (bf16[64,5120]{1,0:T(8,128)(2,1)S(1)}, bf16[64,5120]{1,0:T(8,128)(2,1)S(1)}, u32[]{:S(2)}, u32[]{:S(2)}) collective-permute-start(bf16[64,5120]{1,0:T(8,128)(2,1)S(1)} %collective-permute-done.5), channel_id=1, source_target_pairs={{0,12},{4,128},{8,132},{12,136},{128,140},{132,0},{136,4},{140,8},... | collective-permute-start | bytes 1966088 | tf_op jit(solution)/shard_map/ppermute | solution.py:223
  259.4 0.0 collective-permute-done.7
  259.4 0.0 collective-permute-start.8
  259.4 0.0 collective-permute-done.3
  259.4 39.0 %collective-permute-done.6 = bf16[64,5120]{1,0:T(8,128)(2,1)S(1)} collective-permute-done((bf16[64,5120]{1,0:T(8,128)(2,1)S(1)}, bf16[64,5120]{1,0:T(8,128)(2,1)S(1)}, u32[]{:S(2)}, u32[]{:S(2)}) %collective-permute-start.6) | collective-permute-done | bytes 655392 | tf_op jit(solution)/shard_map/ppermute | solution.py:223
  298.4 7.3 %collective-permute-done.8 = bf16[64,5120]{1,0:T(8,128)(2,1)S(1)} collective-permute-done((bf16[64,5120]{1,0:T(8,128)(2,1)S(1)}, bf16[64,5120]{1,0:T(8,128)(2,1)S(1)}, u32[]{:S(2)}, u32[]{:S(2)}) %collective-permute-start.8) | collective-permute-done | bytes 655392 | tf_op jit(solution)/shard_map/ppermute | solution.py:223
  305.8 3.5 %fusion.2 = bf16[1,128,5120]{2,1,0:T(8,128)(2,1)} fusion(bf16[128,5120]{1,0:T(8,128)(2,1)} %collective-permute-done.3, bf16[64,5120]{1,0:T(8,128)(2,1)S(1)} %collective-permute-done.8, bf16[64,5120]{1,0:T(8,128)(2,1)S(1)} %collective-permute-done.6, bf16[512,5120]{1,0:T(8,128)(2,1)} %copy-done.5, s32[]{:T(128)S(6)} %select_n.155), kind=kLoop, calls=%fused_computation.11 | loop fusion | flops 5898240 | bytes 5242884 | tf_op jit(solution)/shard_map/broadcast_in_dim | solution.py:237
  (24 shorter events, 0.1 us)
Async XLA Ops:
  6.5 5.4 %copy-start = (bf16[128,8,640]{2,1,0:T(8,128)(2,1)S(1)}, bf16[128,8,640]{2,1,0:T(8,128)(2,1)}, u32[]{:S(2)}) copy-start(bf16[128,8,640]{2,1,0:T(8,128)(2,1)} %param.12) | copy-start | bytes 3932164
  6.5 101.2 %all-gather.3.cloned.1.call-start = ((), (), s32[]{:S(2)}) async-start(), calls=%async_computation.1 | async-start | bytes 1740800 | tf_op jit(solution)/shard_map/all_gather | solution.py:147
  11.9 2.5 copy-start.4
  22.2 12.0 %copy-start.9 = (bf16[1,512,640]{2,1,0:T(8,128)(2,1)S(1)}, bf16[1,512,640]{2,1,0:T(8,128)(2,1)}, u32[]{:S(2)}) copy-start(bf16[1,512,640]{2,1,0:T(8,128)(2,1)} %param.11) | copy-start | bytes 1966084
  22.2 12.0 %copy-start.10 = (bf16[1,512,640]{2,1,0:T(8,128)(2,1)S(1)}, bf16[1,512,640]{2,1,0:T(8,128)(2,1)}, u32[]{:S(2)}) copy-start(bf16[1,512,640]{2,1,0:T(8,128)(2,1)} %param.10) | copy-start | bytes 1966084
  22.2 130.4 %all-to-all-start = ((bf16[64,2,4,8,640]{4,3,2,1,0:T(8,128)(2,1)}), bf16[64,2,4,8,640]{4,3,2,1,0:T(8,128)(2,1)}, u32[]{:S(2)}, u32[]{:S(2)}) async-start(bf16[64,2,4,8,640]{4,3,2,1,0:T(8,128)(2,1)} %pad_maximum_fusion), calls=%async_computation | async-start | bytes 10485760 | tf_op jit(solution)/shard_map/all_to_all | solution.py:151
  34.1 180.5 %all-gather.5.cloned.1.call-start = ((), (), s32[]{:S(2)}) async-start(), calls=%async_computation.2 | async-start | bytes 8192000 | tf_op jit(solution)/shard_map/all_gather | solution.py:171
  45.0 62.8 %copy-start.2 = (bf16[1,512,640]{2,1,0:T(8,128)(2,1)S(1)}, bf16[1,512,640]{2,1,0:T(8,128)(2,1)}, u32[]{:S(2)}) copy-start(bf16[1,512,640]{2,1,0:T(8,128)(2,1)} %param.9) | copy-start | bytes 1966084
  107.8 17.3 %collective-permute-start = (bf16[512,640]{1,0:T(8,128)(2,1)S(1)}, bf16[512,640]{1,0:T(8,128)(2,1)S(1)}, u32[]{:S(2)}, u32[]{:S(2)}) collective-permute-start(bf16[512,640]{1,0:T(8,128)(2,1)S(1)} %bitcast.31), channel_id=1, source_target_pairs={{0,1},{1,0},{2,3},{3,2},{4,5},{5,4},{6,7},{7,6},{8,9},{9,8},{10,11... | collective-permute-start | bytes 1966088 | tf_op jit(solution)/shard_map/ppermute | solution.py:154
  125.1 27.4 %copy-start.8 = (bf16[512,640]{1,0:T(8,128)(2,1)}, bf16[512,640]{1,0:T(8,128)(2,1)S(1)}, u32[]{:S(2)}) copy-start(bf16[512,640]{1,0:T(8,128)(2,1)S(1)} %collective-permute-done.refs_2_) | copy-start | bytes 1966084
  169.1 6.0 %copy-start.3 = (f32[512,640]{1,0:T(8,128)S(1)}, f32[512,640]{1,0:T(8,128)}, u32[]{:S(2)}) copy-start(f32[512,640]{1,0:T(8,128)} %get-tuple-element.45) | copy-start | bytes 3932164
  169.1 6.0 %copy-start.7 = (f32[512,640]{1,0:T(8,128)S(1)}, f32[512,640]{1,0:T(8,128)}, u32[]{:S(2)}) copy-start(f32[512,640]{1,0:T(8,128)} %get-tuple-element.46) | copy-start | bytes 3932164
  175.1 12.0 %copy-start.6 = (f32[512,640]{1,0:T(8,128)S(1)}, f32[512,640]{1,0:T(8,128)}, u32[]{:S(2)}) copy-start(f32[512,640]{1,0:T(8,128)} %get-tuple-element.44) | copy-start | bytes 3932164
  175.4 39.2 %collective-permute-start.2 = (bf16[512,640]{1,0:T(8,128)(2,1)S(1)}, bf16[512,640]{1,0:T(8,128)(2,1)}, u32[]{:S(2)}, u32[]{:S(2)}) collective-permute-start(bf16[512,640]{1,0:T(8,128)(2,1)S(1)} %select_convert_fusion), channel_id=1, source_target_pairs={{0,1},{1,0},{2,3},{3,2},{4,5},{5,4},{6,7},{7,6},{8,9},{9,8},{10,11... | collective-permute-start | bytes 1966088 | tf_op jit(solution)/shard_map/ppermute | solution.py:187
  192.8 19.3 %collective-permute-start.1 = (f32[2,512,5]{2,1,0:T(8,128)S(1)}, f32[2,512,5]{2,1,0:T(8,128)S(1)}, u32[]{:S(2)}, u32[]{:S(2)}) collective-permute-start(f32[2,512,5]{2,1,0:T(8,128)S(1)} %slice.15), channel_id=1, source_target_pairs={{0,1},{1,0},{2,3},{3,2},{4,5},{5,4},{6,7},{7,6},{8,9},{9,8},{10,11... | collective-permute-start | bytes 61448 | tf_op jit(solution)/shard_map/ppermute | solution.py:187
  223.8 2.8 copy-start.5
  226.6 3.0 collective-permute-start.4
  226.6 32.8 %collective-permute-start.3 = (bf16[128,5120]{1,0:T(8,128)(2,1)}, bf16[128,5120]{1,0:T(8,128)(2,1)}, u32[]{:S(2)}, u32[]{:S(2)}) collective-permute-start(bf16[128,5120]{1,0:T(8,128)(2,1)} %get-tuple-element.52), channel_id=1, source_target_pairs={{0,64},{64,0},{1,65},{65,1},{2,66},{66,2},{3,67},{67,3},{4,68},{68... | collective-permute-start | bytes 3932168 | tf_op jit(solution)/shard_map/ppermute | solution.py:233
  231.3 22.2 %collective-permute-start.5 = (bf16[64,5120]{1,0:T(8,128)(2,1)S(1)}, bf16[64,5120]{1,0:T(8,128)(2,1)S(1)}, u32[]{:S(2)}, u32[]{:S(2)}) collective-permute-start(bf16[64,5120]{1,0:T(8,128)(2,1)S(1)} %get-tuple-element.53), channel_id=1, source_target_pairs={{0,4},{4,8},{8,12},{12,128},{128,132},{132,136},{136,140},{140,0},... | collective-permute-start | bytes 1966088 | tf_op jit(solution)/shard_map/ppermute | solution.py:223
  231.4 27.9 %collective-permute-start.7 = (bf16[64,5120]{1,0:T(8,128)(2,1)S(1)}, bf16[64,5120]{1,0:T(8,128)(2,1)S(1)}, u32[]{:S(2)}, u32[]{:S(2)}) collective-permute-start(bf16[64,5120]{1,0:T(8,128)(2,1)S(1)} %get-tuple-element.54), channel_id=1, source_target_pairs={{0,140},{4,0},{8,4},{12,8},{128,12},{132,128},{136,132},{140,136},... | collective-permute-start | bytes 1966088 | tf_op jit(solution)/shard_map/ppermute | solution.py:223
  253.5 44.9 %collective-permute-start.6 = (bf16[64,5120]{1,0:T(8,128)(2,1)S(1)}, bf16[64,5120]{1,0:T(8,128)(2,1)S(1)}, u32[]{:S(2)}, u32[]{:S(2)}) collective-permute-start(bf16[64,5120]{1,0:T(8,128)(2,1)S(1)} %collective-permute-done.5), channel_id=1, source_target_pairs={{0,12},{4,128},{8,132},{12,136},{128,140},{132,0},{136,4},{140,8},... | collective-permute-start | bytes 1966088 | tf_op jit(solution)/shard_map/ppermute | solution.py:223
  259.4 46.4 %collective-permute-start.8 = (bf16[64,5120]{1,0:T(8,128)(2,1)S(1)}, bf16[64,5120]{1,0:T(8,128)(2,1)S(1)}, u32[]{:S(2)}, u32[]{:S(2)}) collective-permute-start(bf16[64,5120]{1,0:T(8,128)(2,1)S(1)} %collective-permute-done.7), channel_id=1, source_target_pairs={{0,132},{4,136},{8,140},{12,0},{128,4},{132,8},{136,12},{140,128},... | collective-permute-start | bytes 1966088 | tf_op jit(solution)/shard_map/ppermute | solution.py:223
  305.8 3.5 %copy-start.1 = (bf16[128,8,640]{2,1,0:T(8,128)(2,1)S(1)}, bf16[128,8,640]{2,1,0:T(8,128)(2,1)}, u32[]{:S(2)}) copy-start(bf16[128,8,640]{2,1,0:T(8,128)(2,1)} %param.12) | copy-start | bytes 3932164
Sparse Core Ops, SparseCore 0:
  9.1 98.5 all-gather.2
  109.6 84.5 all-gather.4
